TPU v7x, 512 devices: a whole 4x4x16 slice. The times are simulated.
512 devices in a mesh: req: 32 (over y, x, core), grp: 16 (over z).
Axes of the slice: x: 4, y: 4, z: 16, core: 2. Of those that a mesh axis runs over, the one named last changes fastest.
Arguments:
- normed_token_input: bfloat16 [256, 8192], P(None, 'req'), may hold values from -6 to 6
- key_value_weight: bfloat16 [8192, 2048], P('req', 'grp'), may hold values from -0.0625 to 0.0625
- adapter_down_weight: bfloat16 [8192, 128, 128], P('req', 'grp'), may hold values from -0.0625 to 0.0625
- adapter_up_weight: bfloat16 [128, 64, 2048], P(None, None, 'grp'), may hold values from -0.75 to 0.75
- adapter_index_rows: int32 [256, 1], replicated, may hold values from 0 to 127
- queries: bfloat16 [256, 8192], P('req')
- key_value_pages: bfloat16 [10240, 16, 2, 8, 128], P('req', 'grp')
- lengths: int32 [256], P('req'), may hold values from 0 to 511, as said below
- page_slot_table: int32 [256, 32], P('req'), may hold values from 0 to 255, as said below
- departing_slots: int32 [1024], P('req'), may hold values from 0 to 255, as said below
- departing_target: int32 [1024, 1], P('req'), may hold values from 0 to 31; in each aligned block of 32 rows (0 to 31, 32 to 63, ...) at most 2 rows name the same one
Outputs:
- attention: bfloat16 [256, 8192], P('req')
- migrated_pool: bfloat16 [10240, 16, 2, 8, 128], P('req', 'grp')
Inputs may be any that keep to these rules, and one draw needn't show every extreme that they name: `adapter_index_rows`: each row names one adapter; every adapter is named by some request. `lengths`: some request has an empty cache and some has 511 cached tokens. `page_slot_table`: the rows of the requests of one home together name each of that home's slots 0 .. 255 exactly once. `departing_slots`: the 32 entries of one home are distinct. `departing_target`: the 32 rows of one home name one target at most 2 times; some home names some target exactly 2 times.
All inputs are finite; a program needn't handle non-finite values.
Results may differ from a plain program's by a relative error of at most 0.01345.
Values may be sent and summed in bfloat16 or wider, within the bound.
No kernel may reach another device: no remote copies, remote signals or barrier semaphores. Data moves between devices by JAX's collectives and lax.ppermute only.
A program may use at most 64 MiB of HBM per device.

v0:
```python
import math

import jax
import jax.numpy as jnp
from jax import lax
from jax.sharding import PartitionSpec as P

adapter_scale = 2.0
masked_score = -1e30


def merged_2(part, axis, combine):
    gathered = jax.tree.map(lambda a: lax.all_gather(a, axis), part)

    def take(source):
        return jax.tree.map(lambda a: lax.dynamic_index_in_dim(a, source, 0, False), gathered)

    return lax.fori_loop(
        1, lax.axis_size(axis), lambda source, state: combine(state, take(source)), take(0)
    )


def softmax_join(first, second):
    top = jnp.maximum(first[0], second[0])
    scale_one = jnp.exp(first[0] - top)
    scale_two = jnp.exp(second[0] - top)
    return (
        top,
        first[1] * scale_one + second[1] * scale_two,
        first[2] * scale_one[..., None] + second[2] * scale_two[..., None],
    )


def project_sums(base_part, mid_part):
    return (
        lax.psum_scatter(base_part, "req", scatter_dimension=0, tiled=True),
        lax.psum_scatter(mid_part, "req", scatter_dimension=0, tiled=True),
    )


def shards(
    normed_token_input,
    key_value_weight,
    adapter_down_weight,
    adapter_up_weight,
    adapter_index_rows,
    queries,
    key_value_pages,
    lengths,
    page_slot_table,
    departing_slots,
    departing_target,
):
    selected_adapter = adapter_index_rows[:, 0]
    rank_span_width = adapter_down_weight.shape[2]
    base_part = jnp.dot(normed_token_input, key_value_weight, preferred_element_type=jnp.float32)
    rank_portion = lax.all_gather(adapter_down_weight, "grp", axis=1, tiled=True)
    count = rank_portion.shape[1]
    flat = rank_portion.reshape(rank_portion.shape[0], count * rank_span_width)
    products = jnp.dot(normed_token_input, flat, preferred_element_type=jnp.float32).reshape(
        -1, count, rank_span_width
    )
    picker = (selected_adapter[:, None] == jnp.arange(count, dtype=jnp.int32)[None, :]).astype(
        jnp.float32
    )
    mid_part = jnp.einsum("ia,iaw->iw", picker, products)
    base_resident, mid_home = project_sums(base_part, mid_part)
    rows = lengths.shape[0]
    slot_tokens = key_value_pages.shape[1]
    heads = key_value_pages.shape[3]
    head_dim = key_value_pages.shape[4]
    group_index = lax.axis_index("grp")
    page_size = slot_tokens * lax.axis_size("grp")
    key_width = heads * head_dim
    resident_adapters = lax.dynamic_slice_in_dim(
        selected_adapter, lax.axis_index("req") * rows, rows
    )
    rank_half = adapter_up_weight.shape[1]
    column_span = adapter_up_weight.shape[2]
    mid_cast = mid_home.astype(jnp.bfloat16)
    is_value = group_index * column_span >= key_width
    mid_used = jnp.where(is_value, mid_cast[:, rank_half:], mid_cast[:, :rank_half])
    up_weight_rows = adapter_up_weight[resident_adapters]
    adapter_update = jnp.einsum(
        "ir,irc->ic", mid_used, up_weight_rows, preferred_element_type=jnp.float32
    )
    fresh_columns = (base_resident + adapter_scale * adapter_update).astype(jnp.bfloat16)
    new_all = lax.all_gather(fresh_columns, "grp", axis=1, tiled=True)
    new_keys = new_all[:, :key_width].reshape(rows, heads, head_dim)
    new_values = new_all[:, key_width:].reshape(rows, heads, head_dim)
    request_index = jnp.arange(rows, dtype=jnp.int32)
    page_slot = page_slot_table[request_index, lengths // page_size]
    offset = lengths % page_size
    mine = offset // slot_tokens == group_index
    token_local = offset % slot_tokens
    current = key_value_pages[page_slot, token_local]
    fresh = jnp.stack([new_keys, new_values], axis=1)
    written = key_value_pages.at[page_slot, token_local].set(
        jnp.where(mine[:, None, None, None], fresh, current)
    )
    pages = page_slot_table.shape[1]
    gathered = written[page_slot_table]
    keys = gathered[:, :, :, 0].reshape(rows, pages * slot_tokens, heads, head_dim)
    values = gathered[:, :, :, 1].reshape(rows, pages * slot_tokens, heads, head_dim)
    query = queries.reshape(rows, heads, -1, head_dim)
    scores = jnp.einsum(
        "ihgd,inhd->ihgn", query, keys, preferred_element_type=jnp.float32
    ) / math.sqrt(head_dim)
    positions = (
        jnp.arange(pages, dtype=jnp.int32)[:, None] * page_size
        + group_index * slot_tokens
        + jnp.arange(slot_tokens, dtype=jnp.int32)[None, :]
    ).reshape(-1)
    valid = (positions[None, :] <= lengths[:, None])[:, None, None, :]
    scores = jnp.where(valid, scores, masked_score)
    local_top = jnp.max(scores, axis=3)
    weights = jnp.where(valid, jnp.exp(scores - local_top[..., None]), 0.0)
    local_total = jnp.sum(weights, axis=3)
    local_mixed = jnp.einsum("ihgn,inhd->ihgd", weights, values, preferred_element_type=jnp.float32)
    merged = merged_2((local_top, local_total, local_mixed), "grp", softmax_join)
    total = merged[1]
    mixed = merged[2]
    attention = (mixed / total[..., None]).astype(jnp.bfloat16).reshape(rows, -1)
    targets = departing_target[:, 0]
    count_out = departing_slots.shape[0]
    order = jnp.arange(count_out, dtype=jnp.int32)
    earlier = (targets[:, None] == targets[None, :]) & (order[None, :] < order[:, None])
    place = jnp.sum(earlier.astype(jnp.int32), axis=1)
    live_slots = rows * pages
    home_count = lax.axis_size("req")
    capacity = (key_value_pages.shape[0] - live_slots) // home_count
    outbound = (
        jnp.zeros((home_count, capacity) + key_value_pages.shape[1:], key_value_pages.dtype)
        .at[targets, place]
        .set(written[departing_slots])
    )
    arrived = lax.all_to_all(outbound, "req", split_axis=0, concat_axis=0, tiled=True)
    migrated_pool = jnp.concatenate(
        [
            written[:live_slots],
            arrived.reshape((home_count * capacity,) + key_value_pages.shape[1:]),
        ],
        axis=0,
    )
    return (attention, migrated_pool)


def solution(mesh):
    in_specs = (
        P(None, "req"),
        P("req", "grp"),
        P("req", "grp", None),
        P(None, None, "grp"),
        P(),
        P("req", None),
        P("req", "grp", None, None, None),
        P("req"),
        P("req", None),
        P("req"),
        P("req", None),
    )
    out_specs = (P("req", None), P("req", "grp", None, None, None))
    return jax.shard_map(shards, mesh=mesh, in_specs=in_specs, out_specs=out_specs, check_vma=False)
```

profile of v0, /device:TPU:6, one launch (start us, length us, event | category | flops | bytes accessed | tf_op | source)
XLA Modules:
  0.0 464.6 jit_solution(6286880363566124155)
XLA Ops:
  8.1 1.5 copy.81
  9.6 1.7 fusion.37
  18.2 1.4 fusion.17
  19.6 1.3 dynamic-slice.1
  21.5 1.3 gather_fusion.1
  24.0 119.1 %all-gather.6.cloned.1.call-done = bf16[256,128,128]{2,1,0:T(8,128)(2,1)} async-done(((bf16[256,8,128]{2,1,0:T(8,128)(2,1)}), bf16[256,128,128]{2,1,0:T(8,128)(2,1)}) %all-gather.6.cloned.1.call-update) | async-done | bytes 8388624 | tf_op jit(solution)/shard_map/all_gather | solution.py:57
  143.1 12.8 %copy.40 = bf16[256,128,128]{0,2,1:T(8,128)(2,1)} copy(bf16[256,128,128]{2,1,0:T(8,128)(2,1)} %all-gather.6.cloned.1.call-done) | data formatting | bytes 16777216 | tf_op jit(solution)/shard_map/reshape | solution.py:59
  155.9 11.1 %fusion.5 = bf16[256,128,128]{2,0,1:T(8,128)(2,1)} fusion(bf16[256,128,128]{0,2,1:T(8,128)(2,1)} %copy.40, bf16[256,256]{1,0:T(8,128)(2,1)S(1)} %copy-done.5), kind=kOutput, calls=%fused_computation.17 | convolution fusion | flops 2147483648 | bytes 16908288 | tf_op jit(solution)/shard_map/dot_general | solution.py:60
  167.0 11.1 %fusion.3 = f32[256,1,128]{2,1,0:T(1,128)} fusion(bf16[256,128,128]{2,0,1:T(8,128)(2,1)} %fusion.5, pred[256,128,1]{1,0,2:T(32,128)(4,1)S(1)} %copy-done.8), kind=kOutput, calls=%fused_computation.15 | convolution fusion | flops 8388608 | bytes 8552448 | tf_op jit(solution)/shard_map/ia,iaw->iw/dot_general | solution.py:66
  178.1 110.4 %all-reduce.7 = bf16[256,128]{1,0:T(8,128)(2,1)S(1)} all-reduce(f32[256,128]{1,0:T(8,128)} %bitcast.109), channel_id=6, replica_groups=mesh['req'=32,'grp'=16] {'req'}, use_global_device_ids=true, to_apply=%region_1.0.clone | all-reduce | flops 32768 | bytes 196608
  290.3 28.9 %all_gather.25 = bf16[8,2048]{1,0:T(8,128)(2,1)S(1)} all-gather(bf16[8,128]{1,0:T(8,128)(2,1)S(1)} %fusion.20), channel_id=1, replica_groups=mesh['req'=32,'grp'=16] {'grp'}, dimensions={1}, use_global_device_ids=true | all-gather | bytes 34816 | tf_op jit(solution)/shard_map/all_gather | solution.py:88
  320.3 1.8 gather_fusion.3
  322.0 1.3 fusion.35
  328.5 3.5 scatter_fusion.1
  332.0 19.6 %all-to-all-start = ((bf16[32,2,1,2,8,128]{5,4,3,1,2,0:T(8,128)(2,1)}), bf16[32,2,1,2,8,128]{5,4,3,1,2,0:T(8,128)(2,1)}, u32[]{:S(2)}, u32[]{:S(2)}) async-start(bf16[32,2,1,2,8,128]{5,4,3,1,2,0:T(8,128)(2,1)} %bitcast.105), calls=%async_computation | async-start | bytes 524288 | tf_op jit(solution)/shard_map/all_to_all | solution.py:137
  351.6 33.3 %all-gather = f32[128,8,8]{2,1,0:T(8,128)S(1)} all-gather(f32[8,8,8]{2,1,0:T(8,128)} %copy-done.6), channel_id=2, replica_groups=mesh['req'=32,'grp'=16] {'grp'}, dimensions={0}, use_global_device_ids=true | all-gather | bytes 34816 | tf_op jit(solution)/shard_map/all_gather | solution.py:13
  384.9 1.4 fusion.11
  386.3 33.7 %all-gather.1 = f32[128,8,8]{2,1,0:T(8,128)S(1)} all-gather(f32[8,8,8]{2,1,0:T(8,128)S(1)} %fusion.11), channel_id=3, replica_groups=mesh['req'=32,'grp'=16] {'grp'}, dimensions={0}, use_global_device_ids=true | all-gather | bytes 34816 | tf_op jit(solution)/shard_map/all_gather | solution.py:13
  422.0 2.5 pad_maximum_fusion
  425.4 30.8 %while.19 = (s32[]{:T(128)}, f32[8,8,8]{2,1,0:T(8,128)S(1)}, f32[8,8,8]{2,1,0:T(8,128)S(1)}, f32[8,8,8,128]{3,2,1,0:T(8,128)S(1)}, f32[16,8,8,8]{3,2,1,0:T(8,128...) while((s32[]{:T(128)}, f32[8,8,8]{2,1,0:T(8,128)S(1)}, ...), condition=%wide.region_6.7_spmd, body=%wide.region_5.6_spmd.sunk | while | flops 199685 | bytes 807055 | solution.py:18
  426.3 1.2 fusion.44
  428.3 1.2 fusion.44
  430.4 1.2 fusion.44
  432.4 1.2 fusion.44
  434.5 1.2 fusion.44
  436.6 1.2 fusion.44
  438.6 1.2 fusion.44
  442.7 1.2 fusion.44
  444.8 1.2 fusion.44
  450.9 1.2 fusion.44
  453.0 1.2 fusion.44
  455.1 1.2 fusion.44
  (88 shorter events, 35.8 us)
Async XLA Ops:
  8.0 13.5 %copy-start = (bf16[128,64,128]{2,1,0:T(8,128)(2,1)S(1)}, bf16[128,64,128]{2,1,0:T(8,128)(2,1)}, u32[]{:S(2)}) copy-start(bf16[128,64,128]{2,1,0:T(8,128)(2,1)} %param.16) | copy-start | bytes 6291460
  8.0 1.6 copy-start.5
  8.0 3.9 copy-start.10
  8.0 5.2 %copy-start.1 = (s32[8,32]{1,0:T(8,128)S(1)}, s32[8,32]{1,0:T(8,128)}, u32[]{:S(2)}) copy-start(s32[8,32]{1,0:T(8,128)} %param.21) | copy-start | bytes 3076
  8.0 135.0 %all-gather.6.cloned.1.call-start = ((), (), s32[]{:S(2)}) async-start(), calls=%async_computation.1 | async-start | bytes 8912896 | tf_op jit(solution)/shard_map/all_gather | solution.py:57
  9.6 280.1 %all-reduce.6.cloned.1.call-start = ((), (), s32[]{:S(2)}) async-start(), calls=%async_computation.3 | async-start | bytes 262144
  11.3 413.1 %all-gather.8.cloned.1.call-start = ((), (), s32[]{:S(2)}) async-start(), calls=%async_computation.2 | async-start | bytes 4456448 | tf_op jit(solution)/shard_map/all_gather | solution.py:13
  155.9 11.1 %copy-start.8 = (pred[256,128,1]{1,0,2:T(32,128)(4,1)S(1)}, pred[256,128,1]{1,0,2:T(32,128)(4,1)}, u32[]{:S(2)}) copy-start(pred[256,128,1]{1,0,2:T(32,128)(4,1)} %fusion.17) | copy-start | bytes 98308
  167.0 152.3 %copy-start.7 = (bf16[8,2,8,128]{3,2,1,0:T(8,128)(2,1)S(1)}, bf16[8,2,8,128]{3,2,1,0:T(8,128)(2,1)}, u32[]{:S(2)}) copy-start(bf16[8,2,8,128]{3,2,1,0:T(8,128)(2,1)} %gather_fusion.2) | copy-start | bytes 98308
  167.0 152.3 %copy-start.9 = (pred[8]{0:T(512)(128)(4,1)S(1)}, pred[8]{0:T(512)(128)(4,1)}, u32[]{:S(2)}) copy-start(pred[8]{0:T(512)(128)(4,1)} %fusion.24) | copy-start | bytes 28
  320.3 3.1 copy-start.11
  322.0 3.5 copy-start.12
  323.8 0.7 copy-start.2
  323.8 0.7 copy-start.6
  332.0 90.0 %all-to-all-start = ((bf16[32,2,1,2,8,128]{5,4,3,1,2,0:T(8,128)(2,1)}), bf16[32,2,1,2,8,128]{5,4,3,1,2,0:T(8,128)(2,1)}, u32[]{:S(2)}, u32[]{:S(2)}) async-start(bf16[32,2,1,2,8,128]{5,4,3,1,2,0:T(8,128)(2,1)} %bitcast.105), calls=%async_computation | async-start | bytes 524288 | tf_op jit(solution)/shard_map/all_to_all | solution.py:137
  384.9 1.4 copy-start.3
  420.0 0.8 copy-start.4
Sparse Core Ops, SparseCore 0:
  10.9 132.1 all-gather.5
  325.7 87.7 all-gather.7
Sparse Core Ops, SparseCore 1:
  13.8 138.3 all-reduce.5
where the time goes:
time: 467 us; the launch traced here: 465 us
  blocking collectives  206 us (44%)
  waiting for transfers between devices  119 us (25%)
  other arithmetic  43.3 us (9%)
  local copies, waits for them, and re-layouts  33 us (7%)
  matrix products  26.4 us (6%)
  starting transfers between devices  19.7 us (4%)
  between operations  16.4 us (4%)
    all_gather x1, waiting for transfers between devices, shards(): lax.all_gather(adapter_down_weight, 'grp', axis=1, tiled=True)  119 us
    unnamed x1, blocking collectives  110 us
    all_gather x2, blocking collectives, merged_2(): gathered = jax.tree.map(lambda a: lax.all_gather(a, axis), part)  67.1 us
    all_gather x1, blocking collectives, shards(): new_all = lax.all_gather(fresh_columns, 'grp', axis=1, tiled=True)  28.9 us
    all_to_all x1, starting transfers between devices, shards(): lax.all_to_all(outbound, 'req', split_axis=0, concat_axis=0, tiled=True)  19.6 us
    add x15, other arithmetic, softmax_join(): first[2] * scale_one[..., None] + second[2] * scale_two[..., None]  18.2 us
    reshape x1, local copies, waits for them, and re-layouts, shards(): flat = rank_portion.reshape(rank_portion.shape[0], count * rank_span_width)  12.8 us
    add x15, other arithmetic, softmax_join(): first[1] * scale_one + second[1] * scale_two  12.3 us
  transfers between devices with their start and end apart: 4, of which 1 were waited for; matrix products, arithmetic and copies ran while one was open for 13% of the time, Pallas kernels for 0%

commit v1 on v0

v1 whole, which is shorter than its diff:
```python
import math

import jax
import jax.numpy as jnp
from jax import lax
from jax.sharding import PartitionSpec as P

adapter_scale = 2.0
masked_score = -1e30


def shards(
    normed_token_input,
    key_value_weight,
    adapter_down_weight,
    adapter_up_weight,
    adapter_index_rows,
    queries,
    key_value_pages,
    lengths,
    page_slot_table,
    departing_slots,
    departing_target,
):
    selected_adapter = adapter_index_rows[:, 0]
    homes = lax.axis_size("req")
    groups = lax.axis_size("grp")
    home_index = lax.axis_index("req")
    group_index = lax.axis_index("grp")
    rows = lengths.shape[0]
    request_count = normed_token_input.shape[0]
    column_span = key_value_weight.shape[1]
    local_adapters = adapter_down_weight.shape[1]
    rank_width = adapter_down_weight.shape[2]
    rank_half = adapter_up_weight.shape[1]
    slot_tokens = key_value_pages.shape[1]
    heads = key_value_pages.shape[3]
    head_dim = key_value_pages.shape[4]
    key_width = heads * head_dim
    query_heads = queries.shape[1] // head_dim
    heads_per_target = query_heads // groups
    page_size = slot_tokens * groups
    pages = page_slot_table.shape[1]

    both = jnp.concatenate(
        [key_value_weight, adapter_down_weight.reshape(adapter_down_weight.shape[0], -1)], axis=1
    )
    products = jnp.dot(normed_token_input, both, preferred_element_type=jnp.float32)
    base_part = products[:, :column_span]
    down_all = products[:, column_span:].reshape(request_count, local_adapters, rank_width)
    local_choice = selected_adapter - group_index * local_adapters
    picker = (local_choice[:, None] == jnp.arange(local_adapters, dtype=jnp.int32)[None, :]).astype(
        jnp.float32
    )
    mid_part = jnp.einsum("ia,iaw->iw", picker, down_all)
    partial = jnp.concatenate([base_part, mid_part], axis=1).reshape(homes, rows, -1)
    summed = jnp.sum(lax.all_to_all(partial, "req", 0, 0, tiled=False), axis=0)
    base_resident = summed[:, :column_span]
    mid_owned = summed[:, column_span:].astype(jnp.bfloat16)

    resident_adapters = lax.dynamic_slice_in_dim(selected_adapter, home_index * rows, rows)
    owner = resident_adapters // local_adapters
    mid_spread = lax.all_to_all(
        jnp.broadcast_to(mid_owned[None], (groups,) + mid_owned.shape), "grp", 0, 0, tiled=False
    )
    request_index = jnp.arange(rows, dtype=jnp.int32)
    mid_home = mid_spread[owner, request_index]
    is_value = group_index * column_span >= key_width
    mid_used = jnp.where(is_value, mid_home[:, rank_half:], mid_home[:, :rank_half])
    up_weight_rows = adapter_up_weight[resident_adapters]
    adapter_update = jnp.einsum(
        "ir,irc->ic", mid_used, up_weight_rows, preferred_element_type=jnp.float32
    )
    fresh_columns = (base_resident + adapter_scale * adapter_update).astype(jnp.bfloat16)

    gathered = key_value_pages[page_slot_table][:, :, 0]
    keys = gathered[:, :, 0]
    values = gathered[:, :, 1]
    query = queries.reshape(rows, heads, -1, head_dim)
    scores = jnp.einsum(
        "ihgd,inhd->ihgn", query, keys, preferred_element_type=jnp.float32
    ) / math.sqrt(head_dim)
    positions = jnp.arange(pages, dtype=jnp.int32) * page_size + group_index * slot_tokens
    valid = (positions[None, :] < lengths[:, None])[:, None, None, :]
    scores = jnp.where(valid, scores, masked_score)
    local_top = jnp.max(scores, axis=3)
    weights = jnp.where(valid, jnp.exp(scores - local_top[..., None]), 0.0)
    local_total = jnp.sum(weights, axis=3)
    local_mixed = jnp.einsum(
        "ihgn,inhd->ihgd", weights, values, preferred_element_type=jnp.float32
    )

    parcel = jnp.concatenate(
        [
            local_mixed.reshape(rows, groups, heads_per_target * head_dim),
            local_top.reshape(rows, groups, heads_per_target),
            local_total.reshape(rows, groups, heads_per_target),
            jnp.broadcast_to(
                fresh_columns.astype(jnp.float32)[:, None, :], (rows, groups, column_span)
            ),
        ],
        axis=2,
    ).transpose(1, 0, 2)
    received = lax.all_to_all(parcel, "grp", 0, 0, tiled=False)
    mixed_width = heads_per_target * head_dim
    shard_mixed = received[:, :, :mixed_width].reshape(groups, rows, heads_per_target, head_dim)
    shard_top = received[:, :, mixed_width : mixed_width + heads_per_target]
    shard_total = received[:, :, mixed_width + heads_per_target : mixed_width + 2 * heads_per_target]
    new_all = received[:, :, mixed_width + 2 * heads_per_target :].astype(jnp.bfloat16)
    new_all = new_all.transpose(1, 0, 2).reshape(rows, groups * column_span)
    new_keys = new_all[:, :key_width].reshape(rows, heads, head_dim)
    new_values = new_all[:, key_width:].reshape(rows, heads, head_dim)

    head_of_target = group_index * heads_per_target // (query_heads // heads)
    own_query = lax.dynamic_slice_in_dim(
        queries, group_index * mixed_width, mixed_width, axis=1
    ).reshape(rows, heads_per_target, head_dim)
    own_key = lax.dynamic_index_in_dim(new_keys, head_of_target, 1, False)
    own_value = lax.dynamic_index_in_dim(new_values, head_of_target, 1, False)
    new_score = jnp.einsum(
        "ihd,id->ih", own_query, own_key, preferred_element_type=jnp.float32
    ) / math.sqrt(head_dim)
    top = jnp.maximum(jnp.max(shard_top, axis=0), new_score)
    shard_scale = jnp.exp(shard_top - top[None])
    new_weight = jnp.exp(new_score - top)
    total = jnp.sum(shard_total * shard_scale, axis=0) + new_weight
    mixed = jnp.sum(shard_mixed * shard_scale[..., None], axis=0) + new_weight[
        ..., None
    ] * own_value.astype(jnp.float32)[:, None, :]
    own_attention = (mixed / total[..., None]).astype(jnp.bfloat16).reshape(rows, mixed_width)
    attention = lax.all_gather(own_attention, "grp", axis=1, tiled=True)

    page_slot = page_slot_table[request_index, lengths // page_size]
    offset = lengths % page_size
    mine = offset // slot_tokens == group_index
    token_local = offset % slot_tokens
    current = key_value_pages[page_slot, token_local]
    fresh = jnp.stack([new_keys, new_values], axis=1)
    written = key_value_pages.at[page_slot, token_local].set(
        jnp.where(mine[:, None, None, None], fresh, current)
    )

    targets = departing_target[:, 0]
    count_out = departing_slots.shape[0]
    order = jnp.arange(count_out, dtype=jnp.int32)
    earlier = (targets[:, None] == targets[None, :]) & (order[None, :] < order[:, None])
    place = jnp.sum(earlier.astype(jnp.int32), axis=1)
    live_slots = rows * pages
    capacity = (key_value_pages.shape[0] - live_slots) // homes
    outbound = (
        jnp.zeros((homes, capacity) + key_value_pages.shape[1:], key_value_pages.dtype)
        .at[targets, place]
        .set(written[departing_slots])
    )
    arrived = lax.all_to_all(outbound, "req", split_axis=0, concat_axis=0, tiled=True)
    migrated_pool = jnp.concatenate(
        [
            written[:live_slots],
            arrived.reshape((homes * capacity,) + key_value_pages.shape[1:]),
        ],
        axis=0,
    )
    return (attention, migrated_pool)


def solution(mesh):
    in_specs = (
        P(None, "req"),
        P("req", "grp"),
        P("req", "grp", None),
        P(None, None, "grp"),
        P(),
        P("req", None),
        P("req", "grp", None, None, None),
        P("req"),
        P("req", None),
        P("req"),
        P("req", None),
    )
    out_specs = (P("req", None), P("req", "grp", None, None, None))
    return jax.shard_map(shards, mesh=mesh, in_specs=in_specs, out_specs=out_specs, check_vma=False)
```

time: 467 us -> 160 us (0.34)
  the two profiles are of different devices: /device:TPU:6 before, /device:TPU:1 now
where the time goes in v1:
time: 160 us; the launch traced here: 158 us
  starting transfers between devices  48.7 us (30%)
  local copies, waits for them, and re-layouts  32.1 us (20%)
  blocking collectives  28.5 us (18%)
  waiting for transfers between devices  23.2 us (14%)
  other arithmetic  20.9 us (13%)
  matrix products  4.13 us (3%)
    all_gather x1, blocking collectives, shards(): attention = lax.all_gather(own_attention, 'grp', axis=1, tiled=True)  28.5 us
    all_to_all x1, starting transfers between devices, shards(): lax.all_to_all(outbound, 'req', split_axis=0, concat_axis=0, tiled=True)  16.8 us
    all_to_all x1, starting transfers between devices, shards(): lax.all_to_all(jnp.broadcast_to(mid_owned[None], (groups,) + mid_owned.sh...  12.5 us
    all_to_all x1, starting transfers between devices, shards(): summed = jnp.sum(lax.all_to_all(partial, 'req', 0, 0, tiled=False), axis=0)  11 us
    all_to_all x1, waiting for transfers between devices, shards(): received = lax.all_to_all(parcel, 'grp', 0, 0, tiled=False)  10.9 us
    all_to_all x1, starting transfers between devices, shards(): received = lax.all_to_all(parcel, 'grp', 0, 0, tiled=False)  8.38 us
    all_to_all x1, waiting for transfers between devices, shards(): lax.all_to_all(outbound, 'req', split_axis=0, concat_axis=0, tiled=True)  7.77 us
    unnamed x29, local copies, waits for them, and re-layouts  4.87 us
  transfers between devices with their start and end apart: 4, of which 4 were waited for; matrix products, arithmetic and copies ran while one was open for 15% of the time, Pallas kernels for 0%

profile of v1, /device:TPU:1, one launch (start us, length us, event | category | flops | bytes accessed | tf_op | source)
XLA Modules:
  0.0 158.4 jit_solution(13711185269570245694)
XLA Ops:
  0.7 1.5 copy.92
  2.8 1.1 slice.84
  4.9 1.0 copy.63
  5.8 1.3 multiply_reduce_fusion
  7.9 1.8 %copy.43 = f32[256,256]{1,0:T(8,128)} copy(f32[256,256]{0,1:T(8,128)} %pad_maximum_fusion.1) | data formatting | bytes 524288 | tf_op jit(solution)/shard_map/concatenate | solution.py:56
  9.7 11.0 %all-to-all-start = ((f32[32,8,256]{2,1,0:T(8,128)}), f32[32,8,256]{2,1,0:T(8,128)}, u32[]{:S(2)}, u32[]{:S(2)}) async-start(f32[32,8,256]{2,1,0:T(8,128)} %bitcast.113), calls=%async_computation | async-start | bytes 524288 | tf_op jit(solution)/shard_map/all_to_all | solution.py:57
  20.8 1.8 %gather_fusion = bf16[256,2,8,128]{3,2,1,0:T(8,128)(2,1)} fusion(bf16[320,2,8,128]{3,2,1,0:T(8,128)(2,1)S(1)} %bitcast.107, s32[1024]{0:T(1024)S(1)} %pad_clamp_fusion.2), kind=kCustom, calls=%fused_computation | custom fusion | bytes 2098176 | tf_op jit(solution)/shard_map/gather | solution.py:76
  22.6 2.1 %fusion.41 = (bf16[8,32,1,8,128]{4,3,2,1,0:T(8,128)(2,1)}, bf16[8,32,1,8,128]{4,3,2,1,0:T(8,128)(2,1)S(1)}) fusion(bf16[8,32,2,8,128]{4,3,2,1,0:T(8,128)(2,1)} %bitcast.110), kind=kLoop, calls=%fused_computation.114 | loop fusion | bytes 2097152 | tf_op jit(solution)/shard_map/slice | solution.py:78
  26.2 2.1 %fusion.5 = f32[8,8,8,128]{3,2,1,0:T(8,128)} fusion(bf16[8,32,1,8,128]{4,3,2,1,0:T(8,128)(2,1)} %get-tuple-element.6, f32[8,8,8,32]{3,2,1,0:T(8,128)} %copy-done.3, f32[8,8,8]{2,1,0:T(8,128)S(1)} %get-tuple-element.16, pred[8,32]{1,0:T(8,128)(4,1)S(1)} %broadcast_compare_fusion), kind=kOutput, calls=%fused_computation.20 | convolution fusion | flops 4227072 | bytes 854272 | tf_op jit(solution)/shard_map/ihgn,inhd->ihgd/dot_general | solution.py:89
  28.4 1.4 all-to-all-done
  29.8 1.0 reduce_sum.48
  31.4 12.5 %all-to-all-start.1 = ((bf16[16,8,128]{2,1,0:T(8,128)(2,1)}), bf16[16,8,128]{2,1,0:T(8,128)(2,1)}, u32[]{:S(2)}, u32[]{:S(2)}) async-start(bf16[16,8,128]{2,1,0:T(8,128)(2,1)} %broadcast_in_dim.45), calls=%async_computation.1 | async-start | bytes 65536 | tf_op jit(solution)/shard_map/all_to_all | solution.py:63
  46.4 1.7 %reshape.115 = f32[8,16,512]{2,1,0:T(8,128)} reshape(f32[8,8,8,128]{3,2,1,0:T(8,128)} %fusion.5) | data formatting | bytes 524288 | tf_op jit(solution)/shard_map/reshape | solution.py:95
  48.0 1.8 %copy.44 = f32[8,16,512]{2,0,1:T(8,128)} copy(f32[8,16,512]{2,1,0:T(8,128)} %reshape.115) | data formatting | bytes 524288 | tf_op jit(solution)/shard_map/reshape | solution.py:95
  49.8 1.2 pad_clamp_fusion.1
  51.1 1.3 gather_fusion.2
  52.4 3.1 %all-to-all-done.1 = bf16[16,8,128]{2,1,0:T(8,128)(2,1)} async-done(((bf16[16,8,128]{2,1,0:T(8,128)(2,1)}), bf16[16,8,128]{2,1,0:T(8,128)(2,1)}, u32[]{:S(2)}, u32[]{:S(2)}) %all-to-all-start.1) | async-done | bytes 32800 | tf_op jit(solution)/shard_map/all_to_all | solution.py:63
  55.5 1.9 %gather_fusion.1 = bf16[8,128]{1,0:T(8,128)(2,1)} fusion(bf16[16,8,128]{2,1,0:T(8,128)(2,1)} %all-to-all-done.1, s32[8]{0:T(128)S(1)} %get-tuple-element.12), kind=kCustom, calls=%fused_computation.1 | custom fusion | bytes 4160 | tf_op jit(solution)/shard_map/gather | solution.py:67
  58.2 1.0 fusion.20
  59.3 1.8 %maximum_bitcast_fusion = f32[16,8,648]{2,1,0:T(8,128)} fusion(f32[8,16,128]{2,0,1:T(8,128)S(1)} %broadcast_in_dim.46, f32[8,16,4]{2,0,1:T(8,128)S(1)} %copy.46, f32[8,16,4]{2,0,1:T(8,128)S(1)} %copy.45, f32[8,16,512]{2,0,1:T(8,128)} %copy.44), kind=kLoop, calls=%fused_computation.22 | loop fusion | flops 248832 | bytes 663552 | tf_op jit(solution)/shard_map/transpose | solution.py:103
  61.1 8.4 %all-to-all-start.2 = ((f32[16,8,648]{2,1,0:T(8,128)}), f32[16,8,648]{2,1,0:T(8,128)}, u32[]{:S(2)}, u32[]{:S(2)}) async-start(f32[16,8,648]{2,1,0:T(8,128)} %maximum_bitcast_fusion), calls=%async_computation.2 | async-start | bytes 786432 | tf_op jit(solution)/shard_map/all_to_all | solution.py:104
  74.9 1.2 fusion.26
  76.7 10.9 %all-to-all-done.2 = f32[16,8,648]{2,1,0:T(8,128)} async-done(((f32[16,8,648]{2,1,0:T(8,128)}), f32[16,8,648]{2,1,0:T(8,128)}, u32[]{:S(2)}, u32[]{:S(2)}) %all-to-all-start.2) | async-done | bytes 331808 | tf_op jit(solution)/shard_map/all_to_all | solution.py:104
  87.7 1.0 fusion.14
  90.3 1.0 fusion.13
  92.3 1.1 fusion.6
  93.5 28.5 %all_gather.3 = bf16[8,8192]{1,0:T(8,128)(2,1)} all-gather(bf16[8,512]{1,0:T(8,128)(2,1)S(1)} %fusion.15), channel_id=1, replica_groups=mesh['req'=32,'grp'=16] {'grp'}, dimensions={1}, use_global_device_ids=true | all-gather | bytes 139264 | tf_op jit(solution)/shard_map/all_gather | solution.py:131
  125.7 3.8 %scatter_fusion.1 = bf16[32,2,2,8,128]{4,3,2,1,0:T(8,128)(2,1)} fusion(bf16[32,2,2,8,128]{4,3,2,1,0:T(8,128)(2,1)} %broadcast.228, s32[32]{0:T(128)S(1)} %fusion.36, bf16[32,2,8,128]{3,2,1,0:T(8,128)(2,1)S(1)} %gather_fusion.5), kind=kCustom, calls=%fused_computation.7 | custom fusion | bytes 393472 | tf_op jit(solution)/shard_map/scatter | solution.py:153
  129.5 16.8 %all-to-all-start.3 = ((bf16[32,2,1,2,8,128]{5,4,3,1,2,0:T(8,128)(2,1)}), bf16[32,2,1,2,8,128]{5,4,3,1,2,0:T(8,128)(2,1)}, u32[]{:S(2)}, u32[]{:S(2)}) async-start(bf16[32,2,1,2,8,128]{5,4,3,1,2,0:T(8,128)(2,1)} %bitcast.112), calls=%async_computation.3 | async-start | bytes 524288 | tf_op jit(solution)/shard_map/all_to_all | solution.py:155
  146.3 1.2 slice_bitcast_fusion
  147.4 7.8 %all-to-all-done.3 = bf16[32,2,1,2,8,128]{5,4,3,1,2,0:T(8,128)(2,1)} async-done(((bf16[32,2,1,2,8,128]{5,4,3,1,2,0:T(8,128)(2,1)}), bf16[32,2,1,2,8,128]{5,4,3,1,2,0:T(8,128)(2,1)}, u32[]{:S(2)}, u32[]{:S(2)}) %all-to-all-start.3) | async-done | bytes 262176 | tf_op jit(solution)/shard_map/all_to_all | solution.py:155
  155.2 2.5 %pad_maximum_fusion = bf16[320,1,2,8,128]{4,3,2,1,0:T(8,128)(2,1)} fusion(bf16[64,1,2,8,128]{4,3,2,1,0:T(8,128)(2,1)} %bitcast.43, bf16[256,1,2,8,128]{4,3,2,1,0:T(8,128)(2,1)} %slice_bitcast_fusion), kind=kLoop, calls=%fused_computation.9 | loop fusion | flops 655360 | bytes 2621440 | tf_op jit(solution)/shard_map/concatenate | solution.py:156
  (74 shorter events, 21.0 us)
Async XLA Ops:
  0.6 50.4 %copy-start = (bf16[128,64,128]{2,1,0:T(8,128)(2,1)S(1)}, bf16[128,64,128]{2,1,0:T(8,128)(2,1)}, u32[]{:S(2)}) copy-start(bf16[128,64,128]{2,1,0:T(8,128)(2,1)} %param.14) | copy-start | bytes 6291460
  0.6 1.7 %copy-start.6 = (bf16[256,256]{1,0:T(8,128)(2,1)S(1)}, bf16[256,256]{1,0:T(8,128)(2,1)}, u32[]{:S(2)}) copy-start(bf16[256,256]{1,0:T(8,128)(2,1)} %param.11) | copy-start | bytes 393220
  0.7 1.7 %copy-start.7 = (bf16[256,128]{1,0:T(8,128)(2,1)S(1)}, bf16[256,128]{1,0:T(8,128)(2,1)}, u32[]{:S(2)}) copy-start(bf16[256,128]{1,0:T(8,128)(2,1)} %param.12) | copy-start | bytes 196612
  0.7 1.6 %copy-start.4 = (bf16[256,8,128]{2,1,0:T(8,128)(2,1)S(1)}, bf16[256,8,128]{2,1,0:T(8,128)(2,1)}, u32[]{:S(2)}) copy-start(bf16[256,8,128]{2,1,0:T(8,128)(2,1)} %param.13) | copy-start | bytes 1572868
  2.7 1.4 copy-start.2
  2.8 1.4 copy-start.8
  4.1 3.1 %slice-start = ((f32[256,1152]{0,1:T(8,128)}), f32[256,128]{0,1:T(8,128)S(1)}, s32[]{:S(2)}) async-start(f32[256,1152]{0,1:T(8,128)} %copy-done.2), calls=%async_computation.4 | async-start | bytes 262144 | tf_op jit(solution)/shard_map/slice | solution.py:49
  5.8 14.9 %copy-start.1 = (s32[8,32]{1,0:T(8,128)S(1)}, s32[8,32]{1,0:T(8,128)}, u32[]{:S(2)}) copy-start(s32[8,32]{1,0:T(8,128)} %param.19) | copy-start | bytes 3076
  9.7 20.1 %all-to-all-start = ((f32[32,8,256]{2,1,0:T(8,128)}), f32[32,8,256]{2,1,0:T(8,128)}, u32[]{:S(2)}, u32[]{:S(2)}) async-start(f32[32,8,256]{2,1,0:T(8,128)} %bitcast.113), calls=%async_computation | async-start | bytes 524288 | tf_op jit(solution)/shard_map/all_to_all | solution.py:57
  22.6 2.1 %copy-start.11 = (s32[8]{0:T(128)S(1)}, s32[8]{0:T(128)}, u32[]{:S(2)}) copy-start(s32[8]{0:T(128)} %param.18) | copy-start | bytes 100
  22.6 2.2 %copy-start.10 = (bf16[8,8192]{1,0:T(8,128)(2,1)S(1)}, bf16[8,8192]{1,0:T(8,128)(2,1)}, u32[]{:S(2)}) copy-start(bf16[8,8192]{1,0:T(8,128)(2,1)} %param.16) | copy-start | bytes 393220
  24.8 19.1 %copy-start.9 = (s32[256,1]{0,1:T(1,128)S(1)}, s32[256,1]{0,1:T(1,128)}, u32[]{:S(2)}) copy-start(s32[256,1]{0,1:T(1,128)} %param.15) | copy-start | bytes 3076
  25.2 0.7 copy-start.3
  31.4 24.1 %all-to-all-start.1 = ((bf16[16,8,128]{2,1,0:T(8,128)(2,1)}), bf16[16,8,128]{2,1,0:T(8,128)(2,1)}, u32[]{:S(2)}, u32[]{:S(2)}) async-start(bf16[16,8,128]{2,1,0:T(8,128)(2,1)} %broadcast_in_dim.45), calls=%async_computation.1 | async-start | bytes 65536 | tf_op jit(solution)/shard_map/all_to_all | solution.py:63
  61.1 26.6 %all-to-all-start.2 = ((f32[16,8,648]{2,1,0:T(8,128)}), f32[16,8,648]{2,1,0:T(8,128)}, u32[]{:S(2)}, u32[]{:S(2)}) async-start(f32[16,8,648]{2,1,0:T(8,128)} %maximum_bitcast_fusion), calls=%async_computation.2 | async-start | bytes 786432 | tf_op jit(solution)/shard_map/all_to_all | solution.py:104
  129.5 25.7 %all-to-all-start.3 = ((bf16[32,2,1,2,8,128]{5,4,3,1,2,0:T(8,128)(2,1)}), bf16[32,2,1,2,8,128]{5,4,3,1,2,0:T(8,128)(2,1)}, u32[]{:S(2)}, u32[]{:S(2)}) async-start(bf16[32,2,1,2,8,128]{5,4,3,1,2,0:T(8,128)(2,1)} %bitcast.112), calls=%async_computation.3 | async-start | bytes 524288 | tf_op jit(solution)/shard_map/all_to_all | solution.py:155
  155.2 2.5 %copy-start.5 = (bf16[8,8192]{1,0:T(8,128)(2,1)S(1)}, bf16[8,8192]{1,0:T(8,128)(2,1)}, u32[]{:S(2)}) copy-start(bf16[8,8192]{1,0:T(8,128)(2,1)} %all_gather.3) | copy-start | bytes 393220

commit v2 on v1

--- a/solution.py
+++ b/solution.py
@@ -128,7 +128,10 @@
         ..., None
     ] * own_value.astype(jnp.float32)[:, None, :]
     own_attention = (mixed / total[..., None]).astype(jnp.bfloat16).reshape(rows, mixed_width)
-    attention = lax.all_gather(own_attention, "grp", axis=1, tiled=True)
+    attention = lax.all_to_all(
+        jnp.broadcast_to(own_attention[None], (groups,) + own_attention.shape), "grp", 0, 0, tiled=False
+    )
+    attention = attention.transpose(1, 0, 2).reshape(rows, groups * mixed_width)
 
     page_slot = page_slot_table[request_index, lengths // page_size]
     offset = lengths % page_size

time: 160 us -> 143 us (0.89)
  blocking collectives: 28.5 us -> 0 us
  waiting for transfers between devices: 23.2 us -> 32 us
    all_gather x1 -> x0, blocking collectives: 28.5 us -> none  [shards(): attention = lax.all_gather(own_attention, 'grp', axis=1, tiled=True)]
    all_to_all x0 -> x1, waiting for transfers between devices: none -> 9.8 us  [shards(): lax.all_to_all(jnp.broadcast_to(own_attention[None], (groups,) + own_atte...]
    all_to_all x0 -> x1, starting transfers between devices: none -> 6.03 us  [shards(): lax.all_to_all(jnp.broadcast_to(own_attention[None], (groups,) + own_atte...]
    all_to_all x1, starting transfers between devices: 16.8 us -> 12.1 us  [shards(): lax.all_to_all(outbound, 'req', split_axis=0, concat_axis=0, tiled=True)]
    unnamed x29 -> x31, local copies, waits for them, and re-layouts: 4.87 us -> 4.86 us
  transfers between devices with their start and end apart: 4 -> 5, of which waited for: 4 -> 5; matrix products, arithmetic and copies ran while one was open for 15% -> 19% of each run, Pallas kernels for 0% -> 0%
where the time goes in v2:
time: 143 us; the launch traced here: 140 us
  starting transfers between devices  50.1 us (35%)
  waiting for transfers between devices  32 us (22%)
  local copies, waits for them, and re-layouts  31.7 us (22%)
  other arithmetic  21.3 us (15%)
  matrix products  4.13 us (3%)
    all_to_all x1, starting transfers between devices, shards(): lax.all_to_all(jnp.broadcast_to(mid_owned[None], (groups,) + mid_owned.sh...  12.5 us
    all_to_all x1, starting transfers between devices, shards(): lax.all_to_all(outbound, 'req', split_axis=0, concat_axis=0, tiled=True)  12.1 us
    all_to_all x1, starting transfers between devices, shards(): summed = jnp.sum(lax.all_to_all(partial, 'req', 0, 0, tiled=False), axis=0)  11 us
    all_to_all x1, waiting for transfers between devices, shards(): received = lax.all_to_all(parcel, 'grp', 0, 0, tiled=False)  10.9 us
    all_to_all x1, waiting for transfers between devices, shards(): lax.all_to_all(jnp.broadcast_to(own_attention[None], (groups,) + own_atte...  9.8 us
    all_to_all x1, starting transfers between devices, shards(): received = lax.all_to_all(parcel, 'grp', 0, 0, tiled=False)  8.49 us
    all_to_all x1, waiting for transfers between devices, shards(): lax.all_to_all(outbound, 'req', split_axis=0, concat_axis=0, tiled=True)  6.91 us
    all_to_all x1, starting transfers between devices, shards(): lax.all_to_all(jnp.broadcast_to(own_attention[None], (groups,) + own_atte...  6.03 us
  transfers between devices with their start and end apart: 5, of which 5 were waited for; matrix products, arithmetic and copies ran while one was open for 19% of the time, Pallas kernels for 0%

profile of v2, /device:TPU:1, one launch (start us, length us, event | category | flops | bytes accessed | tf_op | source)
XLA Modules:
  0.0 140.1 jit_solution(6995970577039890552)
XLA Ops:
  0.7 1.5 %copy.92 = bf16[320,1,2,8,128]{4,3,2,1,0:T(8,128)(2,1)S(1)} copy(bf16[320,1,2,8,128]{4,3,2,1,0:T(8,128)(2,1)} %param.17) | data formatting | bytes 2621440
  2.8 1.1 slice.84
  4.9 1.0 copy.63
  5.8 1.3 multiply_reduce_fusion
  7.9 1.8 %copy.43 = f32[256,256]{1,0:T(8,128)} copy(f32[256,256]{0,1:T(8,128)} %pad_maximum_fusion.1) | data formatting | bytes 524288 | tf_op jit(solution)/shard_map/concatenate | solution.py:56
  9.7 11.0 %all-to-all-start = ((f32[32,8,256]{2,1,0:T(8,128)}), f32[32,8,256]{2,1,0:T(8,128)}, u32[]{:S(2)}, u32[]{:S(2)}) async-start(f32[32,8,256]{2,1,0:T(8,128)} %bitcast.116), calls=%async_computation | async-start | bytes 524288 | tf_op jit(solution)/shard_map/all_to_all | solution.py:57
  20.8 1.8 %gather_fusion = bf16[256,2,8,128]{3,2,1,0:T(8,128)(2,1)} fusion(bf16[320,2,8,128]{3,2,1,0:T(8,128)(2,1)S(1)} %bitcast.110, s32[1024]{0:T(1024)S(1)} %pad_clamp_fusion.2), kind=kCustom, calls=%fused_computation | custom fusion | bytes 2098176 | tf_op jit(solution)/shard_map/gather | solution.py:76
  22.6 2.1 %fusion.41 = (bf16[8,32,1,8,128]{4,3,2,1,0:T(8,128)(2,1)}, bf16[8,32,1,8,128]{4,3,2,1,0:T(8,128)(2,1)S(1)}) fusion(bf16[8,32,2,8,128]{4,3,2,1,0:T(8,128)(2,1)} %bitcast.113), kind=kLoop, calls=%fused_computation.114 | loop fusion | bytes 2097152 | tf_op jit(solution)/shard_map/slice | solution.py:78
  26.2 2.1 %fusion.5 = f32[8,8,8,128]{3,2,1,0:T(8,128)} fusion(bf16[8,32,1,8,128]{4,3,2,1,0:T(8,128)(2,1)} %get-tuple-element.6, f32[8,8,8,32]{3,2,1,0:T(8,128)} %copy-done.3, f32[8,8,8]{2,1,0:T(8,128)S(1)} %get-tuple-element.16, pred[8,32]{1,0:T(8,128)(4,1)S(1)} %broadcast_compare_fusion), kind=kOutput, calls=%fused_computation.20 | convolution fusion | flops 4227072 | bytes 854272 | tf_op jit(solution)/shard_map/ihgn,inhd->ihgd/dot_general | solution.py:89
  28.4 1.4 all-to-all-done
  29.7 1.0 reduce_sum.48
  31.3 12.5 %all-to-all-start.1 = ((bf16[16,8,128]{2,1,0:T(8,128)(2,1)}), bf16[16,8,128]{2,1,0:T(8,128)(2,1)}, u32[]{:S(2)}, u32[]{:S(2)}) async-start(bf16[16,8,128]{2,1,0:T(8,128)(2,1)} %broadcast_in_dim.47), calls=%async_computation.1 | async-start | bytes 65536 | tf_op jit(solution)/shard_map/all_to_all | solution.py:63
  46.4 1.7 %reshape.137 = f32[8,16,512]{2,1,0:T(8,128)} reshape(f32[8,8,8,128]{3,2,1,0:T(8,128)} %fusion.5) | data formatting | bytes 524288 | tf_op jit(solution)/shard_map/reshape | solution.py:95
  48.1 1.8 %copy.44 = f32[8,16,512]{2,0,1:T(8,128)} copy(f32[8,16,512]{2,1,0:T(8,128)} %reshape.137) | data formatting | bytes 524288 | tf_op jit(solution)/shard_map/reshape | solution.py:95
  49.9 1.3 pad_clamp_fusion.1
  51.2 1.3 gather_fusion.2
  52.5 3.0 %all-to-all-done.1 = bf16[16,8,128]{2,1,0:T(8,128)(2,1)} async-done(((bf16[16,8,128]{2,1,0:T(8,128)(2,1)}), bf16[16,8,128]{2,1,0:T(8,128)(2,1)}, u32[]{:S(2)}, u32[]{:S(2)}) %all-to-all-start.1) | async-done | bytes 32800 | tf_op jit(solution)/shard_map/all_to_all | solution.py:63
  55.5 1.9 %gather_fusion.1 = bf16[8,128]{1,0:T(8,128)(2,1)} fusion(bf16[16,8,128]{2,1,0:T(8,128)(2,1)} %all-to-all-done.1, s32[8]{0:T(128)S(1)} %get-tuple-element.12), kind=kCustom, calls=%fused_computation.1 | custom fusion | bytes 4160 | tf_op jit(solution)/shard_map/gather | solution.py:67
  58.2 1.0 fusion.20
  59.3 1.8 %maximum_bitcast_fusion = f32[16,8,648]{2,1,0:T(8,128)} fusion(f32[8,16,128]{2,0,1:T(8,128)S(1)} %broadcast_in_dim.48, f32[8,16,4]{2,0,1:T(8,128)S(1)} %copy.46, f32[8,16,4]{2,0,1:T(8,128)S(1)} %copy.45, f32[8,16,512]{2,0,1:T(8,128)} %copy.44), kind=kLoop, calls=%fused_computation.22 | loop fusion | flops 248832 | bytes 663552 | tf_op jit(solution)/shard_map/transpose | solution.py:103
  61.1 8.5 %all-to-all-start.2 = ((f32[16,8,648]{2,1,0:T(8,128)}), f32[16,8,648]{2,1,0:T(8,128)}, u32[]{:S(2)}, u32[]{:S(2)}) async-start(f32[16,8,648]{2,1,0:T(8,128)} %maximum_bitcast_fusion), calls=%async_computation.2 | async-start | bytes 786432 | tf_op jit(solution)/shard_map/all_to_all | solution.py:104
  74.9 1.3 fusion.26
  76.9 10.9 %all-to-all-done.2 = f32[16,8,648]{2,1,0:T(8,128)} async-done(((f32[16,8,648]{2,1,0:T(8,128)}), f32[16,8,648]{2,1,0:T(8,128)}, u32[]{:S(2)}, u32[]{:S(2)}) %all-to-all-start.2) | async-done | bytes 331808 | tf_op jit(solution)/shard_map/all_to_all | solution.py:104
  87.8 1.0 fusion.14
  90.4 1.0 fusion.13
  95.9 3.8 %scatter_fusion.1 = bf16[32,2,2,8,128]{4,3,2,1,0:T(8,128)(2,1)} fusion(bf16[32,2,2,8,128]{4,3,2,1,0:T(8,128)(2,1)} %broadcast.231, s32[32]{0:T(128)S(1)} %fusion.36, bf16[32,2,8,128]{3,2,1,0:T(8,128)(2,1)S(1)} %gather_fusion.5), kind=kCustom, calls=%fused_computation.7 | custom fusion | bytes 393472 | tf_op jit(solution)/shard_map/scatter | solution.py:156
  99.6 12.1 %all-to-all-start.4 = ((bf16[32,2,1,2,8,128]{5,4,3,1,2,0:T(8,128)(2,1)}), bf16[32,2,1,2,8,128]{5,4,3,1,2,0:T(8,128)(2,1)}, u32[]{:S(2)}, u32[]{:S(2)}) async-start(bf16[32,2,1,2,8,128]{5,4,3,1,2,0:T(8,128)(2,1)} %bitcast.115), calls=%async_computation.4 | async-start | bytes 524288 | tf_op jit(solution)/shard_map/all_to_all | solution.py:158
  111.7 1.1 fusion.6
  113.7 6.9 %all-to-all-done.4 = bf16[32,2,1,2,8,128]{5,4,3,1,2,0:T(8,128)(2,1)} async-done(((bf16[32,2,1,2,8,128]{5,4,3,1,2,0:T(8,128)(2,1)}), bf16[32,2,1,2,8,128]{5,4,3,1,2,0:T(8,128)(2,1)}, u32[]{:S(2)}, u32[]{:S(2)}) %all-to-all-start.4) | async-done | bytes 262176 | tf_op jit(solution)/shard_map/all_to_all | solution.py:158
  121.3 6.0 %all-to-all-start.3 = ((bf16[16,8,512]{2,1,0:T(8,128)(2,1)}), bf16[16,8,512]{2,1,0:T(8,128)(2,1)S(1)}, u32[]{:S(2)}, u32[]{:S(2)}) async-start(bf16[16,8,512]{2,1,0:T(8,128)(2,1)} %broadcast_in_dim.49), calls=%async_computation.3 | async-start | bytes 262144 | tf_op jit(solution)/shard_map/all_to_all | solution.py:131
  127.5 2.1 %pad_maximum_fusion = bf16[320,1,2,8,128]{4,3,2,1,0:T(8,128)(2,1)} fusion(bf16[64,1,2,8,128]{4,3,2,1,0:T(8,128)(2,1)} %bitcast.45, bf16[256,1,2,8,128]{4,3,2,1,0:T(8,128)(2,1)S(1)} %slice_bitcast_fusion), kind=kLoop, calls=%fused_computation.9 | loop fusion | flops 655360 | bytes 2621440 | tf_op jit(solution)/shard_map/concatenate | solution.py:159
  129.6 9.8 %all-to-all-done.3 = bf16[16,8,512]{2,1,0:T(8,128)(2,1)S(1)} async-done(((bf16[16,8,512]{2,1,0:T(8,128)(2,1)}), bf16[16,8,512]{2,1,0:T(8,128)(2,1)S(1)}, u32[]{:S(2)}, u32[]{:S(2)}) %all-to-all-start.3) | async-done | bytes 131104 | tf_op jit(solution)/shard_map/all_to_all | solution.py:131
  (78 shorter events, 22.3 us)
Async XLA Ops:
  0.6 50.5 %copy-start = (bf16[128,64,128]{2,1,0:T(8,128)(2,1)S(1)}, bf16[128,64,128]{2,1,0:T(8,128)(2,1)}, u32[]{:S(2)}) copy-start(bf16[128,64,128]{2,1,0:T(8,128)(2,1)} %param.14) | copy-start | bytes 6291460
  0.6 1.7 %copy-start.5 = (bf16[256,256]{1,0:T(8,128)(2,1)S(1)}, bf16[256,256]{1,0:T(8,128)(2,1)}, u32[]{:S(2)}) copy-start(bf16[256,256]{1,0:T(8,128)(2,1)} %param.11) | copy-start | bytes 393220
  0.7 1.7 %copy-start.6 = (bf16[256,128]{1,0:T(8,128)(2,1)S(1)}, bf16[256,128]{1,0:T(8,128)(2,1)}, u32[]{:S(2)}) copy-start(bf16[256,128]{1,0:T(8,128)(2,1)} %param.12) | copy-start | bytes 196612
  0.7 1.6 %copy-start.4 = (bf16[256,8,128]{2,1,0:T(8,128)(2,1)S(1)}, bf16[256,8,128]{2,1,0:T(8,128)(2,1)}, u32[]{:S(2)}) copy-start(bf16[256,8,128]{2,1,0:T(8,128)(2,1)} %param.13) | copy-start | bytes 1572868
  2.7 1.4 copy-start.2
  2.8 1.4 copy-start.9
  4.1 3.1 %slice-start = ((f32[256,1152]{0,1:T(8,128)}), f32[256,128]{0,1:T(8,128)S(1)}, s32[]{:S(2)}) async-start(f32[256,1152]{0,1:T(8,128)} %copy-done.2), calls=%async_computation.5 | async-start | bytes 262144 | tf_op jit(solution)/shard_map/slice | solution.py:49
  5.8 14.9 %copy-start.1 = (s32[8,32]{1,0:T(8,128)S(1)}, s32[8,32]{1,0:T(8,128)}, u32[]{:S(2)}) copy-start(s32[8,32]{1,0:T(8,128)} %param.19) | copy-start | bytes 3076
  9.7 20.1 %all-to-all-start = ((f32[32,8,256]{2,1,0:T(8,128)}), f32[32,8,256]{2,1,0:T(8,128)}, u32[]{:S(2)}, u32[]{:S(2)}) async-start(f32[32,8,256]{2,1,0:T(8,128)} %bitcast.116), calls=%async_computation | async-start | bytes 524288 | tf_op jit(solution)/shard_map/all_to_all | solution.py:57
  22.6 2.1 %copy-start.12 = (s32[8]{0:T(128)S(1)}, s32[8]{0:T(128)}, u32[]{:S(2)}) copy-start(s32[8]{0:T(128)} %param.18) | copy-start | bytes 100
  22.6 2.2 %copy-start.11 = (bf16[8,8192]{1,0:T(8,128)(2,1)S(1)}, bf16[8,8192]{1,0:T(8,128)(2,1)}, u32[]{:S(2)}) copy-start(bf16[8,8192]{1,0:T(8,128)(2,1)} %param.16) | copy-start | bytes 393220
  24.8 19.1 %copy-start.10 = (s32[256,1]{0,1:T(1,128)S(1)}, s32[256,1]{0,1:T(1,128)}, u32[]{:S(2)}) copy-start(s32[256,1]{0,1:T(1,128)} %param.15) | copy-start | bytes 3076
  25.2 0.7 copy-start.3
  31.3 24.1 %all-to-all-start.1 = ((bf16[16,8,128]{2,1,0:T(8,128)(2,1)}), bf16[16,8,128]{2,1,0:T(8,128)(2,1)}, u32[]{:S(2)}, u32[]{:S(2)}) async-start(bf16[16,8,128]{2,1,0:T(8,128)(2,1)} %broadcast_in_dim.47), calls=%async_computation.1 | async-start | bytes 65536 | tf_op jit(solution)/shard_map/all_to_all | solution.py:63
  61.1 26.7 %all-to-all-start.2 = ((f32[16,8,648]{2,1,0:T(8,128)}), f32[16,8,648]{2,1,0:T(8,128)}, u32[]{:S(2)}, u32[]{:S(2)}) async-start(f32[16,8,648]{2,1,0:T(8,128)} %maximum_bitcast_fusion), calls=%async_computation.2 | async-start | bytes 786432 | tf_op jit(solution)/shard_map/all_to_all | solution.py:104
  92.8 20.7 %copy-start.8 = (f32[8,4]{1,0:T(8,128)S(1)}, f32[8,4]{1,0:T(8,128)}, u32[]{:S(2)}) copy-start(f32[8,4]{1,0:T(8,128)} %get-tuple-element.2) | copy-start | bytes 388
  92.8 20.8 %copy-start.7 = (f32[8,4]{1,0:T(8,128)S(1)}, f32[8,4]{1,0:T(8,128)}, u32[]{:S(2)}) copy-start(f32[8,4]{1,0:T(8,128)} %get-tuple-element.3) | copy-start | bytes 388
  99.6 21.0 %all-to-all-start.4 = ((bf16[32,2,1,2,8,128]{5,4,3,1,2,0:T(8,128)(2,1)}), bf16[32,2,1,2,8,128]{5,4,3,1,2,0:T(8,128)(2,1)}, u32[]{:S(2)}, u32[]{:S(2)}) async-start(bf16[32,2,1,2,8,128]{5,4,3,1,2,0:T(8,128)(2,1)} %bitcast.115), calls=%async_computation.4 | async-start | bytes 524288 | tf_op jit(solution)/shard_map/all_to_all | solution.py:158
  121.3 18.2 %all-to-all-start.3 = ((bf16[16,8,512]{2,1,0:T(8,128)(2,1)}), bf16[16,8,512]{2,1,0:T(8,128)(2,1)S(1)}, u32[]{:S(2)}, u32[]{:S(2)}) async-start(bf16[16,8,512]{2,1,0:T(8,128)(2,1)} %broadcast_in_dim.49), calls=%async_computation.3 | async-start | bytes 262144 | tf_op jit(solution)/shard_map/all_to_all | solution.py:131

commit v3 on v2

--- a/solution.py
+++ b/solution.py
@@ -45,20 +45,25 @@
     both = jnp.concatenate(
         [key_value_weight, adapter_down_weight.reshape(adapter_down_weight.shape[0], -1)], axis=1
     )
-    products = jnp.dot(normed_token_input, both, preferred_element_type=jnp.float32)
-    base_part = products[:, :column_span]
-    down_all = products[:, column_span:].reshape(request_count, local_adapters, rank_width)
-    local_choice = selected_adapter - group_index * local_adapters
-    picker = (local_choice[:, None] == jnp.arange(local_adapters, dtype=jnp.int32)[None, :]).astype(
-        jnp.float32
+    by_home = normed_token_input.reshape(homes, rows, -1)
+    products = jnp.einsum("hiw,wc->hic", by_home, both, preferred_element_type=jnp.float32)
+    base_part = products[:, :, :column_span]
+    down_all = products[:, :, column_span:].reshape(homes, rows, local_adapters, rank_width)
+    local_choice = (selected_adapter - group_index * local_adapters).reshape(homes, rows)
+    picker = (
+        local_choice[:, :, None] == jnp.arange(local_adapters, dtype=jnp.int32)[None, None, :]
+    ).astype(jnp.float32)
+    mid_part = jnp.einsum("hia,hiaw->hiw", picker, down_all)
+    partial = jnp.concatenate([base_part, mid_part], axis=2)
+    resident_adapters = lax.dynamic_slice_in_dim(selected_adapter, home_index * rows, rows)
+    up_weight_rows = adapter_up_weight[resident_adapters]
+    summed, up_weight_rows = lax.optimization_barrier(
+        (lax.all_to_all(partial, "req", 0, 0, tiled=False), up_weight_rows)
     )
-    mid_part = jnp.einsum("ia,iaw->iw", picker, down_all)
-    partial = jnp.concatenate([base_part, mid_part], axis=1).reshape(homes, rows, -1)
-    summed = jnp.sum(lax.all_to_all(partial, "req", 0, 0, tiled=False), axis=0)
+    summed = jnp.sum(summed, axis=0)
     base_resident = summed[:, :column_span]
     mid_owned = summed[:, column_span:].astype(jnp.bfloat16)
 
-    resident_adapters = lax.dynamic_slice_in_dim(selected_adapter, home_index * rows, rows)
     owner = resident_adapters // local_adapters
     mid_spread = lax.all_to_all(
         jnp.broadcast_to(mid_owned[None], (groups,) + mid_owned.shape), "grp", 0, 0, tiled=False
@@ -67,7 +72,6 @@
     mid_home = mid_spread[owner, request_index]
     is_value = group_index * column_span >= key_width
     mid_used = jnp.where(is_value, mid_home[:, rank_half:], mid_home[:, :rank_half])
-    up_weight_rows = adapter_up_weight[resident_adapters]
     adapter_update = jnp.einsum(
         "ir,irc->ic", mid_used, up_weight_rows, preferred_element_type=jnp.float32
     )
@@ -133,6 +137,19 @@
     )
     attention = attention.transpose(1, 0, 2).reshape(rows, groups * mixed_width)
 
+    targets = departing_target[:, 0]
+    count_out = departing_slots.shape[0]
+    order = jnp.arange(count_out, dtype=jnp.int32)
+    earlier = (targets[:, None] == targets[None, :]) & (order[None, :] < order[:, None])
+    place = jnp.sum(earlier.astype(jnp.int32), axis=1)
+    live_slots = rows * pages
+    capacity = (key_value_pages.shape[0] - live_slots) // homes
+    lands = (targets[None, None, :] == jnp.arange(homes, dtype=jnp.int32)[:, None, None]) & (
+        place[None, None, :] == jnp.arange(capacity, dtype=jnp.int32)[None, :, None]
+    )
+    filled = jnp.any(lands, axis=2)
+    source_slot = jnp.sum(jnp.where(lands, departing_slots[None, None, :], 0), axis=2)
+
     page_slot = page_slot_table[request_index, lengths // page_size]
     offset = lengths % page_size
     mine = offset // slot_tokens == group_index
@@ -142,25 +159,18 @@
     written = key_value_pages.at[page_slot, token_local].set(
         jnp.where(mine[:, None, None, None], fresh, current)
     )
+    attention, written = lax.optimization_barrier((attention, written))
 
-    targets = departing_target[:, 0]
-    count_out = departing_slots.shape[0]
-    order = jnp.arange(count_out, dtype=jnp.int32)
-    earlier = (targets[:, None] == targets[None, :]) & (order[None, :] < order[:, None])
-    place = jnp.sum(earlier.astype(jnp.int32), axis=1)
-    live_slots = rows * pages
-    capacity = (key_value_pages.shape[0] - live_slots) // homes
-    outbound = (
-        jnp.zeros((homes, capacity) + key_value_pages.shape[1:], key_value_pages.dtype)
-        .at[targets, place]
-        .set(written[departing_slots])
+    outbound = jnp.where(
+        filled[:, :, None, None, None, None],
+        written[source_slot],
+        jnp.zeros((), key_value_pages.dtype),
     )
     arrived = lax.all_to_all(outbound, "req", split_axis=0, concat_axis=0, tiled=True)
-    migrated_pool = jnp.concatenate(
-        [
-            written[:live_slots],
-            arrived.reshape((homes * capacity,) + key_value_pages.shape[1:]),
-        ],
+    migrated_pool = lax.dynamic_update_slice_in_dim(
+        written,
+        arrived.reshape((homes * capacity,) + key_value_pages.shape[1:]),
+        live_slots,
         axis=0,
     )
     return (attention, migrated_pool)

time: 143 us -> 141 us (0.986); the launches traced: 140 us -> 140 us
  other arithmetic: 21.3 us -> 16.4 us
  matrix products: 4.13 us -> 7.28 us
  local copies, waits for them, and re-layouts: 31.7 us -> 29.8 us
  waiting for transfers between devices: 32 us -> 33.8 us
  starting transfers between devices: 50.1 us -> 51.7 us
    all_to_all x1, starting transfers between devices: 6.03 us -> 11.5 us  [shards(): lax.all_to_all(jnp.broadcast_to(own_attention[None], (groups,) + own_atte...]
    all_to_all x1, waiting for transfers between devices: 9.8 us -> 5.1 us  [shards(): lax.all_to_all(jnp.broadcast_to(own_attention[None], (groups,) + own_atte...]
    concatenate x4 -> x1, other arithmetic: 4.18 us -> 0.02 us  [shards(): partial = jnp.concatenate([base_part, mid_part], axis=2)]
    scatter x1 -> x0, local copies, waits for them, and re-layouts: 3.75 us -> none  [shards(): outbound = jnp.zeros((homes, capacity) + key_value_pages.shape[1:], key_v...]
    all_to_all x1, waiting for transfers between devices: 10.9 us -> 14.2 us  [shards(): received = lax.all_to_all(parcel, 'grp', 0, 0, tiled=False)]
    all_to_all x1, waiting for transfers between devices: 2.97 us -> 5.65 us  [shards(): lax.all_to_all(jnp.broadcast_to(mid_owned[None], (groups,) + mid_owned.sh...]
    all_to_all x1, starting transfers between devices: 8.49 us -> 5.94 us  [shards(): received = lax.all_to_all(parcel, 'grp', 0, 0, tiled=False)]
    all_to_all x1, waiting for transfers between devices: 6.91 us -> 8.92 us  [shards(): lax.all_to_all(outbound, 'req', split_axis=0, concat_axis=0, tiled=True)]
  transfers between devices with their start and end apart: 5 -> 5, of which waited for: 5 -> 4; matrix products, arithmetic and copies ran while one was open for 19% -> 20% of each run, Pallas kernels for 0% -> 0%
where the time goes in v3:
time: 141 us; the launch traced here: 140 us
  starting transfers between devices  51.7 us (37%)
  waiting for transfers between devices  33.8 us (24%)
  local copies, waits for them, and re-layouts  29.8 us (21%)
  other arithmetic  16.4 us (12%)
  matrix products  7.28 us (5%)
    all_to_all x1, waiting for transfers between devices, shards(): received = lax.all_to_all(parcel, 'grp', 0, 0, tiled=False)  14.2 us
    all_to_all x1, starting transfers between devices, shards(): lax.all_to_all(jnp.broadcast_to(mid_owned[None], (groups,) + mid_owned.sh...  12.6 us
    all_to_all x1, starting transfers between devices, shards(): lax.all_to_all(jnp.broadcast_to(own_attention[None], (groups,) + own_atte...  11.5 us
    all_to_all x1, starting transfers between devices, shards(): lax.all_to_all(partial, 'req', 0, 0, tiled=False)  11 us
    all_to_all x1, starting transfers between devices, shards(): lax.all_to_all(outbound, 'req', split_axis=0, concat_axis=0, tiled=True)  10.7 us
    all_to_all x1, waiting for transfers between devices, shards(): lax.all_to_all(outbound, 'req', split_axis=0, concat_axis=0, tiled=True)  8.92 us
    all_to_all x1, starting transfers between devices, shards(): received = lax.all_to_all(parcel, 'grp', 0, 0, tiled=False)  5.94 us
    unnamed x25, local copies, waits for them, and re-layouts  5.75 us
  transfers between devices with their start and end apart: 5, of which 4 were waited for; matrix products, arithmetic and copies ran while one was open for 20% of the time, Pallas kernels for 0%

profile of v3, /device:TPU:1, one launch (start us, length us, event | category | flops | bytes accessed | tf_op | source)
XLA Modules:
  0.0 140.0 jit_solution(12344752869634203426)
XLA Ops:
  0.7 1.5 %copy.107 = bf16[320,1,2,8,128]{4,3,2,1,0:T(8,128)(2,1)S(1)} copy(bf16[320,1,2,8,128]{4,3,2,1,0:T(8,128)(2,1)} %param.17) | data formatting | bytes 2621440
  5.3 1.5 %fusion.2 = f32[32,8,1,128]{3,2,1,0:T(1,128)S(1)} fusion(bf16[32,8,8,128]{3,2,0,1:T(8,128)(2,1)} %bitcast.128, pred[32,8,8,1]{2,1,0,3:T(8,128)(4,1)S(1)} %fusion.14), kind=kOutput, calls=%fused_computation.11 | convolution fusion | flops 524288 | bytes 657408 | tf_op jit(solution)/shard_map/hia,hiaw->hiw/dot_general | solution.py:56
  7.7 11.0 %all-to-all-start = ((f32[32,8,256]{2,1,0:T(8,128)}), f32[32,8,256]{2,1,0:T(8,128)}, u32[]{:S(2)}, u32[]{:S(2)}) async-start(f32[32,8,256]{2,1,0:T(8,128)} %copy.49), calls=%async_computation | async-start | bytes 524288 | tf_op jit(solution)/shard_map/all_to_all | solution.py:61
  19.5 1.8 %gather_fusion = bf16[256,2,8,128]{3,2,1,0:T(8,128)(2,1)} fusion(bf16[320,2,8,128]{3,2,1,0:T(8,128)(2,1)S(1)} %bitcast.121, s32[1024]{0:T(1024)S(1)} %pad_clamp_fusion.2), kind=kCustom, calls=%fused_computation | custom fusion | bytes 2098176 | tf_op jit(solution)/shard_map/gather | solution.py:80
  21.3 2.3 %fusion.43 = (bf16[8,32,1,8,128]{4,3,2,1,0:T(8,128)(2,1)}, bf16[8,32,1,8,128]{4,3,2,1,0:T(8,128)(2,1)}) fusion(bf16[8,32,2,8,128]{4,3,2,1,0:T(8,128)(2,1)} %bitcast.124), kind=kLoop, calls=%fused_computation.115 | loop fusion | bytes 2097152 | tf_op jit(solution)/shard_map/slice | solution.py:82
  24.2 2.2 %fusion.44 = (f32[8,8,8]{2,1,0:T(8,128)S(1)}, f32[8,8,8,32]{3,2,1,0:T(8,128)}) fusion(bf16[8,8,8,128]{3,0,2,1:T(8,128)(2,1)} %bitcast.141, bf16[8,32,1,8,128]{4,3,2,1,0:T(8,128)(2,1)} %get-tuple-element.15, pred[8,32]{1,0:T(8,128)(4,1)S(1)} %broadcast_compare_fusion), kind=kOutput, calls=%fused_computation.116 | convolution fusion | flops 4242944 | bytes 723200 | tf_op jit(solution)/shard_map/ihgd,inhd->ihgn/dot_general | solution.py:84
  27.0 1.2 gather_fusion.1
  28.2 2.1 %fusion.6 = f32[8,8,8,128]{3,2,1,0:T(8,128)} fusion(bf16[8,32,1,8,128]{4,3,2,1,0:T(8,128)(2,1)} %get-tuple-element.14, f32[8,8,8,32]{3,2,1,0:T(8,128)} %get-tuple-element.25, f32[8,8,8]{2,1,0:T(8,128)S(1)} %get-tuple-element.24, pred[8,32]{1,0:T(8,128)(4,1)S(1)} %broadcast_compare_fusion), kind=kOutput, calls=%fused_computation.18 | convolution fusion | flops 4227072 | bytes 854272 | tf_op jit(solution)/shard_map/ihgn,inhd->ihgd/dot_general | solution.py:93
  30.4 1.0 reduce_sum.57
  32.0 12.6 %all-to-all-start.1 = ((bf16[16,8,128]{2,1,0:T(8,128)(2,1)}), bf16[16,8,128]{2,1,0:T(8,128)(2,1)}, u32[]{:S(2)}, u32[]{:S(2)}) async-start(bf16[16,8,128]{2,1,0:T(8,128)(2,1)} %broadcast_in_dim.63), calls=%async_computation.1 | async-start | bytes 65536 | tf_op jit(solution)/shard_map/all_to_all | solution.py:68
  44.6 1.2 fusion.9
  47.0 1.7 %reshape.205 = f32[8,16,512]{2,1,0:T(8,128)} reshape(f32[8,8,8,128]{3,2,1,0:T(8,128)} %fusion.6) | data formatting | bytes 524288 | tf_op jit(solution)/shard_map/reshape | solution.py:99
  48.7 1.8 %copy.50 = f32[8,16,512]{2,0,1:T(8,128)} copy(f32[8,16,512]{2,1,0:T(8,128)} %reshape.205) | data formatting | bytes 524288 | tf_op jit(solution)/shard_map/reshape | solution.py:99
  50.5 5.6 %all-to-all-done.1 = bf16[16,8,128]{2,1,0:T(8,128)(2,1)} async-done(((bf16[16,8,128]{2,1,0:T(8,128)(2,1)}), bf16[16,8,128]{2,1,0:T(8,128)(2,1)}, u32[]{:S(2)}, u32[]{:S(2)}) %all-to-all-start.1) | async-done | bytes 32800 | tf_op jit(solution)/shard_map/all_to_all | solution.py:68
  56.1 1.9 %gather_fusion.2 = bf16[8,128]{1,0:T(8,128)(2,1)} fusion(bf16[16,8,128]{2,1,0:T(8,128)(2,1)} %all-to-all-done.1, s32[8]{0:T(128)S(1)} %get-tuple-element.27), kind=kCustom, calls=%fused_computation.2 | custom fusion | bytes 4160 | tf_op jit(solution)/shard_map/gather | solution.py:72
  58.9 1.0 fusion.24
  60.0 1.8 %maximum_bitcast_fusion.2 = f32[16,8,648]{2,1,0:T(8,128)} fusion(f32[8,16,128]{2,0,1:T(8,128)S(1)} %broadcast_in_dim.64, f32[8,16,4]{2,0,1:T(8,128)S(1)} %copy.52, f32[8,16,4]{2,0,1:T(8,128)S(1)} %copy.51, f32[8,16,512]{2,0,1:T(8,128)} %copy.50), kind=kLoop, calls=%fused_computation.21 | loop fusion | flops 248832 | bytes 663552 | tf_op jit(solution)/shard_map/transpose | solution.py:107
  61.8 5.9 %all-to-all-start.2 = ((f32[16,8,648]{2,1,0:T(8,128)}), f32[16,8,648]{2,1,0:T(8,128)}, u32[]{:S(2)}, u32[]{:S(2)}) async-start(f32[16,8,648]{2,1,0:T(8,128)} %maximum_bitcast_fusion.2), calls=%async_computation.2 | async-start | bytes 786432 | tf_op jit(solution)/shard_map/all_to_all | solution.py:108
  71.7 14.2 %all-to-all-done.2 = f32[16,8,648]{2,1,0:T(8,128)} async-done(((f32[16,8,648]{2,1,0:T(8,128)}), f32[16,8,648]{2,1,0:T(8,128)}, u32[]{:S(2)}, u32[]{:S(2)}) %all-to-all-start.2) | async-done | bytes 331808 | tf_op jit(solution)/shard_map/all_to_all | solution.py:108
  85.9 1.0 fusion.18
  88.5 1.0 fusion.16
  89.9 1.1 fusion.8
  91.7 11.5 %all-to-all-start.3 = ((bf16[16,8,512]{2,1,0:T(8,128)(2,1)}), bf16[16,8,512]{2,1,0:T(8,128)(2,1)S(1)}, u32[]{:S(2)}, u32[]{:S(2)}) async-start(bf16[16,8,512]{2,1,0:T(8,128)(2,1)} %broadcast_in_dim.65), calls=%async_computation.3 | async-start | bytes 262144 | tf_op jit(solution)/shard_map/all_to_all | solution.py:135
  103.2 1.2 gather_fusion.4
  107.3 1.5 %maximum_select_fusion = bf16[8,2,8,128]{3,2,1,0:T(8,128)(2,1)} fusion(bf16[8,2,8,128]{3,2,1,0:T(8,128)(2,1)} %gather_fusion.4, bf16[8,1,8,128]{3,2,1,0:T(8,128)(2,1)S(1)} %bitcast.134, bf16[8,1,8,128]{3,2,1,0:T(8,128)(2,1)S(1)} %bitcast.135, pred[8]{0:T(512)(128)(4,1)S(1)} %fusion.29), kind=kLoop, calls=%fused_computation.45 | loop fusion | flops 32768 | bytes 98312 | tf_op jit(solution)/shard_map/jit(_where)/select_n | solution.py:160
  108.7 1.3 scatter_fusion
  110.0 5.1 %all-to-all-done.3 = bf16[16,8,512]{2,1,0:T(8,128)(2,1)S(1)} async-done(((bf16[16,8,512]{2,1,0:T(8,128)(2,1)}), bf16[16,8,512]{2,1,0:T(8,128)(2,1)S(1)}, u32[]{:S(2)}, u32[]{:S(2)}) %all-to-all-start.3) | async-done | bytes 131104 | tf_op jit(solution)/shard_map/all_to_all | solution.py:135
  115.1 1.3 gather_fusion.5
  116.5 1.8 %broadcast_select_fusion = bf16[32,2,1,2,8,128]{5,4,3,1,2,0:T(8,128)(2,1)} fusion(bf16[32,2,1,2,8,128]{5,4,3,1,2,0:T(8,128)(2,1)} %bitcast.126, pred[32,2]{1,0:T(8,128)(4,1)S(1)} %copy.56), kind=kLoop, calls=%fused_computation.26 | loop fusion | flops 131072 | bytes 524352 | tf_op jit(solution)/shard_map/jit(_where)/select_n | solution.py:164
  118.2 10.7 %all-to-all-start.4 = ((bf16[32,2,1,2,8,128]{5,4,3,1,2,0:T(8,128)(2,1)}), bf16[32,2,1,2,8,128]{5,4,3,1,2,0:T(8,128)(2,1)}, u32[]{:S(2)}, u32[]{:S(2)}) async-start(bf16[32,2,1,2,8,128]{5,4,3,1,2,0:T(8,128)(2,1)} %broadcast_select_fusion), calls=%async_computation.4 | async-start | bytes 524288 | tf_op jit(solution)/shard_map/all_to_all | solution.py:169
  129.0 8.9 %all-to-all-done.4 = bf16[32,2,1,2,8,128]{5,4,3,1,2,0:T(8,128)(2,1)} async-done(((bf16[32,2,1,2,8,128]{5,4,3,1,2,0:T(8,128)(2,1)}), bf16[32,2,1,2,8,128]{5,4,3,1,2,0:T(8,128)(2,1)}, u32[]{:S(2)}, u32[]{:S(2)}) %all-to-all-start.4) | async-done | bytes 262176 | tf_op jit(solution)/shard_map/all_to_all | solution.py:169
  137.9 1.0 constant_dynamic-update-slice_fusion
  (75 shorter events, 19.4 us)
Async XLA Ops:
  0.6 26.4 %copy-start = (bf16[128,64,128]{2,1,0:T(8,128)(2,1)S(1)}, bf16[128,64,128]{2,1,0:T(8,128)(2,1)}, u32[]{:S(2)}) copy-start(bf16[128,64,128]{2,1,0:T(8,128)(2,1)} %param.14) | copy-start | bytes 6291460
  0.6 1.7 %copy-start.7 = (bf16[256,256]{1,0:T(8,128)(2,1)S(1)}, bf16[256,256]{1,0:T(8,128)(2,1)}, u32[]{:S(2)}) copy-start(bf16[256,256]{1,0:T(8,128)(2,1)} %param.11) | copy-start | bytes 393220
  0.7 1.7 %copy-start.8 = (bf16[256,128]{1,0:T(8,128)(2,1)S(1)}, bf16[256,128]{1,0:T(8,128)(2,1)}, u32[]{:S(2)}) copy-start(bf16[256,128]{1,0:T(8,128)(2,1)} %param.12) | copy-start | bytes 196612
  0.7 1.6 %copy-start.3 = (bf16[256,8,128]{2,1,0:T(8,128)(2,1)S(1)}, bf16[256,8,128]{2,1,0:T(8,128)(2,1)}, u32[]{:S(2)}) copy-start(bf16[256,8,128]{2,1,0:T(8,128)(2,1)} %param.13) | copy-start | bytes 1572868
  2.7 1.0 copy-start.4
  5.3 13.5 %copy-start.6 = (s32[8]{0:T(128)S(1)}, s32[8]{0:T(128)}, u32[]{:S(2)}) copy-start(s32[8]{0:T(128)} %param.18) | copy-start | bytes 100
  5.3 13.5 %copy-start.1 = (s32[8,32]{1,0:T(8,128)S(1)}, s32[8,32]{1,0:T(8,128)}, u32[]{:S(2)}) copy-start(s32[8,32]{1,0:T(8,128)} %param.19) | copy-start | bytes 3076
  7.7 22.7 %all-to-all-start = ((f32[32,8,256]{2,1,0:T(8,128)}), f32[32,8,256]{2,1,0:T(8,128)}, u32[]{:S(2)}, u32[]{:S(2)}) async-start(f32[32,8,256]{2,1,0:T(8,128)} %copy.49), calls=%async_computation | async-start | bytes 524288 | tf_op jit(solution)/shard_map/all_to_all | solution.py:61
  32.0 24.1 %all-to-all-start.1 = ((bf16[16,8,128]{2,1,0:T(8,128)(2,1)}), bf16[16,8,128]{2,1,0:T(8,128)(2,1)}, u32[]{:S(2)}, u32[]{:S(2)}) async-start(bf16[16,8,128]{2,1,0:T(8,128)(2,1)} %broadcast_in_dim.63), calls=%async_computation.1 | async-start | bytes 65536 | tf_op jit(solution)/shard_map/all_to_all | solution.py:68
  61.8 46.9 %copy-start.5 = (s32[8]{0:T(128)S(1)}, s32[8]{0:T(128)}, u32[]{:S(2)}) copy-start(s32[8]{0:T(128)} %get-tuple-element.23) | copy-start | bytes 100
  61.8 24.1 %all-to-all-start.2 = ((f32[16,8,648]{2,1,0:T(8,128)}), f32[16,8,648]{2,1,0:T(8,128)}, u32[]{:S(2)}, u32[]{:S(2)}) async-start(f32[16,8,648]{2,1,0:T(8,128)} %maximum_bitcast_fusion.2), calls=%async_computation.2 | async-start | bytes 786432 | tf_op jit(solution)/shard_map/all_to_all | solution.py:108
  91.7 23.4 %all-to-all-start.3 = ((bf16[16,8,512]{2,1,0:T(8,128)(2,1)}), bf16[16,8,512]{2,1,0:T(8,128)(2,1)S(1)}, u32[]{:S(2)}, u32[]{:S(2)}) async-start(bf16[16,8,512]{2,1,0:T(8,128)(2,1)} %broadcast_in_dim.65), calls=%async_computation.3 | async-start | bytes 262144 | tf_op jit(solution)/shard_map/all_to_all | solution.py:135
  118.2 19.6 %all-to-all-start.4 = ((bf16[32,2,1,2,8,128]{5,4,3,1,2,0:T(8,128)(2,1)}), bf16[32,2,1,2,8,128]{5,4,3,1,2,0:T(8,128)(2,1)}, u32[]{:S(2)}, u32[]{:S(2)}) async-start(bf16[32,2,1,2,8,128]{5,4,3,1,2,0:T(8,128)(2,1)} %broadcast_select_fusion), calls=%async_computation.4 | async-start | bytes 524288 | tf_op jit(solution)/shard_map/all_to_all | solution.py:169
  138.9 1.1 copy-start.2

commit v4 on v3

--- a/solution.py
+++ b/solution.py
@@ -62,20 +62,11 @@
     )
     summed = jnp.sum(summed, axis=0)
     base_resident = summed[:, :column_span]
-    mid_owned = summed[:, column_span:].astype(jnp.bfloat16)
 
     owner = resident_adapters // local_adapters
-    mid_spread = lax.all_to_all(
-        jnp.broadcast_to(mid_owned[None], (groups,) + mid_owned.shape), "grp", 0, 0, tiled=False
-    )
     request_index = jnp.arange(rows, dtype=jnp.int32)
-    mid_home = mid_spread[owner, request_index]
     is_value = group_index * column_span >= key_width
-    mid_used = jnp.where(is_value, mid_home[:, rank_half:], mid_home[:, :rank_half])
-    adapter_update = jnp.einsum(
-        "ir,irc->ic", mid_used, up_weight_rows, preferred_element_type=jnp.float32
-    )
-    fresh_columns = (base_resident + adapter_scale * adapter_update).astype(jnp.bfloat16)
+    mixed_width = heads_per_target * head_dim
 
     gathered = key_value_pages[page_slot_table][:, :, 0]
     keys = gathered[:, :, 0]
@@ -96,46 +87,67 @@
 
     parcel = jnp.concatenate(
         [
-            local_mixed.reshape(rows, groups, heads_per_target * head_dim),
+            local_mixed.reshape(rows, groups, mixed_width),
             local_top.reshape(rows, groups, heads_per_target),
             local_total.reshape(rows, groups, heads_per_target),
             jnp.broadcast_to(
-                fresh_columns.astype(jnp.float32)[:, None, :], (rows, groups, column_span)
+                summed[:, None, column_span:], (rows, groups, summed.shape[1] - column_span)
             ),
         ],
         axis=2,
     ).transpose(1, 0, 2)
     received = lax.all_to_all(parcel, "grp", 0, 0, tiled=False)
-    mixed_width = heads_per_target * head_dim
     shard_mixed = received[:, :, :mixed_width].reshape(groups, rows, heads_per_target, head_dim)
     shard_top = received[:, :, mixed_width : mixed_width + heads_per_target]
     shard_total = received[:, :, mixed_width + heads_per_target : mixed_width + 2 * heads_per_target]
-    new_all = received[:, :, mixed_width + 2 * heads_per_target :].astype(jnp.bfloat16)
-    new_all = new_all.transpose(1, 0, 2).reshape(rows, groups * column_span)
+    mid_spread = received[:, :, mixed_width + 2 * heads_per_target :]
+    top_own = jnp.max(shard_top, axis=0)
+    shard_scale = jnp.exp(shard_top - top_own[None])
+    total_own = jnp.sum(shard_total * shard_scale, axis=0)
+    mixed_own = jnp.sum(shard_mixed * shard_scale[..., None], axis=0)
+
+    mid_home = mid_spread[owner, request_index].astype(jnp.bfloat16)
+    mid_used = jnp.where(is_value, mid_home[:, rank_half:], mid_home[:, :rank_half])
+    adapter_update = jnp.einsum(
+        "ir,irc->ic", mid_used, up_weight_rows, preferred_element_type=jnp.float32
+    )
+    fresh_columns = (base_resident + adapter_scale * adapter_update).astype(jnp.bfloat16)
+
+    merged = jnp.concatenate(
+        [
+            mixed_own.reshape(rows, mixed_width),
+            top_own,
+            total_own,
+            fresh_columns.astype(jnp.float32),
+        ],
+        axis=1,
+    )
+    everything = lax.all_to_all(
+        jnp.broadcast_to(merged[None], (groups,) + merged.shape), "grp", 0, 0, tiled=False
+    ).transpose(1, 0, 2)
+    all_mixed = everything[:, :, :mixed_width].reshape(rows, query_heads, head_dim)
+    all_top = everything[:, :, mixed_width : mixed_width + heads_per_target].reshape(rows, query_heads)
+    all_total = everything[
+        :, :, mixed_width + heads_per_target : mixed_width + 2 * heads_per_target
+    ].reshape(rows, query_heads)
+    new_all = everything[:, :, mixed_width + 2 * heads_per_target :].astype(jnp.bfloat16)
+    new_all = new_all.reshape(rows, groups * column_span)
     new_keys = new_all[:, :key_width].reshape(rows, heads, head_dim)
     new_values = new_all[:, key_width:].reshape(rows, heads, head_dim)
 
-    head_of_target = group_index * heads_per_target // (query_heads // heads)
-    own_query = lax.dynamic_slice_in_dim(
-        queries, group_index * mixed_width, mixed_width, axis=1
-    ).reshape(rows, heads_per_target, head_dim)
-    own_key = lax.dynamic_index_in_dim(new_keys, head_of_target, 1, False)
-    own_value = lax.dynamic_index_in_dim(new_values, head_of_target, 1, False)
-    new_score = jnp.einsum(
-        "ihd,id->ih", own_query, own_key, preferred_element_type=jnp.float32
-    ) / math.sqrt(head_dim)
-    top = jnp.maximum(jnp.max(shard_top, axis=0), new_score)
-    shard_scale = jnp.exp(shard_top - top[None])
+    new_score = (
+        jnp.einsum("ihgd,ihd->ihg", query, new_keys, preferred_element_type=jnp.float32)
+        / math.sqrt(head_dim)
+    ).reshape(rows, query_heads)
+    top = jnp.maximum(all_top, new_score)
+    old_scale = jnp.exp(all_top - top)
     new_weight = jnp.exp(new_score - top)
-    total = jnp.sum(shard_total * shard_scale, axis=0) + new_weight
-    mixed = jnp.sum(shard_mixed * shard_scale[..., None], axis=0) + new_weight[
-        ..., None
-    ] * own_value.astype(jnp.float32)[:, None, :]
-    own_attention = (mixed / total[..., None]).astype(jnp.bfloat16).reshape(rows, mixed_width)
-    attention = lax.all_to_all(
-        jnp.broadcast_to(own_attention[None], (groups,) + own_attention.shape), "grp", 0, 0, tiled=False
-    )
-    attention = attention.transpose(1, 0, 2).reshape(rows, groups * mixed_width)
+    total = all_total * old_scale + new_weight
+    new_value_rows = jnp.broadcast_to(
+        new_values.astype(jnp.float32)[:, :, None, :], (rows, heads, query_heads // heads, head_dim)
+    ).reshape(rows, query_heads, head_dim)
+    mixed = all_mixed * old_scale[..., None] + new_weight[..., None] * new_value_rows
+    attention = (mixed / total[..., None]).astype(jnp.bfloat16).reshape(rows, -1)
 
     targets = departing_target[:, 0]
     count_out = departing_slots.shape[0]
@@ -159,7 +171,6 @@
     written = key_value_pages.at[page_slot, token_local].set(
         jnp.where(mine[:, None, None, None], fresh, current)
     )
-    attention, written = lax.optimization_barrier((attention, written))
 
     outbound = jnp.where(
         filled[:, :, None, None, None, None],

time: 141 us -> 146 us (1.035)
  waiting for transfers between devices: 33.8 us -> 40.2 us
  other arithmetic: 16.4 us -> 13.9 us
  local copies, waits for them, and re-layouts: 29.8 us -> 31.5 us
    all_to_all x2 -> x1, starting transfers between devices: 24.1 us -> 12.6 us  [shards(): lax.all_to_all(jnp.broadcast_to(merged[None], (groups,) + merged.shape),...]
    all_to_all x1, starting transfers between devices: 5.94 us -> 12.7 us  [shards(): received = lax.all_to_all(parcel, 'grp', 0, 0, tiled=False)]
    slice x1 -> x6, local copies, waits for them, and re-layouts: 0.01 us -> 5.18 us  [the longest x2 1.76 us: shards(): everything[:, :, mixed_width:mixed_width + heads_per_target]]
    all_to_all x2 -> x1, waiting for transfers between devices: 10.7 us -> 15.8 us  [shards(): lax.all_to_all(jnp.broadcast_to(merged[None], (groups,) + merged.shape),...]
    all_to_all x1, starting transfers between devices: 10.7 us -> 14.3 us  [shards(): lax.all_to_all(outbound, 'req', split_axis=0, concat_axis=0, tiled=True)]
    all_to_all x1, waiting for transfers between devices: 14.2 us -> 17.4 us  [shards(): received = lax.all_to_all(parcel, 'grp', 0, 0, tiled=False)]
    all_to_all x1, waiting for transfers between devices: 8.92 us -> 6.94 us  [shards(): lax.all_to_all(outbound, 'req', split_axis=0, concat_axis=0, tiled=True)]
    convert_element_type x2, other arithmetic: 0.09 us -> 1.89 us  [the longest x1 1.88 us: shards(): (mixed / total[..., None]).astype(jnp.bfloat16).reshape(rows, -1)]
  transfers between devices with their start and end apart: 5 -> 4, of which waited for: 4 -> 3; matrix products, arithmetic and copies ran while one was open for 20% -> 14% of each run, Pallas kernels for 0% -> 0%
where the time goes in v4:
time: 146 us; the launch traced here: 144 us
  starting transfers between devices  50.6 us (35%)
  waiting for transfers between devices  40.2 us (28%)
  local copies, waits for them, and re-layouts  31.5 us (22%)
  other arithmetic  13.9 us (10%)
  matrix products  7.24 us (5%)
    all_to_all x1, waiting for transfers between devices, shards(): received = lax.all_to_all(parcel, 'grp', 0, 0, tiled=False)  17.4 us
    all_to_all x1, waiting for transfers between devices, shards(): lax.all_to_all(jnp.broadcast_to(merged[None], (groups,) + merged.shape),...  15.8 us
    all_to_all x1, starting transfers between devices, shards(): lax.all_to_all(outbound, 'req', split_axis=0, concat_axis=0, tiled=True)  14.3 us
    all_to_all x1, starting transfers between devices, shards(): received = lax.all_to_all(parcel, 'grp', 0, 0, tiled=False)  12.7 us
    all_to_all x1, starting transfers between devices, shards(): lax.all_to_all(jnp.broadcast_to(merged[None], (groups,) + merged.shape),...  12.6 us
    all_to_all x1, starting transfers between devices, shards(): lax.all_to_all(partial, 'req', 0, 0, tiled=False)  11 us
    all_to_all x1, waiting for transfers between devices, shards(): lax.all_to_all(outbound, 'req', split_axis=0, concat_axis=0, tiled=True)  6.94 us
    unnamed x37, local copies, waits for them, and re-layouts  5.13 us
  transfers between devices with their start and end apart: 4, of which 3 were waited for; matrix products, arithmetic and copies ran while one was open for 14% of the time, Pallas kernels for 0%

profile of v4, /device:TPU:1, one launch (start us, length us, event | category | flops | bytes accessed | tf_op | source)
XLA Modules:
  0.0 144.4 jit_solution(6475212551836167909)
XLA Ops:
  0.7 1.5 %copy.110 = bf16[320,1,2,8,128]{4,3,2,1,0:T(8,128)(2,1)S(1)} copy(bf16[320,1,2,8,128]{4,3,2,1,0:T(8,128)(2,1)} %param.17) | data formatting | bytes 2621440
  5.3 1.5 %fusion.2 = f32[32,8,1,128]{3,2,1,0:T(1,128)S(1)} fusion(bf16[32,8,8,128]{3,2,0,1:T(8,128)(2,1)} %bitcast.141, pred[32,8,8,1]{2,1,0,3:T(8,128)(4,1)S(1)} %fusion.15), kind=kOutput, calls=%fused_computation.11 | convolution fusion | flops 524288 | bytes 657408 | tf_op jit(solution)/shard_map/hia,hiaw->hiw/dot_general | solution.py:56
  7.7 11.0 %all-to-all-start = ((f32[32,8,256]{2,1,0:T(8,128)}), f32[32,8,256]{2,1,0:T(8,128)}, u32[]{:S(2)}, u32[]{:S(2)}) async-start(f32[32,8,256]{2,1,0:T(8,128)} %copy.54), calls=%async_computation | async-start | bytes 524288 | tf_op jit(solution)/shard_map/all_to_all | solution.py:61
  19.5 1.8 %gather_fusion = bf16[256,2,8,128]{3,2,1,0:T(8,128)(2,1)} fusion(bf16[320,2,8,128]{3,2,1,0:T(8,128)(2,1)S(1)} %bitcast.132, s32[1024]{0:T(1024)S(1)} %pad_clamp_fusion.2), kind=kCustom, calls=%fused_computation | custom fusion | bytes 2098176 | tf_op jit(solution)/shard_map/gather | solution.py:71
  21.3 2.1 %fusion.47 = (bf16[8,32,1,8,128]{4,3,2,1,0:T(8,128)(2,1)}, bf16[8,32,1,8,128]{4,3,2,1,0:T(8,128)(2,1)S(1)}) fusion(bf16[8,32,2,8,128]{4,3,2,1,0:T(8,128)(2,1)} %bitcast.135), kind=kLoop, calls=%fused_computation.117 | loop fusion | bytes 2097152 | tf_op jit(solution)/shard_map/slice | solution.py:73
  23.5 1.1 fusion.49
  24.6 1.2 fusion.11
  28.3 2.2 %fusion.6 = f32[8,8,8,128]{3,2,1,0:T(8,128)} fusion(bf16[8,32,1,8,128]{4,3,2,1,0:T(8,128)(2,1)} %get-tuple-element.11, f32[8,8,8,32]{3,2,1,0:T(8,128)} %get-tuple-element.24, f32[8,8,8]{2,1,0:T(8,128)S(1)} %get-tuple-element.23, pred[8,32]{1,0:T(8,128)(4,1)S(1)} %broadcast_compare_fusion), kind=kOutput, calls=%fused_computation.18 | convolution fusion | flops 4227072 | bytes 854272 | tf_op jit(solution)/shard_map/ihgn,inhd->ihgd/dot_general | solution.py:84
  30.4 1.7 %reshape.240 = f32[8,16,512]{2,1,0:T(8,128)} reshape(f32[8,8,8,128]{3,2,1,0:T(8,128)} %fusion.6) | data formatting | bytes 524288 | tf_op jit(solution)/shard_map/reshape | solution.py:90
  32.1 1.8 %copy.55 = f32[8,16,512]{2,0,1:T(8,128)} copy(f32[8,16,512]{2,1,0:T(8,128)} %reshape.240) | data formatting | bytes 524288 | tf_op jit(solution)/shard_map/reshape | solution.py:90
  34.0 1.2 gather_fusion.1
  35.2 1.0 reduce_sum.57
  36.3 1.9 %maximum_bitcast_fusion.2 = f32[16,8,648]{2,1,0:T(8,128)} fusion(f32[8,16,128]{2,0,1:T(8,128)S(1)} %broadcast_in_dim.63, f32[8,16,4]{2,0,1:T(8,128)S(1)} %copy.57, f32[8,16,4]{2,0,1:T(8,128)} %copy.56, f32[8,16,512]{2,0,1:T(8,128)} %copy.55), kind=kLoop, calls=%fused_computation.21 | loop fusion | flops 248832 | bytes 663552 | tf_op jit(solution)/shard_map/transpose | solution.py:98
  38.1 12.7 %all-to-all-start.1 = ((f32[16,8,648]{2,1,0:T(8,128)}), f32[16,8,648]{2,1,0:T(8,128)}, u32[]{:S(2)}, u32[]{:S(2)}) async-start(f32[16,8,648]{2,1,0:T(8,128)} %maximum_bitcast_fusion.2), calls=%async_computation.1 | async-start | bytes 786432 | tf_op jit(solution)/shard_map/all_to_all | solution.py:99
  50.9 17.4 %all-to-all-done.1 = f32[16,8,648]{2,1,0:T(8,128)} async-done(((f32[16,8,648]{2,1,0:T(8,128)}), f32[16,8,648]{2,1,0:T(8,128)}, u32[]{:S(2)}, u32[]{:S(2)}) %all-to-all-start.1) | async-done | bytes 331808 | tf_op jit(solution)/shard_map/all_to_all | solution.py:99
  68.3 1.0 slice.96
  70.0 1.0 fusion.28
  71.9 1.0 fusion.20
  73.1 1.1 fusion.8
  75.0 12.6 %all-to-all-start.2 = ((f32[16,8,648]{2,1,0:T(8,128)}), f32[16,8,648]{2,1,0:T(8,128)}, u32[]{:S(2)}, u32[]{:S(2)}) async-start(f32[16,8,648]{2,1,0:T(8,128)} %broadcast_in_dim.64), calls=%async_computation.2 | async-start | bytes 786432 | tf_op jit(solution)/shard_map/all_to_all | solution.py:125
  87.8 1.2 gather_fusion.4
  89.6 15.8 %all-to-all-done.2 = f32[16,8,648]{2,1,0:T(8,128)} async-done(((f32[16,8,648]{2,1,0:T(8,128)}), f32[16,8,648]{2,1,0:T(8,128)}, u32[]{:S(2)}, u32[]{:S(2)}) %all-to-all-start.2) | async-done | bytes 331808 | tf_op jit(solution)/shard_map/all_to_all | solution.py:125
  106.3 1.7 %slice.97 = f32[8,16,512]{2,0,1:T(8,128)} slice(f32[8,16,648]{2,0,1:T(8,128)} %bitcast.20), slice={[0:8], [0:16], [0:512]} | slice | bytes 524288 | tf_op jit(solution)/shard_map/slice | solution.py:128
  108.0 1.0 fusion.48
  111.2 1.1 fusion.17
  116.0 1.3 gather_fusion.5
  117.4 1.8 %broadcast_select_fusion = bf16[32,2,1,2,8,128]{5,4,3,1,2,0:T(8,128)(2,1)} fusion(bf16[32,2,1,2,8,128]{5,4,3,1,2,0:T(8,128)(2,1)} %bitcast.139, pred[32,2]{1,0:T(8,128)(4,1)S(1)} %copy.61), kind=kLoop, calls=%fused_computation.31 | loop fusion | flops 131072 | bytes 524352 | tf_op jit(solution)/shard_map/jit(_where)/select_n | solution.py:175
  119.1 14.3 %all-to-all-start.3 = ((bf16[32,2,1,2,8,128]{5,4,3,1,2,0:T(8,128)(2,1)}), bf16[32,2,1,2,8,128]{5,4,3,1,2,0:T(8,128)(2,1)}, u32[]{:S(2)}, u32[]{:S(2)}) async-start(bf16[32,2,1,2,8,128]{5,4,3,1,2,0:T(8,128)(2,1)} %broadcast_select_fusion), calls=%async_computation.3 | async-start | bytes 524288 | tf_op jit(solution)/shard_map/all_to_all | solution.py:180
  133.5 1.9 %fusion.9 = bf16[8,8192]{1,0:T(8,128)(2,1)} fusion(f32[8,8192]{1,0:T(8,128)S(1)} %bitcast.138, f32[8,8192]{1,0:T(8,128)} %bitcast.137, f32[8,64]{0,1:T(8,128)S(1)} %get-tuple-element.6, f32[8,64]{0,1:T(8,128)S(1)} %get-tuple-element.8, f32[8,64]{0,1:T(8,128)S(1)} %get-tuple-element.7), kind=kLoop, calls=%fused_computation.26 | loop fusion | flops 327680 | bytes 661504 | tf_op jit(solution)/shard_map/convert_element_type | solution.py:150
  135.4 6.9 %all-to-all-done.3 = bf16[32,2,1,2,8,128]{5,4,3,1,2,0:T(8,128)(2,1)} async-done(((bf16[32,2,1,2,8,128]{5,4,3,1,2,0:T(8,128)(2,1)}), bf16[32,2,1,2,8,128]{5,4,3,1,2,0:T(8,128)(2,1)}, u32[]{:S(2)}, u32[]{:S(2)}) %all-to-all-start.3) | async-done | bytes 262176 | tf_op jit(solution)/shard_map/all_to_all | solution.py:180
  142.3 1.0 constant_dynamic-update-slice_fusion
  143.3 1.0 copy-done.2
  (87 shorter events, 17.7 us)
Async XLA Ops:
  0.6 33.4 %copy-start = (bf16[128,64,128]{2,1,0:T(8,128)(2,1)S(1)}, bf16[128,64,128]{2,1,0:T(8,128)(2,1)}, u32[]{:S(2)}) copy-start(bf16[128,64,128]{2,1,0:T(8,128)(2,1)} %param.14) | copy-start | bytes 6291460
  0.6 1.7 %copy-start.13 = (bf16[256,256]{1,0:T(8,128)(2,1)S(1)}, bf16[256,256]{1,0:T(8,128)(2,1)}, u32[]{:S(2)}) copy-start(bf16[256,256]{1,0:T(8,128)(2,1)} %param.11) | copy-start | bytes 393220
  0.7 1.7 %copy-start.15 = (bf16[256,128]{1,0:T(8,128)(2,1)S(1)}, bf16[256,128]{1,0:T(8,128)(2,1)}, u32[]{:S(2)}) copy-start(bf16[256,128]{1,0:T(8,128)(2,1)} %param.12) | copy-start | bytes 196612
  0.7 1.6 %copy-start.3 = (bf16[256,8,128]{2,1,0:T(8,128)(2,1)S(1)}, bf16[256,8,128]{2,1,0:T(8,128)(2,1)}, u32[]{:S(2)}) copy-start(bf16[256,8,128]{2,1,0:T(8,128)(2,1)} %param.13) | copy-start | bytes 1572868
  2.7 1.0 copy-start.8
  5.3 13.5 %copy-start.11 = (s32[8]{0:T(128)S(1)}, s32[8]{0:T(128)}, u32[]{:S(2)}) copy-start(s32[8]{0:T(128)} %param.18) | copy-start | bytes 100
  5.3 13.5 %copy-start.1 = (s32[8,32]{1,0:T(8,128)S(1)}, s32[8,32]{1,0:T(8,128)}, u32[]{:S(2)}) copy-start(s32[8,32]{1,0:T(8,128)} %param.19) | copy-start | bytes 3076
  7.7 27.5 %all-to-all-start = ((f32[32,8,256]{2,1,0:T(8,128)}), f32[32,8,256]{2,1,0:T(8,128)}, u32[]{:S(2)}, u32[]{:S(2)}) async-start(f32[32,8,256]{2,1,0:T(8,128)} %copy.54), calls=%async_computation | async-start | bytes 524288 | tf_op jit(solution)/shard_map/all_to_all | solution.py:61
  21.3 2.2 %copy-start.14 = (bf16[8,8192]{1,0:T(8,128)(2,1)S(1)}, bf16[8,8192]{1,0:T(8,128)(2,1)}, u32[]{:S(2)}) copy-start(bf16[8,8192]{1,0:T(8,128)(2,1)} %param.16) | copy-start | bytes 393220
  38.1 49.5 %copy-start.9 = (s32[32,1]{0,1:T(1,128)S(1)}, s32[32,1]{0,1:T(1,128)}, u32[]{:S(2)}) copy-start(s32[32,1]{0,1:T(1,128)} %param.21) | copy-start | bytes 388
  38.1 30.2 %all-to-all-start.1 = ((f32[16,8,648]{2,1,0:T(8,128)}), f32[16,8,648]{2,1,0:T(8,128)}, u32[]{:S(2)}, u32[]{:S(2)}) async-start(f32[16,8,648]{2,1,0:T(8,128)} %maximum_bitcast_fusion.2), calls=%async_computation.1 | async-start | bytes 786432 | tf_op jit(solution)/shard_map/all_to_all | solution.py:99
  50.9 38.1 %copy-start.10 = (s32[32]{0:T(128)S(1)}, s32[32]{0:T(128)}, u32[]{:S(2)}) copy-start(s32[32]{0:T(128)} %param.20) | copy-start | bytes 388
  50.9 38.7 %copy-start.12 = (s32[8]{0:T(128)S(1)}, s32[8]{0:T(128)}, u32[]{:S(2)}) copy-start(s32[8]{0:T(128)} %param.18) | copy-start | bytes 100
  75.0 30.4 %all-to-all-start.2 = ((f32[16,8,648]{2,1,0:T(8,128)}), f32[16,8,648]{2,1,0:T(8,128)}, u32[]{:S(2)}, u32[]{:S(2)}) async-start(f32[16,8,648]{2,1,0:T(8,128)} %broadcast_in_dim.64), calls=%async_computation.2 | async-start | bytes 786432 | tf_op jit(solution)/shard_map/all_to_all | solution.py:125
  110.4 23.0 %copy-start.5 = (f32[8,16,4]{0,2,1:T(4,128)S(1)}, f32[8,16,4]{0,2,1:T(4,128)}, u32[]{:S(2)}) copy-start(f32[8,16,4]{0,2,1:T(4,128)} %copy.60) | copy-start | bytes 6148
  110.4 23.0 %copy-start.4 = (f32[8,8,128]{2,0,1:T(8,128)S(1)}, f32[8,8,128]{2,0,1:T(8,128)}, u32[]{:S(2)}) copy-start(f32[8,8,128]{2,0,1:T(8,128)} %get-tuple-element.17) | copy-start | bytes 98308
  111.2 22.2 %copy-start.6 = (f32[8,16,4]{0,2,1:T(4,128)S(1)}, f32[8,16,4]{0,2,1:T(4,128)}, u32[]{:S(2)}) copy-start(f32[8,16,4]{0,2,1:T(4,128)} %copy.59) | copy-start | bytes 6148
  116.0 17.4 %copy-start.7 = (f32[8,8,1,8]{0,3,1,2:T(8,128)S(1)}, f32[8,8,1,8]{0,3,1,2:T(8,128)}, u32[]{:S(2)}) copy-start(f32[8,8,1,8]{0,3,1,2:T(8,128)} %copy.70) | copy-start | bytes 6148
  119.1 23.2 %all-to-all-start.3 = ((bf16[32,2,1,2,8,128]{5,4,3,1,2,0:T(8,128)(2,1)}), bf16[32,2,1,2,8,128]{5,4,3,1,2,0:T(8,128)(2,1)}, u32[]{:S(2)}, u32[]{:S(2)}) async-start(bf16[32,2,1,2,8,128]{5,4,3,1,2,0:T(8,128)(2,1)} %broadcast_select_fusion), calls=%async_computation.3 | async-start | bytes 524288 | tf_op jit(solution)/shard_map/all_to_all | solution.py:180
  143.3 1.1 copy-start.2

commit v5 on v4

--- a/solution.py
+++ b/solution.py
@@ -7,6 +7,39 @@
 
 adapter_scale = 2.0
 masked_score = -1e30
+
+
+def split_three(value):
+    first = lax.reduce_precision(value, exponent_bits=8, mantissa_bits=7)
+    rest = value - first
+    second = lax.reduce_precision(rest, exponent_bits=8, mantissa_bits=7)
+    third = rest - second
+    return jnp.concatenate([first, second, third], axis=-1).astype(jnp.bfloat16)
+
+
+def join_three(parts, width):
+    wide = parts.astype(jnp.float32)
+    return wide[..., :width] + wide[..., width : 2 * width] + wide[..., 2 * width :]
+
+
+def finish_attention(all_mixed, all_top, all_total, query, new_keys, new_values):
+    rows, heads, group_size, head_dim = query.shape
+    query_heads = heads * group_size
+    new_score = (
+        jnp.einsum("ihgd,ihd->ihg", query, new_keys, preferred_element_type=jnp.float32)
+        / math.sqrt(head_dim)
+    ).reshape(rows, query_heads)
+    top = jnp.maximum(all_top, new_score)
+    old_scale = jnp.exp(all_top - top)
+    new_weight = jnp.exp(new_score - top)
+    total = all_total * old_scale + new_weight
+    new_value_rows = jnp.broadcast_to(
+        new_values.astype(jnp.float32)[:, :, None, :], (rows, heads, query_heads // heads, head_dim)
+    ).reshape(rows, query_heads, head_dim)
+    mixed = all_mixed * old_scale[..., None] + new_weight[..., None] * new_value_rows
+    attention = (mixed / total[..., None]).astype(jnp.bfloat16).reshape(rows, -1)
+
+    return attention
 
 
 def shards(
@@ -87,26 +120,34 @@
 
     parcel = jnp.concatenate(
         [
-            local_mixed.reshape(rows, groups, mixed_width),
-            local_top.reshape(rows, groups, heads_per_target),
-            local_total.reshape(rows, groups, heads_per_target),
+            local_mixed.reshape(rows, groups, mixed_width).astype(jnp.bfloat16),
+            split_three(local_top.reshape(rows, groups, heads_per_target)),
+            split_three(local_total.reshape(rows, groups, heads_per_target)),
             jnp.broadcast_to(
-                summed[:, None, column_span:], (rows, groups, summed.shape[1] - column_span)
+                summed[:, None, column_span:].astype(jnp.bfloat16),
+                (rows, groups, summed.shape[1] - column_span),
             ),
         ],
         axis=2,
     ).transpose(1, 0, 2)
     received = lax.all_to_all(parcel, "grp", 0, 0, tiled=False)
-    shard_mixed = received[:, :, :mixed_width].reshape(groups, rows, heads_per_target, head_dim)
-    shard_top = received[:, :, mixed_width : mixed_width + heads_per_target]
-    shard_total = received[:, :, mixed_width + heads_per_target : mixed_width + 2 * heads_per_target]
-    mid_spread = received[:, :, mixed_width + 2 * heads_per_target :]
+    stat_width = 3 * heads_per_target
+    shard_mixed = (
+        received[:, :, :mixed_width]
+        .astype(jnp.float32)
+        .reshape(groups, rows, heads_per_target, head_dim)
+    )
+    shard_top = join_three(received[:, :, mixed_width : mixed_width + stat_width], heads_per_target)
+    shard_total = join_three(
+        received[:, :, mixed_width + stat_width : mixed_width + 2 * stat_width], heads_per_target
+    )
+    mid_spread = received[:, :, mixed_width + 2 * stat_width :]
     top_own = jnp.max(shard_top, axis=0)
     shard_scale = jnp.exp(shard_top - top_own[None])
     total_own = jnp.sum(shard_total * shard_scale, axis=0)
     mixed_own = jnp.sum(shard_mixed * shard_scale[..., None], axis=0)
 
-    mid_home = mid_spread[owner, request_index].astype(jnp.bfloat16)
+    mid_home = mid_spread[owner, request_index]
     mid_used = jnp.where(is_value, mid_home[:, rank_half:], mid_home[:, :rank_half])
     adapter_update = jnp.einsum(
         "ir,irc->ic", mid_used, up_weight_rows, preferred_element_type=jnp.float32
@@ -115,39 +156,28 @@
 
     merged = jnp.concatenate(
         [
-            mixed_own.reshape(rows, mixed_width),
-            top_own,
-            total_own,
-            fresh_columns.astype(jnp.float32),
+            mixed_own.reshape(rows, mixed_width).astype(jnp.bfloat16),
+            split_three(top_own),
+            split_three(total_own),
+            fresh_columns,
         ],
         axis=1,
     )
     everything = lax.all_to_all(
         jnp.broadcast_to(merged[None], (groups,) + merged.shape), "grp", 0, 0, tiled=False
     ).transpose(1, 0, 2)
-    all_mixed = everything[:, :, :mixed_width].reshape(rows, query_heads, head_dim)
-    all_top = everything[:, :, mixed_width : mixed_width + heads_per_target].reshape(rows, query_heads)
-    all_total = everything[
-        :, :, mixed_width + heads_per_target : mixed_width + 2 * heads_per_target
-    ].reshape(rows, query_heads)
-    new_all = everything[:, :, mixed_width + 2 * heads_per_target :].astype(jnp.bfloat16)
-    new_all = new_all.reshape(rows, groups * column_span)
+    all_mixed = everything[:, :, :mixed_width].astype(jnp.float32).reshape(rows, query_heads, head_dim)
+    all_top = join_three(
+        everything[:, :, mixed_width : mixed_width + stat_width], heads_per_target
+    ).reshape(rows, query_heads)
+    all_total = join_three(
+        everything[:, :, mixed_width + stat_width : mixed_width + 2 * stat_width], heads_per_target
+    ).reshape(rows, query_heads)
+    new_all = everything[:, :, mixed_width + 2 * stat_width :].reshape(rows, groups * column_span)
     new_keys = new_all[:, :key_width].reshape(rows, heads, head_dim)
     new_values = new_all[:, key_width:].reshape(rows, heads, head_dim)
 
-    new_score = (
-        jnp.einsum("ihgd,ihd->ihg", query, new_keys, preferred_element_type=jnp.float32)
-        / math.sqrt(head_dim)
-    ).reshape(rows, query_heads)
-    top = jnp.maximum(all_top, new_score)
-    old_scale = jnp.exp(all_top - top)
-    new_weight = jnp.exp(new_score - top)
-    total = all_total * old_scale + new_weight
-    new_value_rows = jnp.broadcast_to(
-        new_values.astype(jnp.float32)[:, :, None, :], (rows, heads, query_heads // heads, head_dim)
-    ).reshape(rows, query_heads, head_dim)
-    mixed = all_mixed * old_scale[..., None] + new_weight[..., None] * new_value_rows
-    attention = (mixed / total[..., None]).astype(jnp.bfloat16).reshape(rows, -1)
+    attention_parts = (all_mixed, all_top, all_total, query, new_keys, new_values)
 
     targets = departing_target[:, 0]
     count_out = departing_slots.shape[0]
@@ -177,7 +207,9 @@
         written[source_slot],
         jnp.zeros((), key_value_pages.dtype),
     )
+    outbound, attention_parts = lax.optimization_barrier((outbound, attention_parts))
     arrived = lax.all_to_all(outbound, "req", split_axis=0, concat_axis=0, tiled=True)
+    attention = finish_attention(*attention_parts)
     migrated_pool = lax.dynamic_update_slice_in_dim(
         written,
         arrived.reshape((homes * capacity,) + key_value_pages.shape[1:]),

time: 146 us -> 139 us (0.952)
  waiting for transfers between devices: 40.2 us -> 26.1 us
  local copies, waits for them, and re-layouts: 31.5 us -> 40.6 us
  starting transfers between devices: 50.6 us -> 43.9 us
  other arithmetic: 13.9 us -> 19.1 us
    another operation x0 -> x6, local copies, waits for them, and re-layouts: none -> 8.6 us
    all_to_all x1, waiting for transfers between devices: 17.4 us -> 10.6 us  [shards(): received = lax.all_to_all(parcel, 'grp', 0, 0, tiled=False)]
    all_to_all x1, waiting for transfers between devices: 15.8 us -> 9.72 us  [shards(): lax.all_to_all(jnp.broadcast_to(merged[None], (groups,) + merged.shape),...]
    all_to_all x1, starting transfers between devices: 12.6 us -> 8.45 us  [shards(): lax.all_to_all(jnp.broadcast_to(merged[None], (groups,) + merged.shape),...]
    reshape x3 -> x2, local copies, waits for them, and re-layouts: 4.47 us -> 1.53 us  [the longest x1 0.92 us: shards(): everything[:, :, mixed_width + 2 * stat_width:]]
    slice x7 -> x4, local copies, waits for them, and re-layouts: 7.3 us -> 4.6 us  [the longest x1 2.11 us: shards(): keys = gathered[:, :, 0]]
    convert_element_type x0 -> x2, local copies, waits for them, and re-layouts: none -> 2.63 us  [shards(): local_mixed.reshape(rows, groups, mixed_width).astype(jnp.bfloat16)]
    all_to_all x1, starting transfers between devices: 14.3 us -> 11.9 us  [shards(): lax.all_to_all(outbound, 'req', split_axis=0, concat_axis=0, tiled=True)]
  transfers between devices with their start and end apart: 4 -> 4, of which waited for: 3 -> 3; matrix products, arithmetic and copies ran while one was open for 14% -> 25% of each run, Pallas kernels for 0% -> 0%
where the time goes in v5:
time: 139 us; the launch traced here: 137 us
  starting transfers between devices  43.9 us (32%)
  local copies, waits for them, and re-layouts  40.6 us (29%)
  waiting for transfers between devices  26.1 us (19%)
  other arithmetic  19.1 us (14%)
  matrix products  6.1 us (4%)
    all_to_all x1, starting transfers between devices, shards(): received = lax.all_to_all(parcel, 'grp', 0, 0, tiled=False)  12.6 us
    all_to_all x1, starting transfers between devices, shards(): lax.all_to_all(outbound, 'req', split_axis=0, concat_axis=0, tiled=True)  11.9 us
    all_to_all x1, starting transfers between devices, shards(): lax.all_to_all(partial, 'req', 0, 0, tiled=False)  11 us
    all_to_all x1, waiting for transfers between devices, shards(): received = lax.all_to_all(parcel, 'grp', 0, 0, tiled=False)  10.6 us
    all_to_all x1, waiting for transfers between devices, shards(): lax.all_to_all(jnp.broadcast_to(merged[None], (groups,) + merged.shape),...  9.72 us
    another operation x6, local copies, waits for them, and re-layouts  8.6 us
    all_to_all x1, starting transfers between devices, shards(): lax.all_to_all(jnp.broadcast_to(merged[None], (groups,) + merged.shape),...  8.45 us
    all_to_all x1, waiting for transfers between devices, shards(): lax.all_to_all(outbound, 'req', split_axis=0, concat_axis=0, tiled=True)  5.77 us
  transfers between devices with their start and end apart: 4, of which 3 were waited for; matrix products, arithmetic and copies ran while one was open for 25% of the time, Pallas kernels for 0%

profile of v5, /device:TPU:1, one launch (start us, length us, event | category | flops | bytes accessed | tf_op | source)
XLA Modules:
  0.0 136.9 jit_solution(14958223954863002002)
XLA Ops:
  0.7 1.5 %copy.143 = bf16[320,1,2,8,128]{4,3,2,1,0:T(8,128)(2,1)S(1)} copy(bf16[320,1,2,8,128]{4,3,2,1,0:T(8,128)(2,1)} %param.17) | data formatting | bytes 2621440
  5.2 1.1 copy.107
  7.7 11.0 %all-to-all-start = ((f32[32,8,256]{2,1,0:T(8,128)}), f32[32,8,256]{2,1,0:T(8,128)}, u32[]{:S(2)}, u32[]{:S(2)}) async-start(f32[32,8,256]{2,1,0:T(8,128)} %copy.83), calls=%async_computation | async-start | bytes 524288 | tf_op jit(solution)/shard_map/all_to_all | solution.py:94
  18.8 1.2 gather_fusion
  20.1 1.8 %gather_fusion.1 = bf16[256,2,8,128]{3,2,1,0:T(8,128)(2,1)} fusion(bf16[320,2,8,128]{3,2,1,0:T(8,128)(2,1)S(1)} %bitcast.127, s32[1024]{0:T(1024)S(1)} %pad_clamp_fusion.2), kind=kCustom, calls=%fused_computation.1 | custom fusion | bytes 2098176 | tf_op jit(solution)/shard_map/gather | solution.py:104
  21.9 2.1 %fusion.51 = (bf16[8,32,1,8,128]{4,3,2,1,0:T(8,128)(2,1)S(1)}, bf16[8,32,1,8,128]{4,3,2,1,0:T(8,128)(2,1)}) fusion(bf16[8,32,2,8,128]{4,3,2,1,0:T(8,128)(2,1)} %bitcast.130), kind=kLoop, calls=%fused_computation.145 | loop fusion | bytes 2097152 | tf_op jit(solution)/shard_map/slice | solution.py:105
  25.2 1.2 fusion.11
  26.4 2.1 %convolution_convert_fusion = bf16[8,8,8,128]{3,2,1,0:T(8,128)(2,1)} fusion(bf16[8,32,1,8,128]{4,3,2,1,0:T(8,128)(2,1)} %get-tuple-element.26, f32[8,8,8,32]{3,2,1,0:T(8,128)} %get-tuple-element.52, f32[8,8,8]{2,1,0:T(8,128)S(1)} %get-tuple-element.51, pred[8,32]{1,0:T(8,128)(4,1)S(1)} %broadcast_compare_fusion), kind=kOutput, calls=%fused_computation.11 | convolution fusion | flops 4292608 | bytes 723200 | tf_op jit(solution)/shard_map/ihgn,inhd->ihgd/dot_general | solution.py:117
  29.3 1.6 %convert_element_type.46 = bf16[8,16,512]{2,1,0:T(8,128)(2,1)} reshape(bf16[8,8,8,128]{3,2,1,0:T(8,128)(2,1)} %convolution_convert_fusion) | data formatting | bytes 262144 | tf_op jit(solution)/shard_map/convert_element_type | solution.py:123
  32.0 1.3 fusion.27
  33.9 1.4 %copy.87 = bf16[8,16,4]{2,0,1:T(8,128)(2,1)} copy(bf16[8,16,4]{1,0,2:T(8,128)(2,1)} %get-tuple-element.38) | data formatting | bytes 2048 | tf_op jit(solution)/shard_map/convert.13
  35.4 1.4 %copy.90 = bf16[8,16,4]{2,0,1:T(8,128)(2,1)} copy(bf16[8,16,4]{1,0,2:T(8,128)(2,1)} %get-tuple-element.35) | data formatting | bytes 2048 | tf_op jit(solution)/shard_map/convert.10
  36.8 1.4 %copy.86 = bf16[8,16,4]{2,0,1:T(8,128)(2,1)} copy(bf16[8,16,4]{1,0,2:T(8,128)(2,1)} %get-tuple-element.39) | data formatting | bytes 2048 | tf_op jit(solution)/shard_map/convert.12
  38.2 1.4 %copy.85 = bf16[8,16,4]{2,0,1:T(8,128)(2,1)} copy(bf16[8,16,4]{1,0,2:T(8,128)(2,1)} %get-tuple-element.40) | data formatting | bytes 2048 | tf_op jit(solution)/shard_map/convert.11
  39.7 1.4 %copy.89 = bf16[8,16,4]{2,0,1:T(8,128)(2,1)} copy(bf16[8,16,4]{1,0,2:T(8,128)(2,1)} %get-tuple-element.36) | data formatting | bytes 2048 | tf_op jit(solution)/shard_map/convert.9
  41.1 1.4 %copy.88 = bf16[8,16,4]{2,0,1:T(8,128)(2,1)} copy(bf16[8,16,4]{1,0,2:T(8,128)(2,1)} %get-tuple-element.37) | data formatting | bytes 2048 | tf_op jit(solution)/shard_map/convert.8
  42.5 1.2 shift-left_bitcast_fusion
  43.8 1.2 gather_fusion.2
  46.6 1.7 %concatenate.36 = bf16[8,16,664]{2,0,1:T(8,128)(2,1)} concatenate(bf16[8,16,512]{2,0,1:T(8,128)(2,1)S(1)} %copy.84, bf16[8,16,4]{2,0,1:T(8,128)(2,1)} %copy.85, bf16[8,16,4]{2,0,1:T(8,128)(2,1)} %copy.86, bf16[8,16,4]{2,0,1:T(8,128)(2,1)} %copy.87, bf16[8,16,4]{2,0,1:T(8,128)(2,1)} %copy.88, bf16[8,16,4]{2,0,1:T(8,128)(2,1)} %copy.89, bf16[8,16,4]{2,0,1:T(8,128)(2,1)} %copy.90, ...), dimensions={2} | concatenate | bytes 339968 | tf_op jit(solution)/shard_map/concatenate | solution.py:121
  48.3 12.6 %all-to-all-start.1 = ((bf16[16,8,664]{2,1,0:T(8,128)(2,1)}), bf16[16,8,664]{2,1,0:T(8,128)(2,1)}, u32[]{:S(2)}, u32[]{:S(2)}) async-start(bf16[16,8,664]{2,1,0:T(8,128)(2,1)} %bitcast.133), calls=%async_computation.1 | async-start | bytes 393216 | tf_op jit(solution)/shard_map/all_to_all | solution.py:133
  63.3 10.6 %all-to-all-done.1 = bf16[16,8,664]{2,1,0:T(8,128)(2,1)} async-done(((bf16[16,8,664]{2,1,0:T(8,128)(2,1)}), bf16[16,8,664]{2,1,0:T(8,128)(2,1)}, u32[]{:S(2)}, u32[]{:S(2)}) %all-to-all-start.1) | async-done | bytes 170016 | tf_op jit(solution)/shard_map/all_to_all | solution.py:133
  79.7 8.4 %all-to-all-start.2 = ((bf16[16,8,664]{2,1,0:T(8,128)(2,1)}), bf16[16,8,664]{2,1,0:T(8,128)(2,1)}, u32[]{:S(2)}, u32[]{:S(2)}) async-start(bf16[16,8,664]{2,1,0:T(8,128)(2,1)} %broadcast_in_dim.112), calls=%async_computation.2 | async-start | bytes 393216 | tf_op jit(solution)/shard_map/all_to_all | solution.py:166
  89.2 1.2 gather_fusion.4
  91.0 9.7 %all-to-all-done.2 = bf16[16,8,664]{2,1,0:T(8,128)(2,1)} async-done(((bf16[16,8,664]{2,1,0:T(8,128)(2,1)}), bf16[16,8,664]{2,1,0:T(8,128)(2,1)}, u32[]{:S(2)}, u32[]{:S(2)}) %all-to-all-start.2) | async-done | bytes 170016 | tf_op jit(solution)/shard_map/all_to_all | solution.py:166
  101.7 1.6 %slice.154 = bf16[8,16,512]{2,0,1:T(8,128)(2,1)} slice(bf16[8,16,664]{2,0,1:T(8,128)(2,1)} %bitcast.25), slice={[0:8], [0:16], [0:512]} | slice | bytes 262144 | tf_op jit(solution)/shard_map/slice | solution.py:169
  107.7 1.6 %convert.53 = f32[8,64,128]{2,0,1:T(8,128)} convert(bf16[8,64,128]{2,0,1:T(8,128)(2,1)} %bitcast.134) | non-fusion elementwise | flops 65536 | bytes 393216 | tf_op jit(solution)/shard_map/reshape | solution.py:169
  111.0 1.3 gather_fusion.5
  112.3 1.8 %broadcast_select_fusion = bf16[32,2,1,2,8,128]{5,4,3,1,2,0:T(8,128)(2,1)} fusion(bf16[32,2,1,2,8,128]{5,4,3,1,2,0:T(8,128)(2,1)} %bitcast.132, pred[32,2]{1,0:T(8,128)(4,1)S(1)} %copy-done.7), kind=kLoop, calls=%fused_computation.29 | loop fusion | flops 131072 | bytes 524352 | tf_op jit(solution)/shard_map/jit(_where)/select_n | solution.py:205
  114.1 11.9 %all-to-all-start.3 = ((bf16[32,2,1,2,8,128]{5,4,3,1,2,0:T(8,128)(2,1)}), bf16[32,2,1,2,8,128]{5,4,3,1,2,0:T(8,128)(2,1)}, u32[]{:S(2)}, u32[]{:S(2)}) async-start(bf16[32,2,1,2,8,128]{5,4,3,1,2,0:T(8,128)(2,1)} %broadcast_select_fusion), calls=%async_computation.3 | async-start | bytes 524288 | tf_op jit(solution)/shard_map/all_to_all | solution.py:211
  126.0 1.1 fusion.16
  127.2 1.9 %fusion.9 = bf16[8,64,128]{2,0,1:T(8,128)(2,1)} fusion(f32[8,64,128]{2,0,1:T(8,128)} %convert.53, f32[8,64]{0,1:T(8,128)S(1)} %get-tuple-element.20, f32[8,8,128]{2,0,1:T(8,128)S(1)} %convert_element_type.54, f32[8,64]{0,1:T(8,128)S(1)} %get-tuple-element.22, f32[8,64]{0,1:T(8,128)S(1)} %get-tuple-element.21), kind=kLoop, calls=%fused_computation.25 | loop fusion | flops 327680 | bytes 432128 | tf_op jit(solution)/shard_map/convert_element_type | solution.py:40
  129.1 5.8 %all-to-all-done.3 = bf16[32,2,1,2,8,128]{5,4,3,1,2,0:T(8,128)(2,1)} async-done(((bf16[32,2,1,2,8,128]{5,4,3,1,2,0:T(8,128)(2,1)}), bf16[32,2,1,2,8,128]{5,4,3,1,2,0:T(8,128)(2,1)}, u32[]{:S(2)}, u32[]{:S(2)}) %all-to-all-start.3) | async-done | bytes 262176 | tf_op jit(solution)/shard_map/all_to_all | solution.py:211
  (103 shorter events, 28.7 us)
Async XLA Ops:
  0.6 43.1 %copy-start = (bf16[128,64,128]{2,1,0:T(8,128)(2,1)S(1)}, bf16[128,64,128]{2,1,0:T(8,128)(2,1)}, u32[]{:S(2)}) copy-start(bf16[128,64,128]{2,1,0:T(8,128)(2,1)} %param.14) | copy-start | bytes 6291460
  0.6 1.7 %copy-start.14 = (bf16[256,256]{1,0:T(8,128)(2,1)S(1)}, bf16[256,256]{1,0:T(8,128)(2,1)}, u32[]{:S(2)}) copy-start(bf16[256,256]{1,0:T(8,128)(2,1)} %param.11) | copy-start | bytes 393220
  0.7 1.7 %copy-start.16 = (bf16[256,128]{1,0:T(8,128)(2,1)S(1)}, bf16[256,128]{1,0:T(8,128)(2,1)}, u32[]{:S(2)}) copy-start(bf16[256,128]{1,0:T(8,128)(2,1)} %param.12) | copy-start | bytes 196612
  0.7 1.6 %copy-start.3 = (bf16[256,8,128]{2,1,0:T(8,128)(2,1)S(1)}, bf16[256,8,128]{2,1,0:T(8,128)(2,1)}, u32[]{:S(2)}) copy-start(bf16[256,8,128]{2,1,0:T(8,128)(2,1)} %param.13) | copy-start | bytes 1572868
  2.7 0.9 copy-start.9
  6.3 12.4 %copy-start.13 = (s32[8]{0:T(128)S(1)}, s32[8]{0:T(128)}, u32[]{:S(2)}) copy-start(s32[8]{0:T(128)} %param.18) | copy-start | bytes 100
  6.3 12.4 %copy-start.1 = (s32[8,32]{1,0:T(8,128)S(1)}, s32[8,32]{1,0:T(8,128)}, u32[]{:S(2)}) copy-start(s32[8,32]{1,0:T(8,128)} %param.19) | copy-start | bytes 3076
  7.7 37.3 %all-to-all-start = ((f32[32,8,256]{2,1,0:T(8,128)}), f32[32,8,256]{2,1,0:T(8,128)}, u32[]{:S(2)}, u32[]{:S(2)}) async-start(f32[32,8,256]{2,1,0:T(8,128)} %copy.83), calls=%async_computation | async-start | bytes 524288 | tf_op jit(solution)/shard_map/all_to_all | solution.py:94
  21.9 2.1 %copy-start.15 = (bf16[8,8192]{1,0:T(8,128)(2,1)S(1)}, bf16[8,8192]{1,0:T(8,128)(2,1)}, u32[]{:S(2)}) copy-start(bf16[8,8192]{1,0:T(8,128)(2,1)} %param.16) | copy-start | bytes 393220
  48.3 25.6 %all-to-all-start.1 = ((bf16[16,8,664]{2,1,0:T(8,128)(2,1)}), bf16[16,8,664]{2,1,0:T(8,128)(2,1)}, u32[]{:S(2)}, u32[]{:S(2)}) async-start(bf16[16,8,664]{2,1,0:T(8,128)(2,1)} %bitcast.133), calls=%async_computation.1 | async-start | bytes 393216 | tf_op jit(solution)/shard_map/all_to_all | solution.py:133
  61.8 13.0 %copy-start.11 = (pred[2,32]{1,0:T(4,128)(4,1)}, pred[2,32]{1,0:T(4,128)(4,1)S(1)}, u32[]{:S(2)}) copy-start(pred[2,32]{1,0:T(4,128)(4,1)S(1)} %iota_compare_fusion.3) | copy-start | bytes 196
  76.5 11.7 %copy-start.12 = (pred[2,32]{1,0:T(4,128)(4,1)S(1)}, pred[2,32]{1,0:T(4,128)(4,1)}, u32[]{:S(2)}) copy-start(pred[2,32]{1,0:T(4,128)(4,1)} %copy-done.11) | copy-start | bytes 196
  79.0 31.2 %copy-start.10 = (s32[8]{0:T(128)S(1)}, s32[8]{0:T(128)}, u32[]{:S(2)}) copy-start(s32[8]{0:T(128)} %get-tuple-element.50) | copy-start | bytes 100
  79.7 21.0 %all-to-all-start.2 = ((bf16[16,8,664]{2,1,0:T(8,128)(2,1)}), bf16[16,8,664]{2,1,0:T(8,128)(2,1)}, u32[]{:S(2)}, u32[]{:S(2)}) async-start(bf16[16,8,664]{2,1,0:T(8,128)(2,1)} %broadcast_in_dim.112), calls=%async_computation.2 | async-start | bytes 393216 | tf_op jit(solution)/shard_map/all_to_all | solution.py:166
  89.2 23.1 %copy-start.7 = (pred[32,2]{1,0:T(8,128)(4,1)S(1)}, pred[32,2]{1,0:T(8,128)(4,1)}, u32[]{:S(2)}) copy-start(pred[32,2]{1,0:T(8,128)(4,1)} %copy.72) | copy-start | bytes 196
  107.7 19.5 %copy-start.6 = (bf16[8,8,128]{2,0,1:T(8,128)(2,1)S(1)}, bf16[8,8,128]{2,0,1:T(8,128)(2,1)}, u32[]{:S(2)}) copy-start(bf16[8,8,128]{2,0,1:T(8,128)(2,1)} %get-tuple-element.17) | copy-start | bytes 49156
  107.7 19.5 %copy-start.4 = (f32[8,16,4]{0,2,1:T(4,128)S(1)}, f32[8,16,4]{0,2,1:T(4,128)}, u32[]{:S(2)}) copy-start(f32[8,16,4]{0,2,1:T(4,128)} %copy.94) | copy-start | bytes 6148
  107.7 19.5 %copy-start.5 = (f32[8,16,4]{0,2,1:T(4,128)S(1)}, f32[8,16,4]{0,2,1:T(4,128)}, u32[]{:S(2)}) copy-start(f32[8,16,4]{0,2,1:T(4,128)} %copy.93) | copy-start | bytes 6148
  111.0 15.0 %copy-start.8 = (bf16[8,8,128]{2,0,1:T(8,128)(2,1)S(1)}, bf16[8,8,128]{2,0,1:T(8,128)(2,1)}, u32[]{:S(2)}) copy-start(bf16[8,8,128]{2,0,1:T(8,128)(2,1)} %get-tuple-element.16) | copy-start | bytes 49156
  114.1 20.8 %all-to-all-start.3 = ((bf16[32,2,1,2,8,128]{5,4,3,1,2,0:T(8,128)(2,1)}), bf16[32,2,1,2,8,128]{5,4,3,1,2,0:T(8,128)(2,1)}, u32[]{:S(2)}, u32[]{:S(2)}) async-start(bf16[32,2,1,2,8,128]{5,4,3,1,2,0:T(8,128)(2,1)} %broadcast_select_fusion), calls=%async_computation.3 | async-start | bytes 524288 | tf_op jit(solution)/shard_map/all_to_all | solution.py:211
  135.9 1.1 copy-start.2

commit v6 on v5

--- a/solution.py
+++ b/solution.py
@@ -24,23 +24,19 @@
 
 def finish_attention(all_mixed, all_top, all_total, query, new_keys, new_values):
     rows, heads, group_size, head_dim = query.shape
-    query_heads = heads * group_size
-    new_score = (
-        jnp.einsum("ihgd,ihd->ihg", query, new_keys, preferred_element_type=jnp.float32)
-        / math.sqrt(head_dim)
-    ).reshape(rows, query_heads)
+    new_score = jnp.einsum(
+        "ihgd,hid->hgi", query, new_keys, preferred_element_type=jnp.float32
+    ) / math.sqrt(head_dim)
     top = jnp.maximum(all_top, new_score)
     old_scale = jnp.exp(all_top - top)
     new_weight = jnp.exp(new_score - top)
     total = all_total * old_scale + new_weight
-    new_value_rows = jnp.broadcast_to(
-        new_values.astype(jnp.float32)[:, :, None, :], (rows, heads, query_heads // heads, head_dim)
-    ).reshape(rows, query_heads, head_dim)
-    mixed = all_mixed * old_scale[..., None] + new_weight[..., None] * new_value_rows
-    attention = (mixed / total[..., None]).astype(jnp.bfloat16).reshape(rows, -1)
-
-    return attention
-
+    mixed = (
+        all_mixed * old_scale[..., None]
+        + new_weight[..., None] * new_values.astype(jnp.float32)[:, None, :, :]
+    )
+    attention = (mixed / total[..., None]).astype(jnp.bfloat16)
+    return attention.transpose(2, 0, 1, 3).reshape(rows, -1)
 
 def shards(
     normed_token_input,
@@ -99,49 +95,48 @@
     owner = resident_adapters // local_adapters
     request_index = jnp.arange(rows, dtype=jnp.int32)
     is_value = group_index * column_span >= key_width
-    mixed_width = heads_per_target * head_dim
 
     gathered = key_value_pages[page_slot_table][:, :, 0]
     keys = gathered[:, :, 0]
     values = gathered[:, :, 1]
     query = queries.reshape(rows, heads, -1, head_dim)
+    group_size = query.shape[2]
     scores = jnp.einsum(
-        "ihgd,inhd->ihgn", query, keys, preferred_element_type=jnp.float32
+        "ihgd,inhd->hgin", query, keys, preferred_element_type=jnp.float32
     ) / math.sqrt(head_dim)
     positions = jnp.arange(pages, dtype=jnp.int32) * page_size + group_index * slot_tokens
-    valid = (positions[None, :] < lengths[:, None])[:, None, None, :]
+    valid = (positions[None, :] < lengths[:, None])[None, None]
     scores = jnp.where(valid, scores, masked_score)
     local_top = jnp.max(scores, axis=3)
     weights = jnp.where(valid, jnp.exp(scores - local_top[..., None]), 0.0)
     local_total = jnp.sum(weights, axis=3)
     local_mixed = jnp.einsum(
-        "ihgn,inhd->ihgd", weights, values, preferred_element_type=jnp.float32
-    )
-
+        "hgin,inhd->hgid", weights, values, preferred_element_type=jnp.float32
+    )
+
+    block = heads_per_target * rows * head_dim
+    stat_count = heads_per_target * rows
+    stats = jnp.concatenate(
+        [local_top.reshape(groups, stat_count), local_total.reshape(groups, stat_count)], axis=1
+    )
+    mid_flat = summed[:, column_span:].astype(jnp.bfloat16).reshape(1, -1)
     parcel = jnp.concatenate(
         [
-            local_mixed.reshape(rows, groups, mixed_width).astype(jnp.bfloat16),
-            split_three(local_top.reshape(rows, groups, heads_per_target)),
-            split_three(local_total.reshape(rows, groups, heads_per_target)),
-            jnp.broadcast_to(
-                summed[:, None, column_span:].astype(jnp.bfloat16),
-                (rows, groups, summed.shape[1] - column_span),
-            ),
+            local_mixed.reshape(groups, block).astype(jnp.bfloat16),
+            split_three(stats),
+            jnp.broadcast_to(mid_flat, (groups, mid_flat.shape[1])),
         ],
-        axis=2,
-    ).transpose(1, 0, 2)
+        axis=1,
+    )
     received = lax.all_to_all(parcel, "grp", 0, 0, tiled=False)
-    stat_width = 3 * heads_per_target
-    shard_mixed = (
-        received[:, :, :mixed_width]
-        .astype(jnp.float32)
-        .reshape(groups, rows, heads_per_target, head_dim)
-    )
-    shard_top = join_three(received[:, :, mixed_width : mixed_width + stat_width], heads_per_target)
-    shard_total = join_three(
-        received[:, :, mixed_width + stat_width : mixed_width + 2 * stat_width], heads_per_target
-    )
-    mid_spread = received[:, :, mixed_width + 2 * stat_width :]
+    stat_end = block + 6 * stat_count
+    shard_mixed = received[:, :block].astype(jnp.float32).reshape(
+        groups, heads_per_target, rows, head_dim
+    )
+    shard_stats = join_three(received[:, block:stat_end], 2 * stat_count)
+    shard_top = shard_stats[:, :stat_count].reshape(groups, heads_per_target, rows)
+    shard_total = shard_stats[:, stat_count:].reshape(groups, heads_per_target, rows)
+    mid_spread = received[:, stat_end:].reshape(groups, rows, -1)
     top_own = jnp.max(shard_top, axis=0)
     shard_scale = jnp.exp(shard_top - top_own[None])
     total_own = jnp.sum(shard_total * shard_scale, axis=0)
@@ -156,27 +151,26 @@
 
     merged = jnp.concatenate(
         [
-            mixed_own.reshape(rows, mixed_width).astype(jnp.bfloat16),
-            split_three(top_own),
-            split_three(total_own),
-            fresh_columns,
+            mixed_own.reshape(1, block).astype(jnp.bfloat16),
+            split_three(
+                jnp.concatenate(
+                    [top_own.reshape(1, stat_count), total_own.reshape(1, stat_count)], axis=1
+                )
+            ),
+            fresh_columns.reshape(1, -1),
         ],
         axis=1,
     )
     everything = lax.all_to_all(
-        jnp.broadcast_to(merged[None], (groups,) + merged.shape), "grp", 0, 0, tiled=False
-    ).transpose(1, 0, 2)
-    all_mixed = everything[:, :, :mixed_width].astype(jnp.float32).reshape(rows, query_heads, head_dim)
-    all_top = join_three(
-        everything[:, :, mixed_width : mixed_width + stat_width], heads_per_target
-    ).reshape(rows, query_heads)
-    all_total = join_three(
-        everything[:, :, mixed_width + stat_width : mixed_width + 2 * stat_width], heads_per_target
-    ).reshape(rows, query_heads)
-    new_all = everything[:, :, mixed_width + 2 * stat_width :].reshape(rows, groups * column_span)
-    new_keys = new_all[:, :key_width].reshape(rows, heads, head_dim)
-    new_values = new_all[:, key_width:].reshape(rows, heads, head_dim)
-
+        jnp.broadcast_to(merged, (groups, merged.shape[1])), "grp", 0, 0, tiled=False
+    )
+    all_mixed = everything[:, :block].astype(jnp.float32).reshape(heads, group_size, rows, head_dim)
+    all_stats = join_three(everything[:, block:stat_end], 2 * stat_count)
+    all_top = all_stats[:, :stat_count].reshape(heads, group_size, rows)
+    all_total = all_stats[:, stat_count:].reshape(heads, group_size, rows)
+    new_all = everything[:, stat_end:].reshape(groups, rows, column_span)
+    new_keys = new_all[: groups // 2]
+    new_values = new_all[groups // 2 :]
     attention_parts = (all_mixed, all_top, all_total, query, new_keys, new_values)
 
     targets = departing_target[:, 0]
@@ -197,7 +191,7 @@
     mine = offset // slot_tokens == group_index
     token_local = offset % slot_tokens
     current = key_value_pages[page_slot, token_local]
-    fresh = jnp.stack([new_keys, new_values], axis=1)
+    fresh = jnp.stack([new_keys, new_values], axis=0).transpose(2, 0, 1, 3)
     written = key_value_pages.at[page_slot, token_local].set(
         jnp.where(mine[:, None, None, None], fresh, current)
     )

time: 139 us -> 147 us (1.058)
  other arithmetic: 19.1 us -> 25.1 us
  local copies, waits for them, and re-layouts: 40.6 us -> 45.3 us
    another operation x6 -> x0, local copies, waits for them, and re-layouts: 8.6 us -> none
    unnamed x39 -> x35, local copies, waits for them, and re-layouts: 5.14 us -> 13 us
    broadcast_in_dim x0 -> x1, other arithmetic: none -> 3.18 us  [shards(): jnp.broadcast_to(merged, (groups, merged.shape[1]))]
    all_to_all x0 -> x2, local copies, waits for them, and re-layouts: none -> 2.84 us  [shards(): received = lax.all_to_all(parcel, 'grp', 0, 0, tiled=False)]
    gather x1 -> x2, local copies, waits for them, and re-layouts: 1.76 us -> 4.25 us  [shards(): gathered = key_value_pages[page_slot_table][:, :, 0]]
    all_to_all x0 -> x1, other arithmetic: none -> 2.2 us  [shards(): received = lax.all_to_all(parcel, 'grp', 0, 0, tiled=False)]
    slice x4 -> x3, local copies, waits for them, and re-layouts: 4.6 us -> 2.45 us  [the longest x1 1.68 us: shards(): mid_spread = received[:, stat_end:].reshape(groups, rows, -1)]
    reshape x4 -> x6, local copies, waits for them, and re-layouts: 2.29 us -> 4.26 us  [the longest x1 1.7 us: shards(): everything[:, :block].astype(jnp.float32)]
  transfers between devices with their start and end apart: 4 -> 4, of which waited for: 3 -> 3; matrix products, arithmetic and copies ran while one was open for 25% -> 18% of each run, Pallas kernels for 0% -> 0%
where the time goes in v6:
time: 147 us; the launch traced here: 145 us
  local copies, waits for them, and re-layouts  45.3 us (31%)
  starting transfers between devices  43.2 us (29%)
  other arithmetic  25.1 us (17%)
  waiting for transfers between devices  25 us (17%)
  matrix products  5.57 us (4%)
    unnamed x35, local copies, waits for them, and re-layouts  13 us
    all_to_all x1, starting transfers between devices, shards(): received = lax.all_to_all(parcel, 'grp', 0, 0, tiled=False)  12.6 us
    all_to_all x1, starting transfers between devices, shards(): lax.all_to_all(outbound, 'req', split_axis=0, concat_axis=0, tiled=True)  11.5 us
    all_to_all x1, starting transfers between devices, shards(): lax.all_to_all(partial, 'req', 0, 0, tiled=False)  11 us
    all_to_all x1, waiting for transfers between devices, shards(): lax.all_to_all(jnp.broadcast_to(merged, (groups, merged.shape[1])), 'grp'...  9.99 us
    all_to_all x1, waiting for transfers between devices, shards(): received = lax.all_to_all(parcel, 'grp', 0, 0, tiled=False)  9.91 us
    all_to_all x1, starting transfers between devices, shards(): lax.all_to_all(jnp.broadcast_to(merged, (groups, merged.shape[1])), 'grp'...  8.11 us
    all_to_all x1, waiting for transfers between devices, shards(): lax.all_to_all(outbound, 'req', split_axis=0, concat_axis=0, tiled=True)  5.08 us
  transfers between devices with their start and end apart: 4, of which 3 were waited for; matrix products, arithmetic and copies ran while one was open for 18% of the time, Pallas kernels for 0%

profile of v6, /device:TPU:1, one launch (start us, length us, event | category | flops | bytes accessed | tf_op | source)
XLA Modules:
  0.0 145.1 jit_solution(3487945510128037896)
XLA Ops:
  0.7 1.5 %copy.111 = bf16[320,1,2,8,128]{4,3,2,1,0:T(8,128)(2,1)S(1)} copy(bf16[320,1,2,8,128]{4,3,2,1,0:T(8,128)(2,1)} %param.17) | data formatting | bytes 2621440
  7.7 11.0 %all-to-all-start = ((f32[32,8,256]{2,1,0:T(8,128)}), f32[32,8,256]{2,1,0:T(8,128)}, u32[]{:S(2)}, u32[]{:S(2)}) async-start(f32[32,8,256]{2,1,0:T(8,128)} %copy.61), calls=%async_computation | async-start | bytes 524288 | tf_op jit(solution)/shard_map/all_to_all | solution.py:90
  19.6 1.8 %gather_fusion.1 = bf16[256,2,8,128]{3,2,1,0:T(8,128)(2,1)} fusion(bf16[320,2,8,128]{3,2,1,0:T(8,128)(2,1)S(1)} %bitcast.137, s32[1024]{0:T(1024)S(1)} %pad_clamp_fusion.2), kind=kCustom, calls=%fused_computation.1 | custom fusion | bytes 2098176 | tf_op jit(solution)/shard_map/gather | solution.py:99
  21.3 2.5 %copy.55 = bf16[256,2,8,128]{3,0,2,1:T(8,128)(2,1)} copy(bf16[256,2,8,128]{3,2,1,0:T(8,128)(2,1)} %gather_fusion.1) | data formatting | bytes 2097152 | tf_op jit(solution)/shard_map/gather | solution.py:99
  24.5 1.5 %fusion.53 = (f32[8,8,8]{1,2,0:T(8,128)S(1)}, f32[8,8,8,32]{3,1,2,0:T(8,128)S(1)}) fusion(bf16[8,8,8,128]{3,0,2,1:T(8,128)(2,1)} %bitcast.163, bf16[8,32,2,8,128]{4,1,0,3,2:T(8,128)(2,1)} %bitcast.144, pred[8,32]{1,0:T(8,128)(4,1)S(1)} %broadcast_compare_fusion), kind=kOutput, calls=%fused_computation.137 | convolution fusion | flops 4242944 | bytes 723200 | tf_op jit(solution)/shard_map/ihgd,inhd->hgin/dot_general | solution.py:104
  26.0 2.0 %fusion.3 = bf16[8,8,8,128]{3,1,2,0:T(8,128)(2,1)} fusion(bf16[8,32,2,8,128]{4,1,0,3,2:T(8,128)(2,1)} %bitcast.145, f32[8,8,8,32]{3,1,2,0:T(8,128)S(1)} %get-tuple-element.41, f32[8,8,8]{1,2,0:T(8,128)S(1)} %get-tuple-element.40, pred[8,32]{1,0:T(8,128)(4,1)S(1)} %broadcast_compare_fusion), kind=kOutput, calls=%fused_computation.14 | convolution fusion | flops 4292608 | bytes 723200 | tf_op jit(solution)/shard_map/hgin,inhd->hgid/dot_general | solution.py:113
  29.2 1.6 %copy.57 = bf16[8,8,8,128]{3,2,1,0:T(8,128)(2,1)} copy(bf16[8,8,8,128]{3,1,2,0:T(8,128)(2,1)} %fusion.3) | data formatting | bytes 262144 | tf_op jit(solution)/shard_map/convert_element_type | solution.py:125
  31.7 1.3 pad_clamp_fusion.1
  33.0 1.3 gather_fusion.2
  34.3 1.4 fusion.26
  37.3 1.5 %concatenate.85 = bf16[16,5312]{1,0:T(8,128)(2,1)} concatenate(bf16[16,4096]{1,0:T(8,128)(2,1)S(1)} %convert_element_type.60, bf16[16,64]{1,0:T(8,128)(2,1)} %get-tuple-element.31, bf16[16,64]{1,0:T(8,128)(2,1)} %get-tuple-element.30, bf16[16,64]{1,0:T(8,128)(2,1)} %get-tuple-element.29, bf16[16,1024]{1,0:T(8,128)(2,1)} %broadcast_in_dim.107), dimensions={1} | concatenate | bytes 339968 | tf_op jit(solution)/shard_map/concatenate | solution.py:123
  39.4 2.2 %reduce.8 = bf16[16,5312]{1,0:T(8,128)(2,1)} reduce(bf16[16,1,5312]{2,0,1:T(8,128)(2,1)} %bitcast.151, bf16[]{:T(256)} %broadcast.320), dimensions={1}, to_apply=%copy.62.reduce_sub_computation | reduce | bytes 339970 | tf_op jit(solution)/shard_map/all_to_all | solution.py:131
  41.6 1.8 %reshape.463 = bf16[16,2,2656]{2,1,0:T(2,128)(2,1)} reshape(bf16[16,5312]{1,0:T(8,128)(2,1)} %reduce.8) | data formatting | bytes 339968
  43.3 12.6 %all-to-all-start.1 = ((bf16[16,2,2656]{2,1,0:T(2,128)(2,1)}), bf16[16,2,2656]{2,1,0:T(2,128)(2,1)}, u32[]{:S(2)}, u32[]{:S(2)}) async-start(bf16[16,2,2656]{2,1,0:T(2,128)(2,1)} %reshape.463), calls=%async_computation.1 | async-start | bytes 344064 | tf_op jit(solution)/shard_map/all_to_all | solution.py:131
  58.4 9.9 %all-to-all-done.1 = bf16[16,2,2656]{2,1,0:T(2,128)(2,1)} async-done(((bf16[16,2,2656]{2,1,0:T(2,128)(2,1)}), bf16[16,2,2656]{2,1,0:T(2,128)(2,1)}, u32[]{:S(2)}, u32[]{:S(2)}) %all-to-all-start.1) | async-done | bytes 170016 | tf_op jit(solution)/shard_map/all_to_all | solution.py:131
  68.3 2.3 %reshape.464 = bf16[16,1,5312]{2,1,0:T(2,128)(2,1)} reshape(bf16[16,2,2656]{2,1,0:T(2,128)(2,1)} %all-to-all-done.1) | data formatting | bytes 339968
  70.5 2.4 %copy.63 = bf16[16,1,5312]{0,2,1:T(8,128)(2,1)} copy(bf16[16,1,5312]{2,1,0:T(2,128)(2,1)} %reshape.464) | data formatting | bytes 339968 | tf_op jit(solution)/shard_map/all_to_all | solution.py:131
  74.1 1.7 %slice.139 = bf16[16,1024]{0,1:T(8,128)(2,1)} slice(bf16[16,5312]{0,1:T(8,128)(2,1)} %bitcast.141), slice={[0:16], [4288:5312]} | slice | bytes 65536 | tf_op jit(solution)/shard_map/slice | solution.py:139
  77.1 2.5 %fusion = bf16[4096]{0:T(1024)(128)(2,1)} fusion(bf16[16,5312]{0,1:T(8,128)(2,1)} %bitcast.142, f32[16,4,8]{0,2,1:T(8,128)S(1)} %fusion.24), kind=kLoop, calls=%fused_computation.9 | loop fusion | flops 192512 | bytes 141312 | tf_op jit(solution)/shard_map/reduce_sum | solution.py:143
  79.5 1.7 %copy.78 = bf16[16,8,128]{2,1,0:T(8,128)(2,1)} copy(bf16[16,8,128]{0,2,1:T(8,128)(2,1)} %bitcast.146) | data formatting | bytes 65536 | tf_op jit(solution)/shard_map/reshape | solution.py:139
  81.2 1.3 gather_fusion.3
  85.9 3.2 %reduce.9 = bf16[16,5312]{1,0:T(8,128)(2,1)} reduce(bf16[16,1,5312]{2,1,0:T(2,128)(2,1)} %broadcast_in_dim.108, bf16[]{:T(256)} %broadcast.320), dimensions={1}, to_apply=%broadcast_in_dim.108.reduce_sub_computation | reduce | bytes 339970 | tf_op jit(solution)/shard_map/broadcast_in_dim | solution.py:165
  89.1 1.8 %reshape.465 = bf16[16,2,2656]{2,1,0:T(2,128)(2,1)} reshape(bf16[16,5312]{1,0:T(8,128)(2,1)} %reduce.9) | data formatting | bytes 339968
  90.9 8.1 %all-to-all-start.2 = ((bf16[16,2,2656]{2,1,0:T(2,128)(2,1)}), bf16[16,2,2656]{2,1,0:T(2,128)(2,1)}, u32[]{:S(2)}, u32[]{:S(2)}) async-start(bf16[16,2,2656]{2,1,0:T(2,128)(2,1)} %reshape.465), calls=%async_computation.2 | async-start | bytes 344064 | tf_op jit(solution)/shard_map/all_to_all | solution.py:164
  101.3 10.0 %all-to-all-done.2 = bf16[16,2,2656]{2,1,0:T(2,128)(2,1)} async-done(((bf16[16,2,2656]{2,1,0:T(2,128)(2,1)}), bf16[16,2,2656]{2,1,0:T(2,128)(2,1)}, u32[]{:S(2)}, u32[]{:S(2)}) %all-to-all-start.2) | async-done | bytes 170016 | tf_op jit(solution)/shard_map/all_to_all | solution.py:164
  111.3 2.3 %reshape.466 = bf16[16,1,5312]{2,1,0:T(2,128)(2,1)} reshape(bf16[16,2,2656]{2,1,0:T(2,128)(2,1)} %all-to-all-done.2) | data formatting | bytes 339968
  116.3 1.7 %reshape.378 = f32[8,8,8,128]{3,2,1,0:T(8,128)} reshape(f32[16,4096]{1,0:T(8,128)} %slice_convert_fusion) | data formatting | bytes 524288 | tf_op jit(solution)/shard_map/reshape | solution.py:167
  119.5 1.3 gather_fusion.5
  120.9 1.8 %broadcast_select_fusion = bf16[32,2,1,2,8,128]{5,4,3,1,2,0:T(8,128)(2,1)} fusion(bf16[32,2,1,2,8,128]{5,4,3,1,2,0:T(8,128)(2,1)} %bitcast.147, pred[32,2]{1,0:T(8,128)(4,1)S(1)} %copy-done.6), kind=kLoop, calls=%fused_computation.27 | loop fusion | flops 131072 | bytes 524352 | tf_op jit(solution)/shard_map/jit(_where)/select_n | solution.py:199
  122.6 11.5 %all-to-all-start.3 = ((bf16[32,2,1,2,8,128]{5,4,3,1,2,0:T(8,128)(2,1)}), bf16[32,2,1,2,8,128]{5,4,3,1,2,0:T(8,128)(2,1)}, u32[]{:S(2)}, u32[]{:S(2)}) async-start(bf16[32,2,1,2,8,128]{5,4,3,1,2,0:T(8,128)(2,1)} %broadcast_select_fusion), calls=%async_computation.3 | async-start | bytes 524288 | tf_op jit(solution)/shard_map/all_to_all | solution.py:205
  136.1 1.9 %divide_convert_fusion = bf16[8,8,8,128]{3,2,1,0:T(8,128)(2,1)} fusion(f32[8,8,8,128]{3,2,1,0:T(8,128)} %reshape.378, f32[8,8,8]{2,1,0:T(8,128)S(1)} %get-tuple-element.20, f32[8,8,128]{2,1,0:T(8,128)S(1)} %copy.68, f32[8,8,8]{2,1,0:T(8,128)S(1)} %get-tuple-element.22, f32[8,8,8]{2,1,0:T(8,128)S(1)} %get-tuple-element.21), kind=kLoop, calls=%fused_computation.25 | loop fusion | flops 327680 | bytes 432128 | tf_op jit(solution)/shard_map/convert_element_type | solution.py:38
  138.0 5.1 %all-to-all-done.3 = bf16[32,2,1,2,8,128]{5,4,3,1,2,0:T(8,128)(2,1)} async-done(((bf16[32,2,1,2,8,128]{5,4,3,1,2,0:T(8,128)(2,1)}), bf16[32,2,1,2,8,128]{5,4,3,1,2,0:T(8,128)(2,1)}, u32[]{:S(2)}, u32[]{:S(2)}) %all-to-all-start.3) | async-done | bytes 262176 | tf_op jit(solution)/shard_map/all_to_all | solution.py:205
  (100 shorter events, 29.9 us)
Async XLA Ops:
  0.6 32.4 %copy-start = (bf16[128,64,128]{2,1,0:T(8,128)(2,1)S(1)}, bf16[128,64,128]{2,1,0:T(8,128)(2,1)}, u32[]{:S(2)}) copy-start(bf16[128,64,128]{2,1,0:T(8,128)(2,1)} %param.14) | copy-start | bytes 6291460
  0.6 1.7 %copy-start.11 = (bf16[256,256]{1,0:T(8,128)(2,1)S(1)}, bf16[256,256]{1,0:T(8,128)(2,1)}, u32[]{:S(2)}) copy-start(bf16[256,256]{1,0:T(8,128)(2,1)} %param.11) | copy-start | bytes 393220
  0.7 1.7 %copy-start.12 = (bf16[256,128]{1,0:T(8,128)(2,1)S(1)}, bf16[256,128]{1,0:T(8,128)(2,1)}, u32[]{:S(2)}) copy-start(bf16[256,128]{1,0:T(8,128)(2,1)} %param.12) | copy-start | bytes 196612
  0.7 1.6 %copy-start.3 = (bf16[256,8,128]{2,1,0:T(8,128)(2,1)S(1)}, bf16[256,8,128]{2,1,0:T(8,128)(2,1)}, u32[]{:S(2)}) copy-start(bf16[256,8,128]{2,1,0:T(8,128)(2,1)} %param.13) | copy-start | bytes 1572868
  2.7 0.9 copy-start.7
  6.3 12.4 %copy-start.10 = (s32[8]{0:T(128)S(1)}, s32[8]{0:T(128)}, u32[]{:S(2)}) copy-start(s32[8]{0:T(128)} %param.18) | copy-start | bytes 100
  6.3 12.4 %copy-start.1 = (s32[8,32]{1,0:T(8,128)S(1)}, s32[8,32]{1,0:T(8,128)}, u32[]{:S(2)}) copy-start(s32[8,32]{1,0:T(8,128)} %param.19) | copy-start | bytes 3076
  7.7 28.0 %all-to-all-start = ((f32[32,8,256]{2,1,0:T(8,128)}), f32[32,8,256]{2,1,0:T(8,128)}, u32[]{:S(2)}, u32[]{:S(2)}) async-start(f32[32,8,256]{2,1,0:T(8,128)} %copy.61), calls=%async_computation | async-start | bytes 524288 | tf_op jit(solution)/shard_map/all_to_all | solution.py:90
  36.7 20.1 %copy-start.5 = (f32[8,256]{1,0:T(8,128)}, f32[8,256]{1,0:T(8,128)S(1)}, u32[]{:S(2)}) copy-start(f32[8,256]{1,0:T(8,128)S(1)} %reduce_sum.58) | copy-start | bytes 24580
  43.3 24.9 %all-to-all-start.1 = ((bf16[16,2,2656]{2,1,0:T(2,128)(2,1)}), bf16[16,2,2656]{2,1,0:T(2,128)(2,1)}, u32[]{:S(2)}, u32[]{:S(2)}) async-start(bf16[16,2,2656]{2,1,0:T(2,128)(2,1)} %reshape.463), calls=%async_computation.1 | async-start | bytes 344064 | tf_op jit(solution)/shard_map/all_to_all | solution.py:131
  56.9 0.7 copy-start.9
  77.0 5.6 %copy-start.4 = (bf16[8,64,128]{2,1,0:T(8,128)(2,1)S(1)}, bf16[8,64,128]{2,1,0:T(8,128)(2,1)}, u32[]{:S(2)}) copy-start(bf16[8,64,128]{2,1,0:T(8,128)(2,1)} %gather_fusion.2) | copy-start | bytes 393220
  90.9 20.4 %all-to-all-start.2 = ((bf16[16,2,2656]{2,1,0:T(2,128)(2,1)}), bf16[16,2,2656]{2,1,0:T(2,128)(2,1)}, u32[]{:S(2)}, u32[]{:S(2)}) async-start(bf16[16,2,2656]{2,1,0:T(2,128)(2,1)} %reshape.465), calls=%async_computation.2 | async-start | bytes 344064 | tf_op jit(solution)/shard_map/all_to_all | solution.py:164
  99.0 19.8 %copy-start.8 = (s32[8]{0:T(128)S(1)}, s32[8]{0:T(128)}, u32[]{:S(2)}) copy-start(s32[8]{0:T(128)} %get-tuple-element.39) | copy-start | bytes 100
  113.5 7.3 %copy-start.6 = (pred[32,2]{1,0:T(8,128)(4,1)S(1)}, pred[32,2]{1,0:T(8,128)(4,1)}, u32[]{:S(2)}) copy-start(pred[32,2]{1,0:T(8,128)(4,1)} %copy.54) | copy-start | bytes 196
  122.6 20.4 %all-to-all-start.3 = ((bf16[32,2,1,2,8,128]{5,4,3,1,2,0:T(8,128)(2,1)}), bf16[32,2,1,2,8,128]{5,4,3,1,2,0:T(8,128)(2,1)}, u32[]{:S(2)}, u32[]{:S(2)}) async-start(bf16[32,2,1,2,8,128]{5,4,3,1,2,0:T(8,128)(2,1)} %broadcast_select_fusion), calls=%async_computation.3 | async-start | bytes 524288 | tf_op jit(solution)/shard_map/all_to_all | solution.py:205
  144.0 1.1 copy-start.2

commit v7 on v6

--- a/solution.py
+++ b/solution.py
@@ -114,29 +114,39 @@
         "hgin,inhd->hgid", weights, values, preferred_element_type=jnp.float32
     )
 
-    block = heads_per_target * rows * head_dim
+    block_rows = heads_per_target * rows
     stat_count = heads_per_target * rows
+    stat_rows = -(-6 * stat_count // head_dim)
+    spare_rows = 8 - stat_rows
     stats = jnp.concatenate(
         [local_top.reshape(groups, stat_count), local_total.reshape(groups, stat_count)], axis=1
     )
-    mid_flat = summed[:, column_span:].astype(jnp.bfloat16).reshape(1, -1)
+    stat_pack = jnp.concatenate(
+        [split_three(stats), jnp.zeros((groups, stat_rows * head_dim - 6 * stat_count), jnp.bfloat16)],
+        axis=1,
+    ).reshape(groups, stat_rows, head_dim)
+    mid_rows = summed[:, column_span:].astype(jnp.bfloat16)
     parcel = jnp.concatenate(
         [
-            local_mixed.reshape(groups, block).astype(jnp.bfloat16),
-            split_three(stats),
-            jnp.broadcast_to(mid_flat, (groups, mid_flat.shape[1])),
+            local_mixed.reshape(groups, block_rows, head_dim).astype(jnp.bfloat16),
+            jnp.broadcast_to(mid_rows[None], (groups,) + mid_rows.shape),
+            stat_pack,
+            jnp.zeros((groups, spare_rows, head_dim), jnp.bfloat16),
         ],
         axis=1,
     )
     received = lax.all_to_all(parcel, "grp", 0, 0, tiled=False)
-    stat_end = block + 6 * stat_count
-    shard_mixed = received[:, :block].astype(jnp.float32).reshape(
+    stat_at = block_rows + rows
+    shard_mixed = received[:, :block_rows].astype(jnp.float32).reshape(
         groups, heads_per_target, rows, head_dim
     )
-    shard_stats = join_three(received[:, block:stat_end], 2 * stat_count)
+    shard_stats = join_three(
+        received[:, stat_at : stat_at + stat_rows].reshape(groups, -1)[:, : 6 * stat_count],
+        2 * stat_count,
+    )
     shard_top = shard_stats[:, :stat_count].reshape(groups, heads_per_target, rows)
     shard_total = shard_stats[:, stat_count:].reshape(groups, heads_per_target, rows)
-    mid_spread = received[:, stat_end:].reshape(groups, rows, -1)
+    mid_spread = received[:, block_rows:stat_at]
     top_own = jnp.max(shard_top, axis=0)
     shard_scale = jnp.exp(shard_top - top_own[None])
     total_own = jnp.sum(shard_total * shard_scale, axis=0)
@@ -149,26 +159,37 @@
     )
     fresh_columns = (base_resident + adapter_scale * adapter_update).astype(jnp.bfloat16)
 
+    own_stats = jnp.concatenate(
+        [top_own.reshape(1, stat_count), total_own.reshape(1, stat_count)], axis=1
+    )
     merged = jnp.concatenate(
         [
-            mixed_own.reshape(1, block).astype(jnp.bfloat16),
-            split_three(
-                jnp.concatenate(
-                    [top_own.reshape(1, stat_count), total_own.reshape(1, stat_count)], axis=1
-                )
-            ),
-            fresh_columns.reshape(1, -1),
+            mixed_own.reshape(block_rows, head_dim).astype(jnp.bfloat16),
+            fresh_columns,
+            jnp.concatenate(
+                [
+                    split_three(own_stats),
+                    jnp.zeros((1, stat_rows * head_dim - 6 * stat_count), jnp.bfloat16),
+                ],
+                axis=1,
+            ).reshape(stat_rows, head_dim),
+            jnp.zeros((spare_rows, head_dim), jnp.bfloat16),
         ],
-        axis=1,
+        axis=0,
     )
     everything = lax.all_to_all(
-        jnp.broadcast_to(merged, (groups, merged.shape[1])), "grp", 0, 0, tiled=False
-    )
-    all_mixed = everything[:, :block].astype(jnp.float32).reshape(heads, group_size, rows, head_dim)
-    all_stats = join_three(everything[:, block:stat_end], 2 * stat_count)
+        jnp.broadcast_to(merged[None], (groups,) + merged.shape), "grp", 0, 0, tiled=False
+    )
+    all_mixed = everything[:, :block_rows].astype(jnp.float32).reshape(
+        heads, group_size, rows, head_dim
+    )
+    all_stats = join_three(
+        everything[:, stat_at : stat_at + stat_rows].reshape(groups, -1)[:, : 6 * stat_count],
+        2 * stat_count,
+    )
     all_top = all_stats[:, :stat_count].reshape(heads, group_size, rows)
     all_total = all_stats[:, stat_count:].reshape(heads, group_size, rows)
-    new_all = everything[:, stat_end:].reshape(groups, rows, column_span)
+    new_all = everything[:, block_rows:stat_at]
     new_keys = new_all[: groups // 2]
     new_values = new_all[groups // 2 :]
     attention_parts = (all_mixed, all_top, all_total, query, new_keys, new_values)

time: 147 us -> 120 us (0.82)
  local copies, waits for them, and re-layouts: 45.3 us -> 25.9 us
  other arithmetic: 25.1 us -> 19.5 us
    unnamed x35 -> x27, local copies, waits for them, and re-layouts: 13 us -> 3.92 us
    reshape x2 -> x1, local copies, waits for them, and re-layouts: 3.36 us -> 0.01 us  [shards(): stat_pack = jnp.concatenate([split_three(stats), jnp.zeros((groups, stat_...]
    broadcast_in_dim x1 -> x0, other arithmetic: 3.18 us -> none  [shards(): jnp.broadcast_to(merged, (groups, merged.shape[1]))]
    all_to_all x2 -> x0, local copies, waits for them, and re-layouts: 2.84 us -> none  [shards(): received = lax.all_to_all(parcel, 'grp', 0, 0, tiled=False)]
    convert_element_type x3 -> x1, local copies, waits for them, and re-layouts: 3.25 us -> 0.93 us  [shards(): local_mixed.reshape(groups, block_rows, head_dim).astype(jnp.bfloat16)]
    slice x2 -> x6, local copies, waits for them, and re-layouts: 2.38 us -> 4.64 us  [the longest x1 0.92 us: shards(): everything[:, :block_rows].astype(jnp.float32)]
    concatenate x1 -> x3, other arithmetic: 0.07 us -> 2.31 us  [the longest x1 1.46 us: shards(): jnp.concatenate([local_mixed.reshape(groups, block_rows, head_dim).astype...]
    all_to_all x1 -> x0, other arithmetic: 2.2 us -> none  [shards(): received = lax.all_to_all(parcel, 'grp', 0, 0, tiled=False)]
where the time goes in v7:
time: 120 us; the launch traced here: 119 us
  starting transfers between devices  43.9 us (37%)
  local copies, waits for them, and re-layouts  25.9 us (22%)
  waiting for transfers between devices  24.2 us (20%)
  other arithmetic  19.5 us (16%)
  matrix products  4.34 us (4%)
    all_to_all x1, starting transfers between devices, shards(): received = lax.all_to_all(parcel, 'grp', 0, 0, tiled=False)  12.6 us
    all_to_all x1, starting transfers between devices, shards(): lax.all_to_all(outbound, 'req', split_axis=0, concat_axis=0, tiled=True)  11.9 us
    all_to_all x1, waiting for transfers between devices, shards(): received = lax.all_to_all(parcel, 'grp', 0, 0, tiled=False)  11.4 us
    all_to_all x1, starting transfers between devices, shards(): lax.all_to_all(partial, 'req', 0, 0, tiled=False)  11 us
    all_to_all x1, starting transfers between devices, shards(): lax.all_to_all(jnp.broadcast_to(merged[None], (groups,) + merged.shape),...  8.44 us
    all_to_all x1, waiting for transfers between devices, shards(): lax.all_to_all(jnp.broadcast_to(merged[None], (groups,) + merged.shape),...  8.35 us
    all_to_all x1, waiting for transfers between devices, shards(): lax.all_to_all(outbound, 'req', split_axis=0, concat_axis=0, tiled=True)  4.42 us
    unnamed x27, local copies, waits for them, and re-layouts  3.92 us
  transfers between devices with their start and end apart: 4, of which 3 were waited for; matrix products, arithmetic and copies ran while one was open for 18% of the time, Pallas kernels for 0%

profile of v7, /device:TPU:1, one launch (start us, length us, event | category | flops | bytes accessed | tf_op | source)
XLA Modules:
  0.0 118.8 jit_solution(7684170773636284497)
XLA Ops:
  0.7 1.5 %copy.122 = bf16[320,1,2,8,128]{4,3,2,1,0:T(8,128)(2,1)S(1)} copy(bf16[320,1,2,8,128]{4,3,2,1,0:T(8,128)(2,1)} %param.17) | data formatting | bytes 2621440
  2.8 0.9 slice.129
  5.2 1.1 copy.86
  6.8 0.9 copy.66
  7.7 11.0 %all-to-all-start = ((f32[32,8,256]{2,1,0:T(8,128)}), f32[32,8,256]{2,1,0:T(8,128)}, u32[]{:S(2)}, u32[]{:S(2)}) async-start(f32[32,8,256]{2,1,0:T(8,128)} %copy.66), calls=%async_computation | async-start | bytes 524288 | tf_op jit(solution)/shard_map/all_to_all | solution.py:90
  18.9 1.8 %gather_fusion.1 = bf16[256,2,8,128]{3,2,1,0:T(8,128)(2,1)} fusion(bf16[320,2,8,128]{3,2,1,0:T(8,128)(2,1)S(1)} %bitcast.118, s32[1024]{0:T(1024)S(1)} %pad_clamp_fusion.2), kind=kCustom, calls=%fused_computation.1 | custom fusion | bytes 2098176 | tf_op jit(solution)/shard_map/gather | solution.py:99
  20.7 1.5 %copy.62 = bf16[256,2,8,128]{3,0,2,1:T(8,128)(2,1)S(1)} copy(bf16[256,2,8,128]{3,2,1,0:T(8,128)(2,1)} %gather_fusion.1) | data formatting | bytes 2097152 | tf_op jit(solution)/shard_map/gather | solution.py:99
  22.7 1.0 fusion.2
  24.0 1.1 gather_fusion
  25.5 0.9 copy.64
  27.2 1.2 shift-left_bitcast_fusion
  28.9 1.3 %gather_fusion.2 = bf16[8,64,128]{2,1,0:T(8,128)(2,1)} fusion(bf16[128,64,128]{2,1,0:T(8,128)(2,1)S(1)} %copy-done, s32[1024]{0:T(1024)} %pad_clamp_fusion.1), kind=kCustom, calls=%fused_computation.2 | custom fusion | bytes 262176 | tf_op jit(solution)/shard_map/gather | solution.py:88
  30.3 1.6 %reduce_sum.57 = f32[8,256]{1,0:T(8,128)} reduce(f32[32,8,256]{2,1,0:T(8,128)} %all-to-all-done, f32[]{:T(128)} %constant.100.clone.1), dimensions={0}, to_apply=%region_3.4 | reduce | flops 63488 | bytes 270340 | tf_op jit(solution)/shard_map/reduce_sum | solution.py:92
  32.5 1.5 %maximum_maximum_fusion = bf16[16,48,128]{2,1,0:T(8,128)(2,1)} fusion(bf16[16,2,128]{2,1,0:T(2,128)(2,1)S(1)} %reshape.351, bf16[16,8,128]{2,1,0:T(8,128)(2,1)S(1)} %broadcast_in_dim.114, bf16[16,32,128]{2,1,0:T(8,128)(2,1)S(1)} %bitcast.130, bf16[48]{0:T(256)(128)(2,1)} %pad.17.clone), kind=kLoop, calls=%fused_computation.28 | loop fusion | flops 786432 | bytes 368736 | tf_op jit(solution)/shard_map/concatenate | solution.py:129
  34.0 12.6 %all-to-all-start.1 = ((bf16[16,48,128]{2,1,0:T(8,128)(2,1)}), bf16[16,48,128]{2,1,0:T(8,128)(2,1)}, u32[]{:S(2)}, u32[]{:S(2)}) async-start(bf16[16,48,128]{2,1,0:T(8,128)(2,1)} %maximum_maximum_fusion), calls=%async_computation.1 | async-start | bytes 393216 | tf_op jit(solution)/shard_map/all_to_all | solution.py:138
  46.6 0.9 convert_reduce_fusion
  48.2 11.4 %all-to-all-done.1 = bf16[16,48,128]{2,1,0:T(8,128)(2,1)} async-done(((bf16[16,48,128]{2,1,0:T(8,128)(2,1)}), bf16[16,48,128]{2,1,0:T(8,128)(2,1)}, u32[]{:S(2)}, u32[]{:S(2)}) %all-to-all-start.1) | async-done | bytes 196640 | tf_op jit(solution)/shard_map/all_to_all | solution.py:138
  62.1 1.0 fusion.31
  63.9 1.0 multiply_reduce_fusion
  66.4 8.4 %all-to-all-start.2 = ((bf16[16,48,128]{2,1,0:T(8,128)(2,1)}), bf16[16,48,128]{2,1,0:T(8,128)(2,1)}, u32[]{:S(2)}, u32[]{:S(2)}) async-start(bf16[16,48,128]{2,1,0:T(8,128)(2,1)} %broadcast_in_dim.117), calls=%async_computation.2 | async-start | bytes 393216 | tf_op jit(solution)/shard_map/all_to_all | solution.py:180
  77.9 1.2 %fusion.39 = pred[8]{0:T(512)(128)(4,1)} fusion(s32[]{:T(128)S(6)} %axis_index.22, s32[8]{0:T(128)} %param.18), kind=kLoop, calls=%fused_computation.120 | loop fusion | flops 96 | bytes 44 | tf_op jit(solution)/shard_map/eq | solution.py:212
  79.1 8.4 %all-to-all-done.2 = bf16[16,48,128]{2,1,0:T(8,128)(2,1)} async-done(((bf16[16,48,128]{2,1,0:T(8,128)(2,1)}), bf16[16,48,128]{2,1,0:T(8,128)(2,1)}, u32[]{:S(2)}, u32[]{:S(2)}) %all-to-all-start.2) | async-done | bytes 196640 | tf_op jit(solution)/shard_map/all_to_all | solution.py:180
  89.3 0.9 slice.143
  91.7 1.0 scatter_fusion
  92.7 1.4 %gather_fusion.5 = bf16[64,2,8,128]{3,2,1,0:T(8,128)(2,1)} fusion(bf16[320,2,8,128]{3,2,1,0:T(8,128)(2,1)S(1)} %scatter_fusion, s32[1024]{0:T(1024)} %pad_clamp_fusion), kind=kCustom, calls=%fused_computation.5 | custom fusion | bytes 524544 | tf_op jit(solution)/shard_map/gather | solution.py:222
  94.1 1.8 %broadcast_select_fusion = bf16[32,2,1,2,8,128]{5,4,3,1,2,0:T(8,128)(2,1)} fusion(bf16[32,2,1,2,8,128]{5,4,3,1,2,0:T(8,128)(2,1)} %bitcast.125, pred[32,2]{1,0:T(8,128)(4,1)} %copy.61), kind=kLoop, calls=%fused_computation.26 | loop fusion | flops 131072 | bytes 524352 | tf_op jit(solution)/shard_map/jit(_where)/select_n | solution.py:220
  95.9 11.9 %all-to-all-start.3 = ((bf16[32,2,1,2,8,128]{5,4,3,1,2,0:T(8,128)(2,1)}), bf16[32,2,1,2,8,128]{5,4,3,1,2,0:T(8,128)(2,1)}, u32[]{:S(2)}, u32[]{:S(2)}) async-start(bf16[32,2,1,2,8,128]{5,4,3,1,2,0:T(8,128)(2,1)} %broadcast_select_fusion), calls=%async_computation.3 | async-start | bytes 524288 | tf_op jit(solution)/shard_map/all_to_all | solution.py:226
  107.8 1.1 fusion.13
  110.4 1.9 %divide_convert_fusion = bf16[8,8,8,128]{3,2,1,0:T(8,128)(2,1)} fusion(f32[8,8,8,128]{3,2,1,0:T(8,128)} %convert.32, f32[8,8,8]{2,1,0:T(8,128)S(1)} %get-tuple-element.28, f32[8,8,128]{2,1,0:T(8,128)S(1)} %copy.73, f32[8,8,8]{2,1,0:T(8,128)S(1)} %get-tuple-element.30, f32[8,8,8]{2,1,0:T(8,128)S(1)} %get-tuple-element.29), kind=kLoop, calls=%fused_computation.23 | loop fusion | flops 327680 | bytes 432128 | tf_op jit(solution)/shard_map/convert_element_type | solution.py:38
  112.3 4.4 %all-to-all-done.3 = bf16[32,2,1,2,8,128]{5,4,3,1,2,0:T(8,128)(2,1)} async-done(((bf16[32,2,1,2,8,128]{5,4,3,1,2,0:T(8,128)(2,1)}), bf16[32,2,1,2,8,128]{5,4,3,1,2,0:T(8,128)(2,1)}, u32[]{:S(2)}, u32[]{:S(2)}) %all-to-all-start.3) | async-done | bytes 262176 | tf_op jit(solution)/shard_map/all_to_all | solution.py:226
  116.8 1.0 constant_dynamic-update-slice_fusion
  117.8 1.0 copy-done.2
  (91 shorter events, 19.1 us)
Async XLA Ops:
  0.6 28.3 %copy-start = (bf16[128,64,128]{2,1,0:T(8,128)(2,1)S(1)}, bf16[128,64,128]{2,1,0:T(8,128)(2,1)}, u32[]{:S(2)}) copy-start(bf16[128,64,128]{2,1,0:T(8,128)(2,1)} %param.14) | copy-start | bytes 6291460
  0.6 1.7 %copy-start.8 = (bf16[256,256]{1,0:T(8,128)(2,1)S(1)}, bf16[256,256]{1,0:T(8,128)(2,1)}, u32[]{:S(2)}) copy-start(bf16[256,256]{1,0:T(8,128)(2,1)} %param.11) | copy-start | bytes 393220
  0.7 1.7 %copy-start.10 = (bf16[256,128]{1,0:T(8,128)(2,1)S(1)}, bf16[256,128]{1,0:T(8,128)(2,1)}, u32[]{:S(2)}) copy-start(bf16[256,128]{1,0:T(8,128)(2,1)} %param.12) | copy-start | bytes 196612
  0.7 1.6 %copy-start.3 = (bf16[256,8,128]{2,1,0:T(8,128)(2,1)S(1)}, bf16[256,8,128]{2,1,0:T(8,128)(2,1)}, u32[]{:S(2)}) copy-start(bf16[256,8,128]{2,1,0:T(8,128)(2,1)} %param.13) | copy-start | bytes 1572868
  2.7 0.9 copy-start.6
  6.3 12.4 %copy-start.7 = (s32[8]{0:T(128)S(1)}, s32[8]{0:T(128)}, u32[]{:S(2)}) copy-start(s32[8]{0:T(128)} %param.18) | copy-start | bytes 100
  6.3 12.5 %copy-start.1 = (s32[8,32]{1,0:T(8,128)S(1)}, s32[8,32]{1,0:T(8,128)}, u32[]{:S(2)}) copy-start(s32[8,32]{1,0:T(8,128)} %param.19) | copy-start | bytes 3076
  7.7 22.6 %all-to-all-start = ((f32[32,8,256]{2,1,0:T(8,128)}), f32[32,8,256]{2,1,0:T(8,128)}, u32[]{:S(2)}, u32[]{:S(2)}) async-start(f32[32,8,256]{2,1,0:T(8,128)} %copy.66), calls=%async_computation | async-start | bytes 524288 | tf_op jit(solution)/shard_map/all_to_all | solution.py:90
  20.7 1.5 %copy-start.9 = (bf16[8,8192]{1,0:T(8,128)(2,1)S(1)}, bf16[8,8192]{1,0:T(8,128)(2,1)}, u32[]{:S(2)}) copy-start(bf16[8,8192]{1,0:T(8,128)(2,1)} %param.16) | copy-start | bytes 393220
  34.0 25.6 %all-to-all-start.1 = ((bf16[16,48,128]{2,1,0:T(8,128)(2,1)}), bf16[16,48,128]{2,1,0:T(8,128)(2,1)}, u32[]{:S(2)}, u32[]{:S(2)}) async-start(bf16[16,48,128]{2,1,0:T(8,128)(2,1)} %maximum_maximum_fusion), calls=%async_computation.1 | async-start | bytes 393216 | tf_op jit(solution)/shard_map/all_to_all | solution.py:138
  66.4 21.0 %all-to-all-start.2 = ((bf16[16,48,128]{2,1,0:T(8,128)(2,1)}), bf16[16,48,128]{2,1,0:T(8,128)(2,1)}, u32[]{:S(2)}, u32[]{:S(2)}) async-start(bf16[16,48,128]{2,1,0:T(8,128)(2,1)} %broadcast_in_dim.117), calls=%async_computation.2 | async-start | bytes 393216 | tf_op jit(solution)/shard_map/all_to_all | solution.py:180
  89.3 2.4 %copy-start.4 = (bf16[8,8,128]{2,0,1:T(8,128)(2,1)}, bf16[8,8,128]{2,0,1:T(8,128)(2,1)S(1)}, u32[]{:S(2)}) copy-start(bf16[8,8,128]{2,0,1:T(8,128)(2,1)S(1)} %copy.118) | copy-start | bytes 49156
  91.7 16.1 %copy-start.5 = (bf16[8,8,128]{2,0,1:T(8,128)(2,1)S(1)}, bf16[8,8,128]{2,0,1:T(8,128)(2,1)}, u32[]{:S(2)}) copy-start(bf16[8,8,128]{2,0,1:T(8,128)(2,1)} %copy-done.4) | copy-start | bytes 49156
  95.9 20.8 %all-to-all-start.3 = ((bf16[32,2,1,2,8,128]{5,4,3,1,2,0:T(8,128)(2,1)}), bf16[32,2,1,2,8,128]{5,4,3,1,2,0:T(8,128)(2,1)}, u32[]{:S(2)}, u32[]{:S(2)}) async-start(bf16[32,2,1,2,8,128]{5,4,3,1,2,0:T(8,128)(2,1)} %broadcast_select_fusion), calls=%async_computation.3 | async-start | bytes 524288 | tf_op jit(solution)/shard_map/all_to_all | solution.py:226
  117.7 1.1 copy-start.2

commit v8 on v7

--- a/solution.py
+++ b/solution.py
@@ -22,8 +22,23 @@
     return wide[..., :width] + wide[..., width : 2 * width] + wide[..., 2 * width :]
 
 
-def finish_attention(all_mixed, all_top, all_total, query, new_keys, new_values):
+def finish_attention(everything, query, new_keys, new_values):
     rows, heads, group_size, head_dim = query.shape
+    block_rows = heads * group_size * rows // everything.shape[0]
+    stat_count = block_rows
+    stat_at = block_rows + rows
+    stat_rows = -(-6 * stat_count // head_dim)
+    all_mixed = everything[:, :block_rows].astype(jnp.float32).reshape(
+        heads, group_size, rows, head_dim
+    )
+    all_stats = join_three(
+        everything[:, stat_at : stat_at + stat_rows].reshape(everything.shape[0], -1)[
+            :, : 6 * stat_count
+        ],
+        2 * stat_count,
+    )
+    all_top = all_stats[:, :stat_count].reshape(heads, group_size, rows)
+    all_total = all_stats[:, stat_count:].reshape(heads, group_size, rows)
     new_score = jnp.einsum(
         "ihgd,hid->hgi", query, new_keys, preferred_element_type=jnp.float32
     ) / math.sqrt(head_dim)
@@ -180,19 +195,10 @@
     everything = lax.all_to_all(
         jnp.broadcast_to(merged[None], (groups,) + merged.shape), "grp", 0, 0, tiled=False
     )
-    all_mixed = everything[:, :block_rows].astype(jnp.float32).reshape(
-        heads, group_size, rows, head_dim
-    )
-    all_stats = join_three(
-        everything[:, stat_at : stat_at + stat_rows].reshape(groups, -1)[:, : 6 * stat_count],
-        2 * stat_count,
-    )
-    all_top = all_stats[:, :stat_count].reshape(heads, group_size, rows)
-    all_total = all_stats[:, stat_count:].reshape(heads, group_size, rows)
     new_all = everything[:, block_rows:stat_at]
     new_keys = new_all[: groups // 2]
     new_values = new_all[groups // 2 :]
-    attention_parts = (all_mixed, all_top, all_total, query, new_keys, new_values)
+    attention_parts = (everything, query, new_keys, new_values)
 
     targets = departing_target[:, 0]
     count_out = departing_slots.shape[0]
@@ -211,16 +217,27 @@
     offset = lengths % page_size
     mine = offset // slot_tokens == group_index
     token_local = offset % slot_tokens
+    fresh = jnp.stack([new_keys, new_values], axis=0).transpose(2, 0, 1, 3)
     current = key_value_pages[page_slot, token_local]
-    fresh = jnp.stack([new_keys, new_values], axis=0).transpose(2, 0, 1, 3)
     written = key_value_pages.at[page_slot, token_local].set(
         jnp.where(mine[:, None, None, None], fresh, current)
     )
 
+    outbound_old = jnp.where(
+        filled[:, :, None, None, None, None],
+        key_value_pages[source_slot],
+        jnp.zeros((), key_value_pages.dtype),
+    )
+    hits = (source_slot[:, :, None] == page_slot[None, None, :]) & mine[None, None, :]
+    hits = hits & filled[:, :, None]
+    patch_request = jnp.argmax(hits, axis=2)
+    patched = jnp.any(hits, axis=2)[:, :, None] & (
+        jnp.arange(slot_tokens, dtype=jnp.int32)[None, None, :] == token_local[patch_request][:, :, None]
+    )
     outbound = jnp.where(
-        filled[:, :, None, None, None, None],
-        written[source_slot],
-        jnp.zeros((), key_value_pages.dtype),
+        patched[:, :, :, None, None, None],
+        fresh[patch_request][:, :, None],
+        outbound_old,
     )
     outbound, attention_parts = lax.optimization_barrier((outbound, attention_parts))
     arrived = lax.all_to_all(outbound, "req", split_axis=0, concat_axis=0, tiled=True)

time: 120 us -> 124 us (1.033)
  local copies, waits for them, and re-layouts: 25.9 us -> 30.4 us
  waiting for transfers between devices: 24.2 us -> 19.7 us
  matrix products: 4.34 us -> 6.08 us
  other arithmetic: 19.5 us -> 21 us
    all_to_all x1, waiting for transfers between devices: 4.42 us -> 0.01 us  [shards(): lax.all_to_all(outbound, 'req', split_axis=0, concat_axis=0, tiled=True)]
    gather x1 -> x3, local copies, waits for them, and re-layouts: 1.43 us -> 3.41 us  [the longest x1 1.32 us: shards(): fresh[patch_request][:, :, None]]
    all_to_all x1, waiting for transfers between devices: 11.4 us -> 9.94 us  [shards(): received = lax.all_to_all(parcel, 'grp', 0, 0, tiled=False)]
    unnamed x27 -> x37, local copies, waits for them, and re-layouts: 3.92 us -> 5.39 us
    all_to_all x1, waiting for transfers between devices: 8.35 us -> 9.78 us  [shards(): lax.all_to_all(jnp.broadcast_to(merged[None], (groups,) + merged.shape),...]
    another operation x1 -> x2, other arithmetic: 0.08 us -> 1.39 us  [the longest x1 1.3 us: shards(): patch_request = jnp.argmax(hits, axis=2)]
  transfers between devices with their start and end apart: 4 -> 4, of which waited for: 3 -> 2; matrix products, arithmetic and copies ran while one was open for 18% -> 27% of each run, Pallas kernels for 0% -> 0%
where the time goes in v8:
time: 124 us; the launch traced here: 122 us
  starting transfers between devices  43.9 us (35%)
  local copies, waits for them, and re-layouts  30.4 us (25%)
  other arithmetic  21 us (17%)
  waiting for transfers between devices  19.7 us (16%)
  matrix products  6.08 us (5%)
    all_to_all x1, starting transfers between devices, shards(): received = lax.all_to_all(parcel, 'grp', 0, 0, tiled=False)  12.6 us
    all_to_all x1, starting transfers between devices, shards(): lax.all_to_all(outbound, 'req', split_axis=0, concat_axis=0, tiled=True)  11.9 us
    all_to_all x1, starting transfers between devices, shards(): lax.all_to_all(partial, 'req', 0, 0, tiled=False)  11 us
    all_to_all x1, waiting for transfers between devices, shards(): received = lax.all_to_all(parcel, 'grp', 0, 0, tiled=False)  9.94 us
    all_to_all x1, waiting for transfers between devices, shards(): lax.all_to_all(jnp.broadcast_to(merged[None], (groups,) + merged.shape),...  9.78 us
    all_to_all x1, starting transfers between devices, shards(): lax.all_to_all(jnp.broadcast_to(merged[None], (groups,) + merged.shape),...  8.44 us
    unnamed x37, local copies, waits for them, and re-layouts  5.39 us
    gather x2, local copies, waits for them, and re-layouts, shards(): gathered = key_value_pages[page_slot_table][:, :, 0]  3.29 us
  transfers between devices with their start and end apart: 4, of which 2 were waited for; matrix products, arithmetic and copies ran while one was open for 27% of the time, Pallas kernels for 0%

profile of v8, /device:TPU:1, one launch (start us, length us, event | category | flops | bytes accessed | tf_op | source)
XLA Modules:
  0.0 122.2 jit_solution(18059836127516191084)
XLA Ops:
  0.7 1.5 %copy.135 = bf16[320,1,2,8,128]{4,3,2,1,0:T(8,128)(2,1)S(1)} copy(bf16[320,1,2,8,128]{4,3,2,1,0:T(8,128)(2,1)} %param.17) | data formatting | bytes 2621440
  5.2 1.1 copy.99
  7.7 11.0 %all-to-all-start = ((f32[32,8,256]{2,1,0:T(8,128)}), f32[32,8,256]{2,1,0:T(8,128)}, u32[]{:S(2)}, u32[]{:S(2)}) async-start(f32[32,8,256]{2,1,0:T(8,128)} %copy.77), calls=%async_computation | async-start | bytes 524288 | tf_op jit(solution)/shard_map/all_to_all | solution.py:105
  18.8 1.8 %gather_fusion.2 = bf16[256,2,8,128]{3,2,1,0:T(8,128)(2,1)} fusion(bf16[320,2,8,128]{3,2,1,0:T(8,128)(2,1)S(1)} %bitcast.120, s32[1024]{0:T(1024)S(1)} %pad_clamp_fusion.2), kind=kCustom, calls=%fused_computation.2 | custom fusion | bytes 2098176 | tf_op jit(solution)/shard_map/gather | solution.py:114
  20.6 1.5 %copy.73 = bf16[256,2,8,128]{3,0,2,1:T(8,128)(2,1)S(1)} copy(bf16[256,2,8,128]{3,2,1,0:T(8,128)(2,1)} %gather_fusion.2) | data formatting | bytes 2097152 | tf_op jit(solution)/shard_map/gather | solution.py:114
  23.1 1.1 fusion.61
  24.3 1.2 fusion.11
  25.5 2.1 %fusion.2 = bf16[8,8,8,128]{3,1,2,0:T(8,128)(2,1)} fusion(bf16[8,32,2,8,128]{4,1,0,3,2:T(8,128)(2,1)} %bitcast.129, f32[8,8,8,32]{3,1,2,0:T(8,128)} %get-tuple-element.51, f32[8,8,8]{1,2,0:T(8,128)S(1)} %get-tuple-element.50, pred[8,32]{1,0:T(8,128)(4,1)S(1)} %broadcast_compare_fusion), kind=kOutput, calls=%fused_computation.14 | convolution fusion | flops 4292608 | bytes 919808 | tf_op jit(solution)/shard_map/hgin,inhd->hgid/dot_general | solution.py:128
  29.4 0.9 copy.75
  31.0 1.2 shift-left_bitcast_fusion
  32.7 1.2 gather_fusion.7
  33.9 1.3 %gather_fusion.3 = bf16[8,64,128]{2,1,0:T(8,128)(2,1)} fusion(bf16[128,64,128]{2,1,0:T(8,128)(2,1)S(1)} %copy-done, s32[1024]{0:T(1024)} %pad_clamp_fusion.1), kind=kCustom, calls=%fused_computation.3 | custom fusion | bytes 262176 | tf_op jit(solution)/shard_map/gather | solution.py:103
  37.3 1.6 %reduce_sum.58 = f32[8,256]{1,0:T(8,128)} reduce(f32[32,8,256]{2,1,0:T(8,128)} %all-to-all-done, f32[]{:T(128)} %constant.107.clone.1), dimensions={0}, to_apply=%region_6.7 | reduce | flops 63488 | bytes 270340 | tf_op jit(solution)/shard_map/reduce_sum | solution.py:107
  39.6 1.5 %maximum_maximum_fusion = bf16[16,48,128]{2,1,0:T(8,128)(2,1)} fusion(bf16[16,2,128]{2,1,0:T(2,128)(2,1)} %reshape.375, bf16[16,8,128]{2,1,0:T(8,128)(2,1)S(1)} %broadcast_in_dim.84, bf16[16,32,128]{2,1,0:T(8,128)(2,1)S(1)} %bitcast.134, bf16[48]{0:T(256)(128)(2,1)S(1)} %pad.17.clone), kind=kLoop, calls=%fused_computation.33 | loop fusion | flops 786432 | bytes 368736 | tf_op jit(solution)/shard_map/concatenate | solution.py:144
  41.1 12.6 %all-to-all-start.1 = ((bf16[16,48,128]{2,1,0:T(8,128)(2,1)}), bf16[16,48,128]{2,1,0:T(8,128)(2,1)}, u32[]{:S(2)}, u32[]{:S(2)}) async-start(bf16[16,48,128]{2,1,0:T(8,128)(2,1)} %maximum_maximum_fusion), calls=%async_computation.1 | async-start | bytes 393216 | tf_op jit(solution)/shard_map/all_to_all | solution.py:153
  55.4 1.3 %iota_reduce_fusion = (pred[32,2]{0,1:T(4,128)(4,1)}, s32[32,2]{0,1:T(2,128)S(1)}) fusion(s32[32,2]{0,1:T(2,128)S(1)} %fusion.20, s32[8]{0:T(128)} %copy-done.6, pred[8]{0:T(512)(128)(4,1)S(1)} %fusion.42, pred[32,2]{0,1:T(4,128)(4,1)S(1)} %and_reduce_fusion), kind=kLoop, calls=%fused_computation.85 | loop fusion | flops 4672 | bytes 680 | tf_op jit(solution)/shard_map/shards/reduce | solution.py:233
  56.8 9.9 %all-to-all-done.1 = bf16[16,48,128]{2,1,0:T(8,128)(2,1)} async-done(((bf16[16,48,128]{2,1,0:T(8,128)(2,1)}), bf16[16,48,128]{2,1,0:T(8,128)(2,1)}, u32[]{:S(2)}, u32[]{:S(2)}) %all-to-all-start.1) | async-done | bytes 196640 | tf_op jit(solution)/shard_map/all_to_all | solution.py:153
  69.1 1.0 fusion.34
  71.0 1.0 multiply_reduce_fusion
  73.5 8.4 %all-to-all-start.2 = ((bf16[16,48,128]{2,1,0:T(8,128)(2,1)}), bf16[16,48,128]{2,1,0:T(8,128)(2,1)}, u32[]{:S(2)}, u32[]{:S(2)}) async-start(bf16[16,48,128]{2,1,0:T(8,128)(2,1)} %broadcast_in_dim.87), calls=%async_computation.2 | async-start | bytes 393216 | tf_op jit(solution)/shard_map/all_to_all | solution.py:195
  82.0 1.3 %gather_fusion.6 = bf16[64,2,8,128]{3,2,1,0:T(8,128)(2,1)} fusion(bf16[320,2,8,128]{3,2,1,0:T(8,128)(2,1)S(1)} %bitcast.121, s32[1024]{0:T(1024)S(1)} %pad_clamp_fusion), kind=kCustom, calls=%fused_computation.6 | custom fusion | bytes 524544 | tf_op jit(solution)/shard_map/gather | solution.py:228
  84.7 9.8 %all-to-all-done.2 = bf16[16,48,128]{2,1,0:T(8,128)(2,1)} async-done(((bf16[16,48,128]{2,1,0:T(8,128)(2,1)}), bf16[16,48,128]{2,1,0:T(8,128)(2,1)}, u32[]{:S(2)}, u32[]{:S(2)}) %all-to-all-start.2) | async-done | bytes 196640 | tf_op jit(solution)/shard_map/all_to_all | solution.py:195
  95.3 1.3 %gather_fusion.5 = bf16[64,2,8,128]{3,2,1,0:T(8,128)(2,1)} fusion(bf16[8,2,8,128]{3,2,1,0:T(8,128)(2,1)S(1)} %maximum_bitcast_fusion.2, s32[1024]{0:T(1024)S(1)} %pad_clamp_fusion.3), kind=kCustom, calls=%fused_computation.5 | custom fusion | bytes 524544 | tf_op jit(solution)/shard_map/gather | solution.py:239
  96.6 1.9 %select_select_fusion = bf16[32,2,1,2,8,128]{5,4,3,1,2,0:T(8,128)(2,1)} fusion(bf16[32,2,1,2,8,128]{5,4,3,1,2,0:T(8,128)(2,1)} %bitcast.127, bf16[32,2,1,2,8,128]{5,4,3,1,2,0:T(8,128)(2,1)} %bitcast.126, pred[32,2]{1,0:T(8,128)(4,1)S(1)} %copy.82, pred[32,2]{1,0:T(8,128)(4,1)S(1)} %copy.72), kind=kLoop, calls=%fused_computation.29 | loop fusion | flops 262144 | bytes 786560 | tf_op jit(solution)/shard_map/jit(_where)/select_n | solution.py:237
  98.5 11.9 %all-to-all-start.3 = ((bf16[32,2,1,2,8,128]{5,4,3,1,2,0:T(8,128)(2,1)}), bf16[32,2,1,2,8,128]{5,4,3,1,2,0:T(8,128)(2,1)}, u32[]{:S(2)}, u32[]{:S(2)}) async-start(bf16[32,2,1,2,8,128]{5,4,3,1,2,0:T(8,128)(2,1)} %select_select_fusion), calls=%async_computation.3 | async-start | bytes 524288 | tf_op jit(solution)/shard_map/all_to_all | solution.py:243
  110.4 1.1 fusion.16
  113.3 1.4 %multiply_add_fusion = (f32[8,8,8]{2,1,0:T(8,128)}, f32[8,8,8]{2,1,0:T(8,128)}, f32[8,8,8]{2,1,0:T(8,128)}) fusion(f32[8,8,8]{2,1,0:T(8,128)S(1)} %reshape.382, f32[8,8,8]{2,1,0:T(8,128)S(1)} %reshape.381, f32[8,8,1,8]{1,3,0,2:T(8,128)} %copy.95), kind=kLoop, calls=%fused_computation.53 | loop fusion | flops 3072 | bytes 12288 | tf_op jit(solution)/shard_map/add | solution.py:48
  115.4 0.9 slice.104
  117.0 1.4 %scatter_fusion = bf16[320,2,8,128]{3,2,1,0:T(8,128)(2,1)S(1)} fusion(bf16[320,2,8,128]{3,2,1,0:T(8,128)(2,1)S(1)} %bitcast.122, s32[8]{0:T(128)} %get-tuple-element.47, bf16[8,2,8,128]{3,2,1,0:T(8,128)(2,1)} %broadcast_select_fusion), kind=kCustom, calls=%fused_computation.8 | custom fusion | bytes 98336 | tf_op jit(solution)/shard_map/scatter | solution.py:222
  118.4 1.7 %fusion.10 = bf16[8,8,8,128]{3,2,1,0:T(8,128)(2,1)} fusion(bf16[8,8,8,128]{3,2,1,0:T(8,128)(2,1)S(1)} %bitcast.130, f32[8,8,8]{2,1,0:T(8,128)} %get-tuple-element.26, f32[8,8,128]{2,1,0:T(8,128)} %copy.86, f32[8,8,8]{2,1,0:T(8,128)} %get-tuple-element.28, f32[8,8,8]{2,1,0:T(8,128)} %get-tuple-element.27), kind=kLoop, calls=%fused_computation.28 | loop fusion | flops 393216 | bytes 301056 | tf_op jit(solution)/shard_map/convert_element_type | solution.py:53
  120.2 1.0 constant_dynamic-update-slice_fusion
  121.2 1.0 copy-done.2
  (115 shorter events, 23.0 us)
Async XLA Ops:
  0.6 33.2 %copy-start = (bf16[128,64,128]{2,1,0:T(8,128)(2,1)S(1)}, bf16[128,64,128]{2,1,0:T(8,128)(2,1)}, u32[]{:S(2)}) copy-start(bf16[128,64,128]{2,1,0:T(8,128)(2,1)} %param.14) | copy-start | bytes 6291460
  0.6 1.7 %copy-start.13 = (bf16[256,256]{1,0:T(8,128)(2,1)S(1)}, bf16[256,256]{1,0:T(8,128)(2,1)}, u32[]{:S(2)}) copy-start(bf16[256,256]{1,0:T(8,128)(2,1)} %param.11) | copy-start | bytes 393220
  0.7 1.7 %copy-start.15 = (bf16[256,128]{1,0:T(8,128)(2,1)S(1)}, bf16[256,128]{1,0:T(8,128)(2,1)}, u32[]{:S(2)}) copy-start(bf16[256,128]{1,0:T(8,128)(2,1)} %param.12) | copy-start | bytes 196612
  0.7 1.6 %copy-start.4 = (bf16[256,8,128]{2,1,0:T(8,128)(2,1)S(1)}, bf16[256,8,128]{2,1,0:T(8,128)(2,1)}, u32[]{:S(2)}) copy-start(bf16[256,8,128]{2,1,0:T(8,128)(2,1)} %param.13) | copy-start | bytes 1572868
  2.7 0.9 copy-start.8
  6.3 12.4 %copy-start.1 = (s32[8,32]{1,0:T(8,128)S(1)}, s32[8,32]{1,0:T(8,128)}, u32[]{:S(2)}) copy-start(s32[8,32]{1,0:T(8,128)} %param.19) | copy-start | bytes 3076
  7.7 29.6 %all-to-all-start = ((f32[32,8,256]{2,1,0:T(8,128)}), f32[32,8,256]{2,1,0:T(8,128)}, u32[]{:S(2)}, u32[]{:S(2)}) async-start(f32[32,8,256]{2,1,0:T(8,128)} %copy.77), calls=%async_computation | async-start | bytes 524288 | tf_op jit(solution)/shard_map/all_to_all | solution.py:105
  20.6 1.5 %copy-start.12 = (s32[8]{0:T(128)S(1)}, s32[8]{0:T(128)}, u32[]{:S(2)}) copy-start(s32[8]{0:T(128)} %param.18) | copy-start | bytes 100
  20.6 2.5 %copy-start.14 = (bf16[8,8192]{1,0:T(8,128)(2,1)S(1)}, bf16[8,8192]{1,0:T(8,128)(2,1)}, u32[]{:S(2)}) copy-start(bf16[8,8192]{1,0:T(8,128)(2,1)} %param.16) | copy-start | bytes 393220
  22.1 1.0 copy-start.3
  23.1 4.5 %copy-start.11 = (s32[32,1]{0,1:T(1,128)S(1)}, s32[32,1]{0,1:T(1,128)}, u32[]{:S(2)}) copy-start(s32[32,1]{0,1:T(1,128)} %param.21) | copy-start | bytes 388
  30.9 4.4 %copy-start.6 = (s32[8]{0:T(128)}, s32[8]{0:T(128)S(1)}, u32[]{:S(2)}) copy-start(s32[8]{0:T(128)S(1)} %gather_fusion) | copy-start | bytes 100
  35.3 18.4 %copy-start.9 = (bf16[48]{0:T(256)(128)(2,1)}, bf16[48]{0:T(256)(128)(2,1)S(1)}, u32[]{:S(2)}) copy-start(bf16[48]{0:T(256)(128)(2,1)S(1)} %pad.17.clone) | copy-start | bytes 292
  36.0 0.6 copy-start.10
  41.1 25.6 %all-to-all-start.1 = ((bf16[16,48,128]{2,1,0:T(8,128)(2,1)}), bf16[16,48,128]{2,1,0:T(8,128)(2,1)}, u32[]{:S(2)}, u32[]{:S(2)}) async-start(bf16[16,48,128]{2,1,0:T(8,128)(2,1)} %maximum_maximum_fusion), calls=%async_computation.1 | async-start | bytes 393216 | tf_op jit(solution)/shard_map/all_to_all | solution.py:153
  73.5 21.0 %all-to-all-start.2 = ((bf16[16,48,128]{2,1,0:T(8,128)(2,1)}), bf16[16,48,128]{2,1,0:T(8,128)(2,1)}, u32[]{:S(2)}, u32[]{:S(2)}) async-start(bf16[16,48,128]{2,1,0:T(8,128)(2,1)} %broadcast_in_dim.87), calls=%async_computation.2 | async-start | bytes 393216 | tf_op jit(solution)/shard_map/all_to_all | solution.py:195
  83.5 1.0 copy-start.7
  95.3 19.5 %copy-start.5 = (bf16[8,2,8,128]{3,2,1,0:T(8,128)(2,1)S(1)}, bf16[8,2,8,128]{3,2,1,0:T(8,128)(2,1)}, u32[]{:S(2)}) copy-start(bf16[8,2,8,128]{3,2,1,0:T(8,128)(2,1)} %gather_fusion.7) | copy-start | bytes 98308
  98.5 21.6 %all-to-all-start.3 = ((bf16[32,2,1,2,8,128]{5,4,3,1,2,0:T(8,128)(2,1)}), bf16[32,2,1,2,8,128]{5,4,3,1,2,0:T(8,128)(2,1)}, u32[]{:S(2)}, u32[]{:S(2)}) async-start(bf16[32,2,1,2,8,128]{5,4,3,1,2,0:T(8,128)(2,1)} %select_select_fusion), calls=%async_computation.3 | async-start | bytes 524288 | tf_op jit(solution)/shard_map/all_to_all | solution.py:243
  121.1 1.1 copy-start.2

commit v9 on v7

--- a/solution.py
+++ b/solution.py
@@ -79,10 +79,8 @@
     base_part = products[:, :, :column_span]
     down_all = products[:, :, column_span:].reshape(homes, rows, local_adapters, rank_width)
     local_choice = (selected_adapter - group_index * local_adapters).reshape(homes, rows)
-    picker = (
-        local_choice[:, :, None] == jnp.arange(local_adapters, dtype=jnp.int32)[None, None, :]
-    ).astype(jnp.float32)
-    mid_part = jnp.einsum("hia,hiaw->hiw", picker, down_all)
+    picker = local_choice[:, :, None] == jnp.arange(local_adapters, dtype=jnp.int32)[None, None, :]
+    mid_part = jnp.sum(jnp.where(picker[..., None], down_all, 0.0), axis=2)
     partial = jnp.concatenate([base_part, mid_part], axis=2)
     resident_adapters = lax.dynamic_slice_in_dim(selected_adapter, home_index * rows, rows)
     up_weight_rows = adapter_up_weight[resident_adapters]

time: 120 us -> 121 us (level)
  no operation moved by 1% of the time
where the time goes in v9:
time: 121 us; the launch traced here: 119 us
  starting transfers between devices  43.9 us (36%)
  local copies, waits for them, and re-layouts  27.1 us (22%)
  waiting for transfers between devices  24.2 us (20%)
  other arithmetic  19.2 us (16%)
  matrix products  3.93 us (3%)
    all_to_all x1, starting transfers between devices, shards(): received = lax.all_to_all(parcel, 'grp', 0, 0, tiled=False)  12.6 us
    all_to_all x1, starting transfers between devices, shards(): lax.all_to_all(outbound, 'req', split_axis=0, concat_axis=0, tiled=True)  11.9 us
    all_to_all x1, waiting for transfers between devices, shards(): received = lax.all_to_all(parcel, 'grp', 0, 0, tiled=False)  11.4 us
    all_to_all x1, starting transfers between devices, shards(): lax.all_to_all(partial, 'req', 0, 0, tiled=False)  11 us
    all_to_all x1, starting transfers between devices, shards(): lax.all_to_all(jnp.broadcast_to(merged[None], (groups,) + merged.shape),...  8.44 us
    all_to_all x1, waiting for transfers between devices, shards(): lax.all_to_all(jnp.broadcast_to(merged[None], (groups,) + merged.shape),...  8.35 us
    all_to_all x1, waiting for transfers between devices, shards(): lax.all_to_all(outbound, 'req', split_axis=0, concat_axis=0, tiled=True)  4.42 us
    unnamed x27, local copies, waits for them, and re-layouts  4.21 us
  transfers between devices with their start and end apart: 4, of which 3 were waited for; matrix products, arithmetic and copies ran while one was open for 18% of the time, Pallas kernels for 0%

profile of v9, /device:TPU:1, one launch (start us, length us, event | category | flops | bytes accessed | tf_op | source)
XLA Modules:
  0.0 119.4 jit_solution(8767508988931519465)
XLA Ops:
  0.7 1.5 %copy.119 = bf16[320,1,2,8,128]{4,3,2,1,0:T(8,128)(2,1)S(1)} copy(bf16[320,1,2,8,128]{4,3,2,1,0:T(8,128)(2,1)} %param.17) | data formatting | bytes 2621440
  2.8 1.1 slice.129
  5.5 1.4 %copy.89 = f32[32,8,8,128]{3,2,1,0:T(8,128)S(1)} copy(f32[32,8,8,128]{3,1,2,0:T(8,128)} %bitcast.117) | data formatting | bytes 2097152
  7.4 0.9 copy.72
  8.3 11.0 %all-to-all-start = ((f32[32,8,256]{2,1,0:T(8,128)}), f32[32,8,256]{2,1,0:T(8,128)}, u32[]{:S(2)}, u32[]{:S(2)}) async-start(f32[32,8,256]{2,1,0:T(8,128)} %copy.72), calls=%async_computation | async-start | bytes 524288 | tf_op jit(solution)/shard_map/all_to_all | solution.py:88
  19.5 1.8 %gather_fusion.1 = bf16[256,2,8,128]{3,2,1,0:T(8,128)(2,1)} fusion(bf16[320,2,8,128]{3,2,1,0:T(8,128)(2,1)S(1)} %bitcast.113, s32[1024]{0:T(1024)S(1)} %pad_clamp_fusion.2), kind=kCustom, calls=%fused_computation.1 | custom fusion | bytes 2098176 | tf_op jit(solution)/shard_map/gather | solution.py:97
  21.2 1.5 %copy.67 = bf16[256,2,8,128]{3,0,2,1:T(8,128)(2,1)S(1)} copy(bf16[256,2,8,128]{3,2,1,0:T(8,128)(2,1)} %gather_fusion.1) | data formatting | bytes 2097152 | tf_op jit(solution)/shard_map/gather | solution.py:97
  23.2 1.0 fusion.2
  24.6 1.1 gather_fusion
  26.1 0.9 copy.69
  27.7 1.2 shift-left_bitcast_fusion
  29.5 1.3 %gather_fusion.2 = bf16[8,64,128]{2,1,0:T(8,128)(2,1)} fusion(bf16[128,64,128]{2,1,0:T(8,128)(2,1)S(1)} %copy-done, s32[1024]{0:T(1024)} %pad_clamp_fusion.1), kind=kCustom, calls=%fused_computation.2 | custom fusion | bytes 262176 | tf_op jit(solution)/shard_map/gather | solution.py:86
  30.9 1.6 %reduce_sum.67 = f32[8,256]{1,0:T(8,128)} reduce(f32[32,8,256]{2,1,0:T(8,128)} %all-to-all-done, f32[]{:T(128)} %constant.100.clone.1), dimensions={0}, to_apply=%region_4.5 | reduce | flops 63488 | bytes 270340 | tf_op jit(solution)/shard_map/reduce_sum | solution.py:90
  33.1 1.5 %maximum_maximum_fusion = bf16[16,48,128]{2,1,0:T(8,128)(2,1)} fusion(bf16[16,2,128]{2,1,0:T(2,128)(2,1)S(1)} %reshape.354, bf16[16,8,128]{2,1,0:T(8,128)(2,1)S(1)} %broadcast_in_dim.129, bf16[16,32,128]{2,1,0:T(8,128)(2,1)S(1)} %bitcast.125, bf16[48]{0:T(256)(128)(2,1)} %pad.17.clone), kind=kLoop, calls=%fused_computation.26 | loop fusion | flops 786432 | bytes 368736 | tf_op jit(solution)/shard_map/concatenate | solution.py:127
  34.6 12.6 %all-to-all-start.1 = ((bf16[16,48,128]{2,1,0:T(8,128)(2,1)}), bf16[16,48,128]{2,1,0:T(8,128)(2,1)}, u32[]{:S(2)}, u32[]{:S(2)}) async-start(bf16[16,48,128]{2,1,0:T(8,128)(2,1)} %maximum_maximum_fusion), calls=%async_computation.1 | async-start | bytes 393216 | tf_op jit(solution)/shard_map/all_to_all | solution.py:136
  47.2 0.9 convert_reduce_fusion
  48.8 11.4 %all-to-all-done.1 = bf16[16,48,128]{2,1,0:T(8,128)(2,1)} async-done(((bf16[16,48,128]{2,1,0:T(8,128)(2,1)}), bf16[16,48,128]{2,1,0:T(8,128)(2,1)}, u32[]{:S(2)}, u32[]{:S(2)}) %all-to-all-start.1) | async-done | bytes 196640 | tf_op jit(solution)/shard_map/all_to_all | solution.py:136
  62.7 1.0 fusion.27
  64.5 1.0 multiply_reduce_fusion
  67.0 8.4 %all-to-all-start.2 = ((bf16[16,48,128]{2,1,0:T(8,128)(2,1)}), bf16[16,48,128]{2,1,0:T(8,128)(2,1)}, u32[]{:S(2)}, u32[]{:S(2)}) async-start(bf16[16,48,128]{2,1,0:T(8,128)(2,1)} %broadcast_in_dim.132), calls=%async_computation.2 | async-start | bytes 393216 | tf_op jit(solution)/shard_map/all_to_all | solution.py:178
  78.4 1.2 %fusion.35 = pred[8]{0:T(512)(128)(4,1)} fusion(s32[]{:T(128)S(6)} %axis_index.22, s32[8]{0:T(128)} %param.18), kind=kLoop, calls=%fused_computation.116 | loop fusion | flops 96 | bytes 44 | tf_op jit(solution)/shard_map/eq | solution.py:210
  79.7 8.4 %all-to-all-done.2 = bf16[16,48,128]{2,1,0:T(8,128)(2,1)} async-done(((bf16[16,48,128]{2,1,0:T(8,128)(2,1)}), bf16[16,48,128]{2,1,0:T(8,128)(2,1)}, u32[]{:S(2)}, u32[]{:S(2)}) %all-to-all-start.2) | async-done | bytes 196640 | tf_op jit(solution)/shard_map/all_to_all | solution.py:178
  89.9 0.9 slice.143
  92.3 1.0 scatter_fusion
  93.3 1.4 %gather_fusion.5 = bf16[64,2,8,128]{3,2,1,0:T(8,128)(2,1)} fusion(bf16[320,2,8,128]{3,2,1,0:T(8,128)(2,1)S(1)} %scatter_fusion, s32[1024]{0:T(1024)} %pad_clamp_fusion), kind=kCustom, calls=%fused_computation.5 | custom fusion | bytes 524544 | tf_op jit(solution)/shard_map/gather | solution.py:220
  94.7 1.8 %broadcast_select_fusion = bf16[32,2,1,2,8,128]{5,4,3,1,2,0:T(8,128)(2,1)} fusion(bf16[32,2,1,2,8,128]{5,4,3,1,2,0:T(8,128)(2,1)} %bitcast.121, pred[32,2]{1,0:T(8,128)(4,1)} %copy.66), kind=kLoop, calls=%fused_computation.24 | loop fusion | flops 131072 | bytes 524352 | tf_op jit(solution)/shard_map/jit(_where)/select_n | solution.py:218
  96.5 11.9 %all-to-all-start.3 = ((bf16[32,2,1,2,8,128]{5,4,3,1,2,0:T(8,128)(2,1)}), bf16[32,2,1,2,8,128]{5,4,3,1,2,0:T(8,128)(2,1)}, u32[]{:S(2)}, u32[]{:S(2)}) async-start(bf16[32,2,1,2,8,128]{5,4,3,1,2,0:T(8,128)(2,1)} %broadcast_select_fusion), calls=%async_computation.3 | async-start | bytes 524288 | tf_op jit(solution)/shard_map/all_to_all | solution.py:224
  108.4 1.1 fusion.10
  111.0 1.9 %divide_convert_fusion = bf16[8,8,8,128]{3,2,1,0:T(8,128)(2,1)} fusion(f32[8,8,8,128]{3,2,1,0:T(8,128)} %convert.32, f32[8,8,8]{2,1,0:T(8,128)S(1)} %get-tuple-element.28, f32[8,8,128]{2,1,0:T(8,128)S(1)} %copy.79, f32[8,8,8]{2,1,0:T(8,128)S(1)} %get-tuple-element.30, f32[8,8,8]{2,1,0:T(8,128)S(1)} %get-tuple-element.29), kind=kLoop, calls=%fused_computation.21 | loop fusion | flops 327680 | bytes 432128 | tf_op jit(solution)/shard_map/convert_element_type | solution.py:38
  112.9 4.4 %all-to-all-done.3 = bf16[32,2,1,2,8,128]{5,4,3,1,2,0:T(8,128)(2,1)} async-done(((bf16[32,2,1,2,8,128]{5,4,3,1,2,0:T(8,128)(2,1)}), bf16[32,2,1,2,8,128]{5,4,3,1,2,0:T(8,128)(2,1)}, u32[]{:S(2)}, u32[]{:S(2)}) %all-to-all-start.3) | async-done | bytes 262176 | tf_op jit(solution)/shard_map/all_to_all | solution.py:224
  117.3 1.0 constant_dynamic-update-slice_fusion
  118.3 1.0 copy-done.2
  (91 shorter events, 19.1 us)
Async XLA Ops:
  0.6 28.9 %copy-start = (bf16[128,64,128]{2,1,0:T(8,128)(2,1)S(1)}, bf16[128,64,128]{2,1,0:T(8,128)(2,1)}, u32[]{:S(2)}) copy-start(bf16[128,64,128]{2,1,0:T(8,128)(2,1)} %param.14) | copy-start | bytes 6291460
  0.6 1.7 %copy-start.8 = (bf16[256,256]{1,0:T(8,128)(2,1)S(1)}, bf16[256,256]{1,0:T(8,128)(2,1)}, u32[]{:S(2)}) copy-start(bf16[256,256]{1,0:T(8,128)(2,1)} %param.11) | copy-start | bytes 393220
  0.7 1.7 %copy-start.10 = (bf16[256,128]{1,0:T(8,128)(2,1)S(1)}, bf16[256,128]{1,0:T(8,128)(2,1)}, u32[]{:S(2)}) copy-start(bf16[256,128]{1,0:T(8,128)(2,1)} %param.12) | copy-start | bytes 196612
  0.7 1.6 %copy-start.3 = (bf16[256,8,128]{2,1,0:T(8,128)(2,1)S(1)}, bf16[256,8,128]{2,1,0:T(8,128)(2,1)}, u32[]{:S(2)}) copy-start(bf16[256,8,128]{2,1,0:T(8,128)(2,1)} %param.13) | copy-start | bytes 1572868
  2.7 1.1 copy-start.6
  6.9 12.4 %copy-start.7 = (s32[8]{0:T(128)S(1)}, s32[8]{0:T(128)}, u32[]{:S(2)}) copy-start(s32[8]{0:T(128)} %param.18) | copy-start | bytes 100
  6.9 12.5 %copy-start.1 = (s32[8,32]{1,0:T(8,128)S(1)}, s32[8,32]{1,0:T(8,128)}, u32[]{:S(2)}) copy-start(s32[8,32]{1,0:T(8,128)} %param.19) | copy-start | bytes 3076
  8.3 22.6 %all-to-all-start = ((f32[32,8,256]{2,1,0:T(8,128)}), f32[32,8,256]{2,1,0:T(8,128)}, u32[]{:S(2)}, u32[]{:S(2)}) async-start(f32[32,8,256]{2,1,0:T(8,128)} %copy.72), calls=%async_computation | async-start | bytes 524288 | tf_op jit(solution)/shard_map/all_to_all | solution.py:88
  21.2 1.5 %copy-start.9 = (bf16[8,8192]{1,0:T(8,128)(2,1)S(1)}, bf16[8,8192]{1,0:T(8,128)(2,1)}, u32[]{:S(2)}) copy-start(bf16[8,8192]{1,0:T(8,128)(2,1)} %param.16) | copy-start | bytes 393220
  34.6 25.6 %all-to-all-start.1 = ((bf16[16,48,128]{2,1,0:T(8,128)(2,1)}), bf16[16,48,128]{2,1,0:T(8,128)(2,1)}, u32[]{:S(2)}, u32[]{:S(2)}) async-start(bf16[16,48,128]{2,1,0:T(8,128)(2,1)} %maximum_maximum_fusion), calls=%async_computation.1 | async-start | bytes 393216 | tf_op jit(solution)/shard_map/all_to_all | solution.py:136
  67.0 21.0 %all-to-all-start.2 = ((bf16[16,48,128]{2,1,0:T(8,128)(2,1)}), bf16[16,48,128]{2,1,0:T(8,128)(2,1)}, u32[]{:S(2)}, u32[]{:S(2)}) async-start(bf16[16,48,128]{2,1,0:T(8,128)(2,1)} %broadcast_in_dim.132), calls=%async_computation.2 | async-start | bytes 393216 | tf_op jit(solution)/shard_map/all_to_all | solution.py:178
  89.9 2.4 %copy-start.4 = (bf16[8,8,128]{2,0,1:T(8,128)(2,1)}, bf16[8,8,128]{2,0,1:T(8,128)(2,1)S(1)}, u32[]{:S(2)}) copy-start(bf16[8,8,128]{2,0,1:T(8,128)(2,1)S(1)} %copy.115) | copy-start | bytes 49156
  92.3 16.1 %copy-start.5 = (bf16[8,8,128]{2,0,1:T(8,128)(2,1)S(1)}, bf16[8,8,128]{2,0,1:T(8,128)(2,1)}, u32[]{:S(2)}) copy-start(bf16[8,8,128]{2,0,1:T(8,128)(2,1)} %copy-done.4) | copy-start | bytes 49156
  96.5 20.8 %all-to-all-start.3 = ((bf16[32,2,1,2,8,128]{5,4,3,1,2,0:T(8,128)(2,1)}), bf16[32,2,1,2,8,128]{5,4,3,1,2,0:T(8,128)(2,1)}, u32[]{:S(2)}, u32[]{:S(2)}) async-start(bf16[32,2,1,2,8,128]{5,4,3,1,2,0:T(8,128)(2,1)} %broadcast_select_fusion), calls=%async_computation.3 | async-start | bytes 524288 | tf_op jit(solution)/shard_map/all_to_all | solution.py:224
  118.3 1.1 copy-start.2

commit v10 on v9

--- a/solution.py
+++ b/solution.py
@@ -52,6 +52,7 @@
     departing_target,
 ):
     selected_adapter = adapter_index_rows[:, 0]
+    request_index = jnp.arange(lengths.shape[0], dtype=jnp.int32)
     homes = lax.axis_size("req")
     groups = lax.axis_size("grp")
     home_index = lax.axis_index("req")
@@ -84,32 +85,36 @@
     partial = jnp.concatenate([base_part, mid_part], axis=2)
     resident_adapters = lax.dynamic_slice_in_dim(selected_adapter, home_index * rows, rows)
     up_weight_rows = adapter_up_weight[resident_adapters]
-    summed, up_weight_rows = lax.optimization_barrier(
-        (lax.all_to_all(partial, "req", 0, 0, tiled=False), up_weight_rows)
-    )
-    summed = jnp.sum(summed, axis=0)
+    summed = jnp.sum(lax.all_to_all(partial, "req", 0, 0, tiled=False), axis=0)
     base_resident = summed[:, :column_span]
 
     owner = resident_adapters // local_adapters
-    request_index = jnp.arange(rows, dtype=jnp.int32)
     is_value = group_index * column_span >= key_width
 
-    gathered = key_value_pages[page_slot_table][:, :, 0]
-    keys = gathered[:, :, 0]
-    values = gathered[:, :, 1]
+    live_slots = rows * pages
+    live = key_value_pages[:live_slots, 0]
+    keys = live[:, 0]
+    values = live[:, 1]
     query = queries.reshape(rows, heads, -1, head_dim)
     group_size = query.shape[2]
+    entry_of_slot = jnp.argmax(
+        page_slot_table.reshape(1, -1) == jnp.arange(live_slots, dtype=jnp.int32)[:, None], axis=1
+    )
+    slot_request = entry_of_slot // pages
+    slot_position = (entry_of_slot % pages) * page_size + group_index * slot_tokens
+    valid = (slot_request[None, :] == request_index[:, None]) & (
+        slot_position[None, :] < lengths[:, None]
+    )
+    valid = valid[None, None]
     scores = jnp.einsum(
-        "ihgd,inhd->hgin", query, keys, preferred_element_type=jnp.float32
+        "ihgd,shd->hgis", query, keys, preferred_element_type=jnp.float32
     ) / math.sqrt(head_dim)
-    positions = jnp.arange(pages, dtype=jnp.int32) * page_size + group_index * slot_tokens
-    valid = (positions[None, :] < lengths[:, None])[None, None]
     scores = jnp.where(valid, scores, masked_score)
     local_top = jnp.max(scores, axis=3)
     weights = jnp.where(valid, jnp.exp(scores - local_top[..., None]), 0.0)
     local_total = jnp.sum(weights, axis=3)
     local_mixed = jnp.einsum(
-        "hgin,inhd->hgid", weights, values, preferred_element_type=jnp.float32
+        "hgis,shd->hgid", weights, values, preferred_element_type=jnp.float32
     )
 
     block_rows = heads_per_target * rows
@@ -133,7 +138,9 @@
         ],
         axis=1,
     )
-    received = lax.all_to_all(parcel, "grp", 0, 0, tiled=False)
+    received, up_weight_rows = lax.optimization_barrier(
+        (lax.all_to_all(parcel, "grp", 0, 0, tiled=False), up_weight_rows)
+    )
     stat_at = block_rows + rows
     shard_mixed = received[:, :block_rows].astype(jnp.float32).reshape(
         groups, heads_per_target, rows, head_dim

time: 121 us -> 120 us (level)
  other arithmetic: 19.2 us -> 24.5 us
  waiting for transfers between devices: 24.2 us -> 20.8 us
  local copies, waits for them, and re-layouts: 27.1 us -> 24.3 us
    gather x2 -> x0, local copies, waits for them, and re-layouts: 3.29 us -> none  [shards(): gathered = key_value_pages[page_slot_table][:, :, 0]]
    all_to_all x2, waiting for transfers between devices: 11.4 us -> 8.62 us  [the longest x1 8.43 us: shards(): lax.all_to_all(parcel, 'grp', 0, 0, tiled=False)]
    reduce_sum x1, other arithmetic: 0.26 us -> 1.93 us  [shards(): local_total = jnp.sum(weights, axis=3)]
    unnamed x27 -> x32, local copies, waits for them, and re-layouts: 4.21 us -> 5.38 us
  transfers between devices with their start and end apart: 4 -> 4, of which waited for: 3 -> 4; matrix products, arithmetic and copies ran while one was open for 18% -> 18% of each run, Pallas kernels for 0% -> 0%
where the time goes in v10:
time: 120 us; the launch traced here: 118 us
  starting transfers between devices  43.7 us (36%)
  other arithmetic  24.5 us (20%)
  local copies, waits for them, and re-layouts  24.3 us (20%)
  waiting for transfers between devices  20.8 us (17%)
  matrix products  4.04 us (3%)
    all_to_all x1, starting transfers between devices, shards(): lax.all_to_all(parcel, 'grp', 0, 0, tiled=False)  12.5 us
    all_to_all x1, starting transfers between devices, shards(): lax.all_to_all(outbound, 'req', split_axis=0, concat_axis=0, tiled=True)  11.8 us
    all_to_all x1, starting transfers between devices, shards(): summed = jnp.sum(lax.all_to_all(partial, 'req', 0, 0, tiled=False), axis=0)  11 us
    all_to_all x1, waiting for transfers between devices, shards(): lax.all_to_all(parcel, 'grp', 0, 0, tiled=False)  8.43 us
    all_to_all x1, starting transfers between devices, shards(): lax.all_to_all(jnp.broadcast_to(merged[None], (groups,) + merged.shape),...  8.41 us
    all_to_all x1, waiting for transfers between devices, shards(): lax.all_to_all(jnp.broadcast_to(merged[None], (groups,) + merged.shape),...  7.72 us
    unnamed x32, local copies, waits for them, and re-layouts  5.38 us
    all_to_all x1, waiting for transfers between devices, shards(): lax.all_to_all(outbound, 'req', split_axis=0, concat_axis=0, tiled=True)  4.42 us
  transfers between devices with their start and end apart: 4, of which 4 were waited for; matrix products, arithmetic and copies ran while one was open for 18% of the time, Pallas kernels for 0%

profile of v10, /device:TPU:1, one launch (start us, length us, event | category | flops | bytes accessed | tf_op | source)
XLA Modules:
  0.0 118.2 jit_solution(7842013429348961292)
XLA Ops:
  0.7 1.5 %copy.127 = bf16[320,1,2,8,128]{4,3,2,1,0:T(8,128)(2,1)S(1)} copy(bf16[320,1,2,8,128]{4,3,2,1,0:T(8,128)(2,1)} %param.17) | data formatting | bytes 2621440
  2.8 1.1 slice.131
  5.5 1.4 %copy.93 = f32[32,8,8,128]{3,2,1,0:T(8,128)S(1)} copy(f32[32,8,8,128]{3,1,2,0:T(8,128)} %bitcast.124) | data formatting | bytes 2097152
  7.4 0.9 copy.73
  8.3 11.0 %all-to-all-start = ((f32[32,8,256]{2,1,0:T(8,128)}), f32[32,8,256]{2,1,0:T(8,128)}, u32[]{:S(2)}, u32[]{:S(2)}) async-start(f32[32,8,256]{2,1,0:T(8,128)} %copy.73), calls=%async_computation | async-start | bytes 524288 | tf_op jit(solution)/shard_map/all_to_all | solution.py:88
  20.6 0.9 copy-done.3
  21.5 1.1 fusion.53
  22.7 1.9 %fusion.48 = (f32[8,8,8]{1,2,0:T(8,128)S(1)}, bf16[8,8,8,256]{3,1,2,0:T(8,128)(2,1)}) fusion(f32[8,8,8,256]{3,1,2,0:T(8,128)} %get-tuple-element.59, f32[8,8,8]{1,2,0:T(8,128)S(1)} %get-tuple-element.58, pred[8,256]{1,0:T(8,128)(4,1)S(1)} %fusion.22), kind=kLoop, calls=%fused_computation.141 | loop fusion | flops 523776 | bytes 792576 | tf_op jit(solution)/shard_map/reduce_sum | solution.py:115
  25.0 1.1 gather_fusion
  26.8 1.3 %convolution_convert_fusion = bf16[8,8,8,128]{3,2,1,0:T(8,128)(2,1)S(1)} fusion(bf16[256,2,8,128]{3,0,2,1:T(8,128)(2,1)} %bitcast.127, bf16[8,8,8,256]{3,1,2,0:T(8,128)(2,1)} %get-tuple-element.38), kind=kOutput, calls=%fused_computation.10 | convolution fusion | flops 33554432 | bytes 917504 | tf_op jit(solution)/shard_map/hgis,shd->hgid/dot_general | solution.py:116
  28.3 1.0 reduce_sum.67
  29.3 1.4 %maximum_maximum_fusion = bf16[16,48,128]{2,1,0:T(8,128)(2,1)} fusion(bf16[16,2,128]{2,1,0:T(2,128)(2,1)S(1)} %reshape.374, bf16[16,8,128]{2,1,0:T(8,128)(2,1)S(1)} %broadcast_in_dim.80, bf16[16,32,128]{2,1,0:T(8,128)(2,1)S(1)} %bitcast.133, bf16[48]{0:T(256)(128)(2,1)} %pad.17.clone), kind=kLoop, calls=%fused_computation.27 | loop fusion | flops 786432 | bytes 368736 | tf_op jit(solution)/shard_map/concatenate | solution.py:132
  30.7 12.5 %all-to-all-start.1 = ((bf16[16,48,128]{2,1,0:T(8,128)(2,1)}), bf16[16,48,128]{2,1,0:T(8,128)(2,1)}, u32[]{:S(2)}, u32[]{:S(2)}) async-start(bf16[16,48,128]{2,1,0:T(8,128)(2,1)} %maximum_maximum_fusion), calls=%async_computation.1 | async-start | bytes 393216 | tf_op jit(solution)/shard_map/all_to_all | solution.py:142
  43.2 1.2 %shift-left_bitcast_fusion = (s32[8]{0:T(128)S(1)}, s32[8]{0:T(128)}, s32[8]{0:T(128)S(1)}, s32[8]{0:T(128)S(1)}) fusion(s32[8]{0:T(128)} %gather_fusion, s32[256,1]{0,1:T(1,128)} %param.15, s32[]{:T(128)S(6)} %select_n.126), kind=kLoop, calls=%fused_computation.129 | loop fusion | flops 240 | bytes 196 | tf_op jit(solution)/shard_map/concatenate | solution.py:221
  45.7 0.9 convert_reduce_fusion
  47.8 8.4 %all-to-all-done.1 = bf16[16,48,128]{2,1,0:T(8,128)(2,1)} async-done(((bf16[16,48,128]{2,1,0:T(8,128)(2,1)}), bf16[16,48,128]{2,1,0:T(8,128)(2,1)}, u32[]{:S(2)}, u32[]{:S(2)}) %all-to-all-start.1) | async-done | bytes 196640 | tf_op jit(solution)/shard_map/all_to_all | solution.py:142
  57.0 1.4 %slice.102 = bf16[16,8,128]{2,1,0:T(8,128)(2,1)} slice(bf16[16,48,128]{2,1,0:T(8,128)(2,1)} %all-to-all-done.1), slice={[0:16], [32:40], [0:128]} | slice | bytes 65536 | tf_op jit(solution)/shard_map/slice | solution.py:154
  59.8 1.6 %multiply_reduce_fusion = bf16[32,128]{1,0:T(8,128)(2,1)} fusion(f32[16,32]{1,0:T(8,128)S(1)} %get-tuple-element.36, bf16[16,48,128]{2,1,0:T(8,128)(2,1)} %all-to-all-done.1), kind=kLoop, calls=%fused_computation.23 | loop fusion | flops 192512 | bytes 141312 | tf_op jit(solution)/shard_map/reduce_sum | solution.py:158
  61.5 1.3 %gather_fusion.2 = bf16[8,128]{1,0:T(8,128)(2,1)S(1)} fusion(bf16[16,8,128]{2,1,0:T(8,128)(2,1)} %slice.102, s32[8]{0:T(128)S(1)} %get-tuple-element.61), kind=kCustom, calls=%fused_computation.2 | custom fusion | bytes 4160 | tf_op jit(solution)/shard_map/gather | solution.py:160
  66.0 8.4 %all-to-all-start.2 = ((bf16[16,48,128]{2,1,0:T(8,128)(2,1)}), bf16[16,48,128]{2,1,0:T(8,128)(2,1)}, u32[]{:S(2)}, u32[]{:S(2)}) async-start(bf16[16,48,128]{2,1,0:T(8,128)(2,1)} %broadcast_in_dim.128), calls=%async_computation.2 | async-start | bytes 393216 | tf_op jit(solution)/shard_map/all_to_all | solution.py:185
  78.0 1.2 %fusion.34 = pred[8]{0:T(512)(128)(4,1)} fusion(s32[]{:T(128)S(6)} %axis_index.22, s32[8]{0:T(128)} %param.18), kind=kLoop, calls=%fused_computation.120 | loop fusion | flops 96 | bytes 44 | tf_op jit(solution)/shard_map/eq | solution.py:217
  79.2 7.7 %all-to-all-done.2 = bf16[16,48,128]{2,1,0:T(8,128)(2,1)} async-done(((bf16[16,48,128]{2,1,0:T(8,128)(2,1)}), bf16[16,48,128]{2,1,0:T(8,128)(2,1)}, u32[]{:S(2)}, u32[]{:S(2)}) %all-to-all-start.2) | async-done | bytes 196640 | tf_op jit(solution)/shard_map/all_to_all | solution.py:185
  88.8 0.9 slice.142
  91.2 1.0 scatter_fusion
  92.2 1.4 %gather_fusion.4 = bf16[64,2,8,128]{3,2,1,0:T(8,128)(2,1)} fusion(bf16[320,2,8,128]{3,2,1,0:T(8,128)(2,1)S(1)} %scatter_fusion, s32[1024]{0:T(1024)} %pad_clamp_fusion), kind=kCustom, calls=%fused_computation.4 | custom fusion | bytes 524544 | tf_op jit(solution)/shard_map/gather | solution.py:227
  93.6 1.8 %broadcast_select_fusion = bf16[32,2,1,2,8,128]{5,4,3,1,2,0:T(8,128)(2,1)} fusion(bf16[32,2,1,2,8,128]{5,4,3,1,2,0:T(8,128)(2,1)} %bitcast.128, pred[32,2]{1,0:T(8,128)(4,1)} %copy.67), kind=kLoop, calls=%fused_computation.26 | loop fusion | flops 131072 | bytes 524352 | tf_op jit(solution)/shard_map/jit(_where)/select_n | solution.py:225
  95.4 11.8 %all-to-all-start.3 = ((bf16[32,2,1,2,8,128]{5,4,3,1,2,0:T(8,128)(2,1)}), bf16[32,2,1,2,8,128]{5,4,3,1,2,0:T(8,128)(2,1)}, u32[]{:S(2)}, u32[]{:S(2)}) async-start(bf16[32,2,1,2,8,128]{5,4,3,1,2,0:T(8,128)(2,1)} %broadcast_select_fusion), calls=%async_computation.3 | async-start | bytes 524288 | tf_op jit(solution)/shard_map/all_to_all | solution.py:231
  107.2 1.1 fusion.7
  109.8 1.9 %divide_convert_fusion = bf16[8,8,8,128]{3,2,1,0:T(8,128)(2,1)} fusion(f32[8,8,8,128]{3,2,1,0:T(8,128)} %convert.32, f32[8,8,8]{2,1,0:T(8,128)S(1)} %get-tuple-element.30, f32[8,8,128]{2,1,0:T(8,128)S(1)} %copy.80, f32[8,8,8]{2,1,0:T(8,128)S(1)} %get-tuple-element.32, f32[8,8,8]{2,1,0:T(8,128)S(1)} %get-tuple-element.31), kind=kLoop, calls=%fused_computation.22 | loop fusion | flops 327680 | bytes 432128 | tf_op jit(solution)/shard_map/convert_element_type | solution.py:38
  111.7 4.4 %all-to-all-done.3 = bf16[32,2,1,2,8,128]{5,4,3,1,2,0:T(8,128)(2,1)} async-done(((bf16[32,2,1,2,8,128]{5,4,3,1,2,0:T(8,128)(2,1)}), bf16[32,2,1,2,8,128]{5,4,3,1,2,0:T(8,128)(2,1)}, u32[]{:S(2)}, u32[]{:S(2)}) %all-to-all-start.3) | async-done | bytes 262176 | tf_op jit(solution)/shard_map/all_to_all | solution.py:231
  116.1 1.0 constant_dynamic-update-slice_fusion
  117.1 1.0 copy-done.2
  (93 shorter events, 21.4 us)
Async XLA Ops:
  0.6 44.4 %copy-start = (bf16[128,64,128]{2,1,0:T(8,128)(2,1)S(1)}, bf16[128,64,128]{2,1,0:T(8,128)(2,1)}, u32[]{:S(2)}) copy-start(bf16[128,64,128]{2,1,0:T(8,128)(2,1)} %param.14) | copy-start | bytes 6291460
  0.6 1.7 %copy-start.10 = (bf16[256,256]{1,0:T(8,128)(2,1)S(1)}, bf16[256,256]{1,0:T(8,128)(2,1)}, u32[]{:S(2)}) copy-start(bf16[256,256]{1,0:T(8,128)(2,1)} %param.11) | copy-start | bytes 393220
  0.7 1.7 %copy-start.12 = (bf16[256,128]{1,0:T(8,128)(2,1)S(1)}, bf16[256,128]{1,0:T(8,128)(2,1)}, u32[]{:S(2)}) copy-start(bf16[256,128]{1,0:T(8,128)(2,1)} %param.12) | copy-start | bytes 196612
  0.7 1.6 %copy-start.4 = (bf16[256,8,128]{2,1,0:T(8,128)(2,1)S(1)}, bf16[256,8,128]{2,1,0:T(8,128)(2,1)}, u32[]{:S(2)}) copy-start(bf16[256,8,128]{2,1,0:T(8,128)(2,1)} %param.13) | copy-start | bytes 1572868
  2.7 1.1 copy-start.8
  6.9 12.4 %copy-start.9 = (s32[8]{0:T(128)S(1)}, s32[8]{0:T(128)}, u32[]{:S(2)}) copy-start(s32[8]{0:T(128)} %param.18) | copy-start | bytes 100
  6.9 12.4 %copy-start.1 = (s32[8,32]{1,0:T(8,128)S(1)}, s32[8,32]{1,0:T(8,128)}, u32[]{:S(2)}) copy-start(s32[8,32]{1,0:T(8,128)} %param.19) | copy-start | bytes 3076
  8.3 20.0 %all-to-all-start = ((f32[32,8,256]{2,1,0:T(8,128)}), f32[32,8,256]{2,1,0:T(8,128)}, u32[]{:S(2)}, u32[]{:S(2)}) async-start(f32[32,8,256]{2,1,0:T(8,128)} %copy.73), calls=%async_computation | async-start | bytes 524288 | tf_op jit(solution)/shard_map/all_to_all | solution.py:88
  20.3 1.3 %copy-start.11 = (bf16[8,8192]{1,0:T(8,128)(2,1)S(1)}, bf16[8,8192]{1,0:T(8,128)(2,1)}, u32[]{:S(2)}) copy-start(bf16[8,8192]{1,0:T(8,128)(2,1)} %param.16) | copy-start | bytes 393220
  20.6 1.0 copy-start.3
  29.3 17.3 %copy-start.7 = (f32[8,256]{1,0:T(8,128)}, f32[8,256]{1,0:T(8,128)S(1)}, u32[]{:S(2)}) copy-start(f32[8,256]{1,0:T(8,128)S(1)} %reduce_sum.67) | copy-start | bytes 24580
  30.7 25.6 %all-to-all-start.1 = ((bf16[16,48,128]{2,1,0:T(8,128)(2,1)}), bf16[16,48,128]{2,1,0:T(8,128)(2,1)}, u32[]{:S(2)}, u32[]{:S(2)}) async-start(bf16[16,48,128]{2,1,0:T(8,128)(2,1)} %maximum_maximum_fusion), calls=%async_computation.1 | async-start | bytes 393216 | tf_op jit(solution)/shard_map/all_to_all | solution.py:142
  66.0 21.0 %all-to-all-start.2 = ((bf16[16,48,128]{2,1,0:T(8,128)(2,1)}), bf16[16,48,128]{2,1,0:T(8,128)(2,1)}, u32[]{:S(2)}, u32[]{:S(2)}) async-start(bf16[16,48,128]{2,1,0:T(8,128)(2,1)} %broadcast_in_dim.128), calls=%async_computation.2 | async-start | bytes 393216 | tf_op jit(solution)/shard_map/all_to_all | solution.py:185
  88.8 2.4 %copy-start.5 = (bf16[8,8,128]{2,0,1:T(8,128)(2,1)}, bf16[8,8,128]{2,0,1:T(8,128)(2,1)S(1)}, u32[]{:S(2)}) copy-start(bf16[8,8,128]{2,0,1:T(8,128)(2,1)S(1)} %copy.123) | copy-start | bytes 49156
  91.2 16.0 %copy-start.6 = (bf16[8,8,128]{2,0,1:T(8,128)(2,1)S(1)}, bf16[8,8,128]{2,0,1:T(8,128)(2,1)}, u32[]{:S(2)}) copy-start(bf16[8,8,128]{2,0,1:T(8,128)(2,1)} %copy-done.5) | copy-start | bytes 49156
  95.4 20.7 %all-to-all-start.3 = ((bf16[32,2,1,2,8,128]{5,4,3,1,2,0:T(8,128)(2,1)}), bf16[32,2,1,2,8,128]{5,4,3,1,2,0:T(8,128)(2,1)}, u32[]{:S(2)}, u32[]{:S(2)}) async-start(bf16[32,2,1,2,8,128]{5,4,3,1,2,0:T(8,128)(2,1)} %broadcast_select_fusion), calls=%async_computation.3 | async-start | bytes 524288 | tf_op jit(solution)/shard_map/all_to_all | solution.py:231
  117.1 1.1 copy-start.2

commit v11 on v10

--- a/solution.py
+++ b/solution.py
@@ -222,11 +222,8 @@
         jnp.where(mine[:, None, None, None], fresh, current)
     )
 
-    outbound = jnp.where(
-        filled[:, :, None, None, None, None],
-        written[source_slot],
-        jnp.zeros((), key_value_pages.dtype),
-    )
+    written = written.at[live_slots].set(jnp.zeros((), key_value_pages.dtype))
+    outbound = written[jnp.where(filled, source_slot, live_slots)]
     outbound, attention_parts = lax.optimization_barrier((outbound, attention_parts))
     arrived = lax.all_to_all(outbound, "req", split_axis=0, concat_axis=0, tiled=True)
     attention = finish_attention(*attention_parts)

time: 120 us -> 118 us (0.983)
  other arithmetic: 24.5 us -> 22.6 us
    select_n x2 -> x1, other arithmetic: 1.8 us -> 0.01 us  [shards(): outbound = written[jnp.where(filled, source_slot, live_slots)]]
where the time goes in v11:
time: 118 us; the launch traced here: 116 us
  starting transfers between devices  43.7 us (37%)
  local copies, waits for them, and re-layouts  23.6 us (20%)
  other arithmetic  22.6 us (19%)
  waiting for transfers between devices  21.5 us (18%)
  matrix products  4.04 us (3%)
    all_to_all x1, starting transfers between devices, shards(): lax.all_to_all(parcel, 'grp', 0, 0, tiled=False)  12.5 us
    all_to_all x1, starting transfers between devices, shards(): lax.all_to_all(outbound, 'req', split_axis=0, concat_axis=0, tiled=True)  11.8 us
    all_to_all x1, starting transfers between devices, shards(): summed = jnp.sum(lax.all_to_all(partial, 'req', 0, 0, tiled=False), axis=0)  11 us
    all_to_all x1, waiting for transfers between devices, shards(): lax.all_to_all(parcel, 'grp', 0, 0, tiled=False)  8.45 us
    all_to_all x1, waiting for transfers between devices, shards(): lax.all_to_all(jnp.broadcast_to(merged[None], (groups,) + merged.shape),...  8.44 us
    all_to_all x1, starting transfers between devices, shards(): lax.all_to_all(jnp.broadcast_to(merged[None], (groups,) + merged.shape),...  8.41 us
    unnamed x32, local copies, waits for them, and re-layouts  5.38 us
    all_to_all x1, waiting for transfers between devices, shards(): lax.all_to_all(outbound, 'req', split_axis=0, concat_axis=0, tiled=True)  4.42 us
  transfers between devices with their start and end apart: 4, of which 4 were waited for; matrix products, arithmetic and copies ran while one was open for 18% of the time, Pallas kernels for 0%

profile of v11, /device:TPU:1, one launch (start us, length us, event | category | flops | bytes accessed | tf_op | source)
XLA Modules:
  0.0 116.4 jit_solution(7689627947288524708)
XLA Ops:
  0.7 1.5 %copy.127 = bf16[320,1,2,8,128]{4,3,2,1,0:T(8,128)(2,1)S(1)} copy(bf16[320,1,2,8,128]{4,3,2,1,0:T(8,128)(2,1)} %param.19) | data formatting | bytes 2621440
  2.8 1.1 slice.161
  4.6 0.8 copy.71
  5.5 1.4 %copy.92 = f32[32,8,8,128]{3,2,1,0:T(8,128)S(1)} copy(f32[32,8,8,128]{3,1,2,0:T(8,128)} %bitcast.125) | data formatting | bytes 2097152
  7.4 0.9 copy.72
  8.3 11.0 %all-to-all-start = ((f32[32,8,256]{2,1,0:T(8,128)}), f32[32,8,256]{2,1,0:T(8,128)}, u32[]{:S(2)}, u32[]{:S(2)}) async-start(f32[32,8,256]{2,1,0:T(8,128)} %copy.72), calls=%async_computation | async-start | bytes 524288 | tf_op jit(solution)/shard_map/all_to_all | solution.py:88
  20.6 0.9 copy-done.3
  21.5 1.1 fusion.53
  22.7 1.9 %fusion.48 = (f32[8,8,8]{1,2,0:T(8,128)S(1)}, bf16[8,8,8,256]{3,1,2,0:T(8,128)(2,1)}) fusion(f32[8,8,8,256]{3,1,2,0:T(8,128)} %get-tuple-element.71, f32[8,8,8]{1,2,0:T(8,128)S(1)} %get-tuple-element.70, pred[8,256]{1,0:T(8,128)(4,1)S(1)} %fusion.22), kind=kLoop, calls=%fused_computation.141 | loop fusion | flops 523776 | bytes 792576 | tf_op jit(solution)/shard_map/reduce_sum | solution.py:115
  25.0 1.1 gather_fusion
  26.8 1.3 %convolution_convert_fusion = bf16[8,8,8,128]{3,2,1,0:T(8,128)(2,1)S(1)} fusion(bf16[256,2,8,128]{3,0,2,1:T(8,128)(2,1)} %bitcast.128, bf16[8,8,8,256]{3,1,2,0:T(8,128)(2,1)} %get-tuple-element.50), kind=kOutput, calls=%fused_computation.10 | convolution fusion | flops 33554432 | bytes 917504 | tf_op jit(solution)/shard_map/hgis,shd->hgid/dot_general | solution.py:116
  28.3 1.0 reduce_sum.64
  29.3 1.4 %maximum_maximum_fusion = bf16[16,48,128]{2,1,0:T(8,128)(2,1)} fusion(bf16[16,2,128]{2,1,0:T(2,128)(2,1)S(1)} %reshape.409, bf16[16,8,128]{2,1,0:T(8,128)(2,1)S(1)} %broadcast_in_dim.70, bf16[16,32,128]{2,1,0:T(8,128)(2,1)S(1)} %bitcast.134, bf16[48]{0:T(256)(128)(2,1)} %pad.19.clone), kind=kLoop, calls=%fused_computation.26 | loop fusion | flops 786432 | bytes 368736 | tf_op jit(solution)/shard_map/concatenate | solution.py:132
  30.7 12.5 %all-to-all-start.1 = ((bf16[16,48,128]{2,1,0:T(8,128)(2,1)}), bf16[16,48,128]{2,1,0:T(8,128)(2,1)}, u32[]{:S(2)}, u32[]{:S(2)}) async-start(bf16[16,48,128]{2,1,0:T(8,128)(2,1)} %maximum_maximum_fusion), calls=%async_computation.1 | async-start | bytes 393216 | tf_op jit(solution)/shard_map/all_to_all | solution.py:142
  43.2 1.2 %shift-left_bitcast_fusion = (s32[8]{0:T(128)S(1)}, s32[8]{0:T(128)}, s32[8]{0:T(128)S(1)}, s32[8]{0:T(128)S(1)}) fusion(s32[8]{0:T(128)} %gather_fusion, s32[256,1]{0,1:T(1,128)} %param.17, s32[]{:T(128)S(6)} %select_n.128), kind=kLoop, calls=%fused_computation.131 | loop fusion | flops 240 | bytes 196 | tf_op jit(solution)/shard_map/concatenate | solution.py:221
  45.7 0.9 convert_reduce_fusion
  47.8 8.4 %all-to-all-done.1 = bf16[16,48,128]{2,1,0:T(8,128)(2,1)} async-done(((bf16[16,48,128]{2,1,0:T(8,128)(2,1)}), bf16[16,48,128]{2,1,0:T(8,128)(2,1)}, u32[]{:S(2)}, u32[]{:S(2)}) %all-to-all-start.1) | async-done | bytes 196640 | tf_op jit(solution)/shard_map/all_to_all | solution.py:142
  57.1 1.4 %slice.132 = bf16[16,8,128]{2,1,0:T(8,128)(2,1)} slice(bf16[16,48,128]{2,1,0:T(8,128)(2,1)} %all-to-all-done.1), slice={[0:16], [32:40], [0:128]} | slice | bytes 65536 | tf_op jit(solution)/shard_map/slice | solution.py:154
  59.8 1.6 %multiply_reduce_fusion = bf16[32,128]{1,0:T(8,128)(2,1)} fusion(f32[16,32]{1,0:T(8,128)S(1)} %get-tuple-element.48, bf16[16,48,128]{2,1,0:T(8,128)(2,1)} %all-to-all-done.1), kind=kLoop, calls=%fused_computation.23 | loop fusion | flops 192512 | bytes 141312 | tf_op jit(solution)/shard_map/reduce_sum | solution.py:158
  61.5 1.3 %gather_fusion.2 = bf16[8,128]{1,0:T(8,128)(2,1)S(1)} fusion(bf16[16,8,128]{2,1,0:T(8,128)(2,1)} %slice.132, s32[8]{0:T(128)S(1)} %get-tuple-element.73), kind=kCustom, calls=%fused_computation.2 | custom fusion | bytes 4160 | tf_op jit(solution)/shard_map/gather | solution.py:160
  66.0 8.4 %all-to-all-start.2 = ((bf16[16,48,128]{2,1,0:T(8,128)(2,1)}), bf16[16,48,128]{2,1,0:T(8,128)(2,1)}, u32[]{:S(2)}, u32[]{:S(2)}) async-start(bf16[16,48,128]{2,1,0:T(8,128)(2,1)} %broadcast_in_dim.74), calls=%async_computation.2 | async-start | bytes 393216 | tf_op jit(solution)/shard_map/all_to_all | solution.py:185
  77.3 1.2 %fusion.34 = pred[8]{0:T(512)(128)(4,1)} fusion(s32[]{:T(128)S(6)} %axis_index.22, s32[8]{0:T(128)} %param.20), kind=kLoop, calls=%fused_computation.122 | loop fusion | flops 96 | bytes 44 | tf_op jit(solution)/shard_map/eq | solution.py:217
  78.5 8.4 %all-to-all-done.2 = bf16[16,48,128]{2,1,0:T(8,128)(2,1)} async-done(((bf16[16,48,128]{2,1,0:T(8,128)(2,1)}), bf16[16,48,128]{2,1,0:T(8,128)(2,1)}, u32[]{:S(2)}, u32[]{:S(2)}) %all-to-all-start.2) | async-done | bytes 196640 | tf_op jit(solution)/shard_map/all_to_all | solution.py:185
  89.5 1.0 scatter_fusion
  90.5 0.9 slice.172
  92.2 1.4 %gather_fusion.4 = bf16[64,2,8,128]{3,2,1,0:T(8,128)(2,1)} fusion(bf16[320,2,8,128]{3,2,1,0:T(8,128)(2,1)S(1)} %bitcast.123, s32[1024]{0:T(1024)} %pad_clamp_fusion), kind=kCustom, calls=%fused_computation.4 | custom fusion | bytes 524544 | tf_op jit(solution)/shard_map/gather | solution.py:226
  93.6 11.8 %all-to-all-start.3 = ((bf16[32,2,1,2,8,128]{5,4,3,1,2,0:T(8,128)(2,1)}), bf16[32,2,1,2,8,128]{5,4,3,1,2,0:T(8,128)(2,1)}, u32[]{:S(2)}, u32[]{:S(2)}) async-start(bf16[32,2,1,2,8,128]{5,4,3,1,2,0:T(8,128)(2,1)} %bitcast.129), calls=%async_computation.3 | async-start | bytes 524288 | tf_op jit(solution)/shard_map/all_to_all | solution.py:228
  105.5 1.1 fusion.7
  108.1 1.9 %divide_convert_fusion = bf16[8,8,8,128]{3,2,1,0:T(8,128)(2,1)} fusion(f32[8,8,8,128]{3,2,1,0:T(8,128)} %convert.32, f32[8,8,8]{2,1,0:T(8,128)S(1)} %get-tuple-element.42, f32[8,8,128]{2,1,0:T(8,128)S(1)} %copy.78, f32[8,8,8]{2,1,0:T(8,128)S(1)} %get-tuple-element.44, f32[8,8,8]{2,1,0:T(8,128)S(1)} %get-tuple-element.43), kind=kLoop, calls=%fused_computation.22 | loop fusion | flops 327680 | bytes 432128 | tf_op jit(solution)/shard_map/convert_element_type | solution.py:38
  110.0 4.4 %all-to-all-done.3 = bf16[32,2,1,2,8,128]{5,4,3,1,2,0:T(8,128)(2,1)} async-done(((bf16[32,2,1,2,8,128]{5,4,3,1,2,0:T(8,128)(2,1)}), bf16[32,2,1,2,8,128]{5,4,3,1,2,0:T(8,128)(2,1)}, u32[]{:S(2)}, u32[]{:S(2)}) %all-to-all-start.3) | async-done | bytes 262176 | tf_op jit(solution)/shard_map/all_to_all | solution.py:228
  114.4 1.0 constant_dynamic-update-slice_fusion
  115.4 1.0 copy-done.2
  (92 shorter events, 19.9 us)
Async XLA Ops:
  0.6 44.4 %copy-start = (bf16[128,64,128]{2,1,0:T(8,128)(2,1)S(1)}, bf16[128,64,128]{2,1,0:T(8,128)(2,1)}, u32[]{:S(2)}) copy-start(bf16[128,64,128]{2,1,0:T(8,128)(2,1)} %param.16) | copy-start | bytes 6291460
  0.6 1.7 %copy-start.10 = (bf16[256,256]{1,0:T(8,128)(2,1)S(1)}, bf16[256,256]{1,0:T(8,128)(2,1)}, u32[]{:S(2)}) copy-start(bf16[256,256]{1,0:T(8,128)(2,1)} %param.13) | copy-start | bytes 393220
  0.7 1.7 %copy-start.12 = (bf16[256,128]{1,0:T(8,128)(2,1)S(1)}, bf16[256,128]{1,0:T(8,128)(2,1)}, u32[]{:S(2)}) copy-start(bf16[256,128]{1,0:T(8,128)(2,1)} %param.14) | copy-start | bytes 196612
  0.7 1.6 %copy-start.4 = (bf16[256,8,128]{2,1,0:T(8,128)(2,1)S(1)}, bf16[256,8,128]{2,1,0:T(8,128)(2,1)}, u32[]{:S(2)}) copy-start(bf16[256,8,128]{2,1,0:T(8,128)(2,1)} %param.15) | copy-start | bytes 1572868
  2.7 1.1 copy-start.8
  6.9 12.4 %copy-start.9 = (s32[8]{0:T(128)S(1)}, s32[8]{0:T(128)}, u32[]{:S(2)}) copy-start(s32[8]{0:T(128)} %param.20) | copy-start | bytes 100
  6.9 12.4 %copy-start.1 = (s32[8,32]{1,0:T(8,128)S(1)}, s32[8,32]{1,0:T(8,128)}, u32[]{:S(2)}) copy-start(s32[8,32]{1,0:T(8,128)} %param.21) | copy-start | bytes 3076
  8.3 20.0 %all-to-all-start = ((f32[32,8,256]{2,1,0:T(8,128)}), f32[32,8,256]{2,1,0:T(8,128)}, u32[]{:S(2)}, u32[]{:S(2)}) async-start(f32[32,8,256]{2,1,0:T(8,128)} %copy.72), calls=%async_computation | async-start | bytes 524288 | tf_op jit(solution)/shard_map/all_to_all | solution.py:88
  20.3 1.3 %copy-start.11 = (bf16[8,8192]{1,0:T(8,128)(2,1)S(1)}, bf16[8,8192]{1,0:T(8,128)(2,1)}, u32[]{:S(2)}) copy-start(bf16[8,8192]{1,0:T(8,128)(2,1)} %param.18) | copy-start | bytes 393220
  20.6 1.0 copy-start.3
  29.3 17.3 %copy-start.7 = (f32[8,256]{1,0:T(8,128)}, f32[8,256]{1,0:T(8,128)S(1)}, u32[]{:S(2)}) copy-start(f32[8,256]{1,0:T(8,128)S(1)} %reduce_sum.64) | copy-start | bytes 24580
  30.7 25.6 %all-to-all-start.1 = ((bf16[16,48,128]{2,1,0:T(8,128)(2,1)}), bf16[16,48,128]{2,1,0:T(8,128)(2,1)}, u32[]{:S(2)}, u32[]{:S(2)}) async-start(bf16[16,48,128]{2,1,0:T(8,128)(2,1)} %maximum_maximum_fusion), calls=%async_computation.1 | async-start | bytes 393216 | tf_op jit(solution)/shard_map/all_to_all | solution.py:142
  66.0 21.0 %all-to-all-start.2 = ((bf16[16,48,128]{2,1,0:T(8,128)(2,1)}), bf16[16,48,128]{2,1,0:T(8,128)(2,1)}, u32[]{:S(2)}, u32[]{:S(2)}) async-start(bf16[16,48,128]{2,1,0:T(8,128)(2,1)} %broadcast_in_dim.74), calls=%async_computation.2 | async-start | bytes 393216 | tf_op jit(solution)/shard_map/all_to_all | solution.py:185
  88.8 0.7 copy-start.5
  89.5 15.9 %copy-start.6 = (bf16[8,8,128]{2,0,1:T(8,128)(2,1)S(1)}, bf16[8,8,128]{2,0,1:T(8,128)(2,1)}, u32[]{:S(2)}) copy-start(bf16[8,8,128]{2,0,1:T(8,128)(2,1)} %copy-done.5) | copy-start | bytes 49156
  93.6 20.8 %all-to-all-start.3 = ((bf16[32,2,1,2,8,128]{5,4,3,1,2,0:T(8,128)(2,1)}), bf16[32,2,1,2,8,128]{5,4,3,1,2,0:T(8,128)(2,1)}, u32[]{:S(2)}, u32[]{:S(2)}) async-start(bf16[32,2,1,2,8,128]{5,4,3,1,2,0:T(8,128)(2,1)} %bitcast.129), calls=%async_computation.3 | async-start | bytes 524288 | tf_op jit(solution)/shard_map/all_to_all | solution.py:228
  115.4 1.1 copy-start.2

commit v12 on v11

--- a/solution.py
+++ b/solution.py
@@ -157,7 +157,10 @@
     total_own = jnp.sum(shard_total * shard_scale, axis=0)
     mixed_own = jnp.sum(shard_mixed * shard_scale[..., None], axis=0)
 
-    mid_home = mid_spread[owner, request_index]
+    from_owner = owner[None, :, None] == jnp.arange(groups, dtype=jnp.int32)[:, None, None]
+    mid_home = jnp.sum(
+        jnp.where(from_owner, mid_spread.astype(jnp.float32), 0.0), axis=0
+    ).astype(jnp.bfloat16)
     mid_used = jnp.where(is_value, mid_home[:, rank_half:], mid_home[:, :rank_half])
     adapter_update = jnp.einsum(
         "ir,irc->ic", mid_used, up_weight_rows, preferred_element_type=jnp.float32

time: 118 us -> 116 us (0.983)
  local copies, waits for them, and re-layouts: 23.6 us -> 20.9 us
  waiting for transfers between devices: 21.5 us -> 23.2 us
  other arithmetic: 22.6 us -> 21.3 us
    all_to_all x1, waiting for transfers between devices: 8.45 us -> 10.5 us  [shards(): lax.all_to_all(parcel, 'grp', 0, 0, tiled=False)]
    slice x1 -> x0, local copies, waits for them, and re-layouts: 1.37 us -> none  [shards(): mid_spread = received[:, block_rows:stat_at]]
    gather x1 -> x0, local copies, waits for them, and re-layouts: 1.35 us -> none  [shards(): mid_home = mid_spread[owner, request_index]]
    unnamed x32 -> x34, local copies, waits for them, and re-layouts: 5.38 us -> 5.38 us
  transfers between devices with their start and end apart: 4 -> 4, of which waited for: 4 -> 3; matrix products, arithmetic and copies ran while one was open for 18% -> 18% of each run, Pallas kernels for 0% -> 0%
where the time goes in v12:
time: 116 us; the launch traced here: 115 us
  starting transfers between devices  43.9 us (38%)
  waiting for transfers between devices  23.2 us (20%)
  other arithmetic  21.3 us (18%)
  local copies, waits for them, and re-layouts  20.9 us (18%)
  matrix products  4.71 us (4%)
    all_to_all x1, starting transfers between devices, shards(): lax.all_to_all(parcel, 'grp', 0, 0, tiled=False)  12.6 us
    all_to_all x1, starting transfers between devices, shards(): lax.all_to_all(outbound, 'req', split_axis=0, concat_axis=0, tiled=True)  11.9 us
    all_to_all x1, starting transfers between devices, shards(): summed = jnp.sum(lax.all_to_all(partial, 'req', 0, 0, tiled=False), axis=0)  11 us
    all_to_all x1, waiting for transfers between devices, shards(): lax.all_to_all(parcel, 'grp', 0, 0, tiled=False)  10.5 us
    all_to_all x1, starting transfers between devices, shards(): lax.all_to_all(jnp.broadcast_to(merged[None], (groups,) + merged.shape),...  8.45 us
    all_to_all x1, waiting for transfers between devices, shards(): lax.all_to_all(jnp.broadcast_to(merged[None], (groups,) + merged.shape),...  8.37 us
    unnamed x34, local copies, waits for them, and re-layouts  5.38 us
    all_to_all x1, waiting for transfers between devices, shards(): lax.all_to_all(outbound, 'req', split_axis=0, concat_axis=0, tiled=True)  4.42 us
  transfers between devices with their start and end apart: 4, of which 3 were waited for; matrix products, arithmetic and copies ran while one was open for 18% of the time, Pallas kernels for 0%

profile of v12, /device:TPU:1, one launch (start us, length us, event | category | flops | bytes accessed | tf_op | source)
XLA Modules:
  0.0 115.1 jit_solution(2320544990589365718)
XLA Ops:
  0.7 1.5 %copy.127 = bf16[320,1,2,8,128]{4,3,2,1,0:T(8,128)(2,1)S(1)} copy(bf16[320,1,2,8,128]{4,3,2,1,0:T(8,128)(2,1)} %param.19) | data formatting | bytes 2621440
  2.8 1.1 slice.159
  4.6 0.8 copy.71
  5.5 1.4 %copy.92 = f32[32,8,8,128]{3,2,1,0:T(8,128)S(1)} copy(f32[32,8,8,128]{3,1,2,0:T(8,128)} %bitcast.131) | data formatting | bytes 2097152
  7.4 0.9 copy.72
  8.3 11.0 %all-to-all-start = ((f32[32,8,256]{2,1,0:T(8,128)}), f32[32,8,256]{2,1,0:T(8,128)}, u32[]{:S(2)}, u32[]{:S(2)}) async-start(f32[32,8,256]{2,1,0:T(8,128)} %copy.72), calls=%async_computation | async-start | bytes 524288 | tf_op jit(solution)/shard_map/all_to_all | solution.py:88
  22.0 0.9 copy-done.3
  22.9 1.1 fusion.49
  24.1 1.9 %fusion.44 = (f32[8,8,8]{1,2,0:T(8,128)S(1)}, bf16[8,8,8,256]{3,1,2,0:T(8,128)(2,1)}) fusion(f32[8,8,8,256]{3,1,2,0:T(8,128)} %get-tuple-element.69, f32[8,8,8]{1,2,0:T(8,128)S(1)} %get-tuple-element.68, pred[8,256]{1,0:T(8,128)(4,1)S(1)} %fusion.22), kind=kLoop, calls=%fused_computation.137 | loop fusion | flops 523776 | bytes 792576 | tf_op jit(solution)/shard_map/reduce_sum | solution.py:115
  28.2 2.0 %convolution_convert_fusion = bf16[8,8,8,128]{3,2,1,0:T(8,128)(2,1)} fusion(bf16[256,2,8,128]{3,0,2,1:T(8,128)(2,1)} %bitcast.134, bf16[8,8,8,256]{3,1,2,0:T(8,128)(2,1)} %get-tuple-element.50), kind=kOutput, calls=%fused_computation.9 | convolution fusion | flops 33554432 | bytes 917504 | tf_op jit(solution)/shard_map/hgis,shd->hgid/dot_general | solution.py:116
  30.2 1.6 %reduce_sum.73 = f32[8,256]{1,0:T(8,128)} reduce(f32[32,8,256]{2,1,0:T(8,128)} %all-to-all-done, f32[]{:T(128)} %constant.152.clone.1), dimensions={0}, to_apply=%region_3.4 | reduce | flops 63488 | bytes 270340 | tf_op jit(solution)/shard_map/reduce_sum | solution.py:88
  32.4 1.7 %maximum_maximum_fusion = bf16[16,48,128]{2,1,0:T(8,128)(2,1)} fusion(bf16[16,2,128]{2,1,0:T(2,128)(2,1)S(1)} %reshape.460, bf16[16,8,128]{2,1,0:T(8,128)(2,1)S(1)} %broadcast_in_dim.83, bf16[16,32,128]{2,1,0:T(8,128)(2,1)} %bitcast.140, bf16[48]{0:T(256)(128)(2,1)} %pad.19.clone), kind=kLoop, calls=%fused_computation.25 | loop fusion | flops 786432 | bytes 368736 | tf_op jit(solution)/shard_map/concatenate | solution.py:132
  34.1 12.6 %all-to-all-start.1 = ((bf16[16,48,128]{2,1,0:T(8,128)(2,1)}), bf16[16,48,128]{2,1,0:T(8,128)(2,1)}, u32[]{:S(2)}, u32[]{:S(2)}) async-start(bf16[16,48,128]{2,1,0:T(8,128)(2,1)} %maximum_maximum_fusion), calls=%async_computation.1 | async-start | bytes 393216 | tf_op jit(solution)/shard_map/all_to_all | solution.py:142
  47.5 1.2 %iota_compare_fusion.7 = pred[2,32]{1,0:T(4,128)(4,1)} fusion(s32[32]{0:T(128)} %convert_reduce_fusion), kind=kLoop, calls=%fused_computation.107 | loop fusion | flops 64 | bytes 192 | tf_op jit(solution)/shard_map/eq | solution.py:213
  49.3 10.5 %all-to-all-done.1 = bf16[16,48,128]{2,1,0:T(8,128)(2,1)} async-done(((bf16[16,48,128]{2,1,0:T(8,128)(2,1)}), bf16[16,48,128]{2,1,0:T(8,128)(2,1)}, u32[]{:S(2)}, u32[]{:S(2)}) %all-to-all-start.1) | async-done | bytes 196640 | tf_op jit(solution)/shard_map/all_to_all | solution.py:142
  60.5 0.8 select_reduce_fusion.1
  62.5 1.0 multiply_reduce_fusion
  64.5 8.4 %all-to-all-start.2 = ((bf16[16,48,128]{2,1,0:T(8,128)(2,1)}), bf16[16,48,128]{2,1,0:T(8,128)(2,1)}, u32[]{:S(2)}, u32[]{:S(2)}) async-start(bf16[16,48,128]{2,1,0:T(8,128)(2,1)} %broadcast_in_dim.133), calls=%async_computation.2 | async-start | bytes 393216 | tf_op jit(solution)/shard_map/all_to_all | solution.py:188
  72.9 0.8 and_reduce_fusion
  73.7 0.8 fusion.9
  75.9 1.2 %fusion.33 = pred[8]{0:T(512)(128)(4,1)} fusion(s32[]{:T(128)S(6)} %axis_index.22, s32[8]{0:T(128)} %param.20), kind=kLoop, calls=%fused_computation.121 | loop fusion | flops 96 | bytes 44 | tf_op jit(solution)/shard_map/eq | solution.py:220
  77.1 8.4 %all-to-all-done.2 = bf16[16,48,128]{2,1,0:T(8,128)(2,1)} async-done(((bf16[16,48,128]{2,1,0:T(8,128)(2,1)}), bf16[16,48,128]{2,1,0:T(8,128)(2,1)}, u32[]{:S(2)}, u32[]{:S(2)}) %all-to-all-start.2) | async-done | bytes 196640 | tf_op jit(solution)/shard_map/all_to_all | solution.py:188
  88.1 1.0 scatter_fusion
  89.1 0.9 slice.170
  90.8 1.4 %gather_fusion.3 = bf16[64,2,8,128]{3,2,1,0:T(8,128)(2,1)} fusion(bf16[320,2,8,128]{3,2,1,0:T(8,128)(2,1)S(1)} %bitcast.129, s32[1024]{0:T(1024)} %pad_clamp_fusion), kind=kCustom, calls=%fused_computation.3 | custom fusion | bytes 524544 | tf_op jit(solution)/shard_map/gather | solution.py:229
  92.2 11.9 %all-to-all-start.3 = ((bf16[32,2,1,2,8,128]{5,4,3,1,2,0:T(8,128)(2,1)}), bf16[32,2,1,2,8,128]{5,4,3,1,2,0:T(8,128)(2,1)}, u32[]{:S(2)}, u32[]{:S(2)}) async-start(bf16[32,2,1,2,8,128]{5,4,3,1,2,0:T(8,128)(2,1)} %bitcast.135), calls=%async_computation.3 | async-start | bytes 524288 | tf_op jit(solution)/shard_map/all_to_all | solution.py:231
  104.1 1.1 fusion.7
  105.9 0.8 multiply_add_fusion
  106.7 1.9 %divide_convert_fusion = bf16[8,8,8,128]{3,2,1,0:T(8,128)(2,1)} fusion(f32[8,8,8,128]{3,2,1,0:T(8,128)} %convert.32, f32[8,8,8]{2,1,0:T(8,128)S(1)} %get-tuple-element.42, f32[8,8,128]{2,1,0:T(8,128)S(1)} %copy.78, f32[8,8,8]{2,1,0:T(8,128)S(1)} %get-tuple-element.44, f32[8,8,8]{2,1,0:T(8,128)S(1)} %get-tuple-element.43), kind=kLoop, calls=%fused_computation.21 | loop fusion | flops 327680 | bytes 432128 | tf_op jit(solution)/shard_map/convert_element_type | solution.py:38
  108.6 4.4 %all-to-all-done.3 = bf16[32,2,1,2,8,128]{5,4,3,1,2,0:T(8,128)(2,1)} async-done(((bf16[32,2,1,2,8,128]{5,4,3,1,2,0:T(8,128)(2,1)}), bf16[32,2,1,2,8,128]{5,4,3,1,2,0:T(8,128)(2,1)}, u32[]{:S(2)}, u32[]{:S(2)}) %all-to-all-start.3) | async-done | bytes 262176 | tf_op jit(solution)/shard_map/all_to_all | solution.py:231
  113.0 1.0 constant_dynamic-update-slice_fusion
  114.0 1.0 copy-done.2
  (95 shorter events, 17.1 us)
Async XLA Ops:
  0.6 26.9 %copy-start = (bf16[128,64,128]{2,1,0:T(8,128)(2,1)S(1)}, bf16[128,64,128]{2,1,0:T(8,128)(2,1)}, u32[]{:S(2)}) copy-start(bf16[128,64,128]{2,1,0:T(8,128)(2,1)} %param.16) | copy-start | bytes 6291460
  0.6 1.7 %copy-start.11 = (bf16[256,256]{1,0:T(8,128)(2,1)S(1)}, bf16[256,256]{1,0:T(8,128)(2,1)}, u32[]{:S(2)}) copy-start(bf16[256,256]{1,0:T(8,128)(2,1)} %param.13) | copy-start | bytes 393220
  0.7 1.7 %copy-start.13 = (bf16[256,128]{1,0:T(8,128)(2,1)S(1)}, bf16[256,128]{1,0:T(8,128)(2,1)}, u32[]{:S(2)}) copy-start(bf16[256,128]{1,0:T(8,128)(2,1)} %param.14) | copy-start | bytes 196612
  0.7 1.6 %copy-start.4 = (bf16[256,8,128]{2,1,0:T(8,128)(2,1)S(1)}, bf16[256,8,128]{2,1,0:T(8,128)(2,1)}, u32[]{:S(2)}) copy-start(bf16[256,8,128]{2,1,0:T(8,128)(2,1)} %param.15) | copy-start | bytes 1572868
  2.7 1.1 copy-start.7
  6.9 12.4 %copy-start.9 = (s32[32,1]{0,1:T(1,128)S(1)}, s32[32,1]{0,1:T(1,128)}, u32[]{:S(2)}) copy-start(s32[32,1]{0,1:T(1,128)} %param.23) | copy-start | bytes 388
  6.9 13.1 %copy-start.10 = (s32[8]{0:T(128)S(1)}, s32[8]{0:T(128)}, u32[]{:S(2)}) copy-start(s32[8]{0:T(128)} %param.20) | copy-start | bytes 100
  6.9 13.1 %copy-start.1 = (s32[8,32]{1,0:T(8,128)S(1)}, s32[8,32]{1,0:T(8,128)}, u32[]{:S(2)}) copy-start(s32[8,32]{1,0:T(8,128)} %param.21) | copy-start | bytes 3076
  8.3 21.9 %all-to-all-start = ((f32[32,8,256]{2,1,0:T(8,128)}), f32[32,8,256]{2,1,0:T(8,128)}, u32[]{:S(2)}, u32[]{:S(2)}) async-start(f32[32,8,256]{2,1,0:T(8,128)} %copy.72), calls=%async_computation | async-start | bytes 524288 | tf_op jit(solution)/shard_map/all_to_all | solution.py:88
  21.6 1.3 %copy-start.12 = (bf16[8,8192]{1,0:T(8,128)(2,1)S(1)}, bf16[8,8192]{1,0:T(8,128)(2,1)}, u32[]{:S(2)}) copy-start(bf16[8,8192]{1,0:T(8,128)(2,1)} %param.18) | copy-start | bytes 393220
  21.9 1.0 copy-start.3
  28.2 35.5 %copy-start.8 = (bf16[48]{0:T(256)(128)(2,1)S(1)}, bf16[48]{0:T(256)(128)(2,1)}, u32[]{:S(2)}) copy-start(bf16[48]{0:T(256)(128)(2,1)} %pad.19.clone) | copy-start | bytes 292
  34.1 25.6 %all-to-all-start.1 = ((bf16[16,48,128]{2,1,0:T(8,128)(2,1)}), bf16[16,48,128]{2,1,0:T(8,128)(2,1)}, u32[]{:S(2)}, u32[]{:S(2)}) async-start(bf16[16,48,128]{2,1,0:T(8,128)(2,1)} %maximum_maximum_fusion), calls=%async_computation.1 | async-start | bytes 393216 | tf_op jit(solution)/shard_map/all_to_all | solution.py:142
  64.5 21.0 %all-to-all-start.2 = ((bf16[16,48,128]{2,1,0:T(8,128)(2,1)}), bf16[16,48,128]{2,1,0:T(8,128)(2,1)}, u32[]{:S(2)}, u32[]{:S(2)}) async-start(bf16[16,48,128]{2,1,0:T(8,128)(2,1)} %broadcast_in_dim.133), calls=%async_computation.2 | async-start | bytes 393216 | tf_op jit(solution)/shard_map/all_to_all | solution.py:188
  87.3 0.8 copy-start.5
  88.1 16.0 %copy-start.6 = (bf16[8,8,128]{2,0,1:T(8,128)(2,1)S(1)}, bf16[8,8,128]{2,0,1:T(8,128)(2,1)}, u32[]{:S(2)}) copy-start(bf16[8,8,128]{2,0,1:T(8,128)(2,1)} %copy-done.5) | copy-start | bytes 49156
  92.2 20.8 %all-to-all-start.3 = ((bf16[32,2,1,2,8,128]{5,4,3,1,2,0:T(8,128)(2,1)}), bf16[32,2,1,2,8,128]{5,4,3,1,2,0:T(8,128)(2,1)}, u32[]{:S(2)}, u32[]{:S(2)}) async-start(bf16[32,2,1,2,8,128]{5,4,3,1,2,0:T(8,128)(2,1)} %bitcast.135), calls=%async_computation.3 | async-start | bytes 524288 | tf_op jit(solution)/shard_map/all_to_all | solution.py:231
  114.0 1.1 copy-start.2

commit v13 on v12

--- a/solution.py
+++ b/solution.py
@@ -75,8 +75,9 @@
     both = jnp.concatenate(
         [key_value_weight, adapter_down_weight.reshape(adapter_down_weight.shape[0], -1)], axis=1
     )
-    by_home = normed_token_input.reshape(homes, rows, -1)
-    products = jnp.einsum("hiw,wc->hic", by_home, both, preferred_element_type=jnp.float32)
+    products = jnp.dot(normed_token_input, both, preferred_element_type=jnp.float32).reshape(
+        homes, rows, -1
+    )
     base_part = products[:, :, :column_span]
     down_all = products[:, :, column_span:].reshape(homes, rows, local_adapters, rank_width)
     local_choice = (selected_adapter - group_index * local_adapters).reshape(homes, rows)

time: 116 us -> 113 us (0.974)
  other arithmetic: 21.3 us -> 13.1 us
  waiting for transfers between devices: 23.2 us -> 30.8 us
  local copies, waits for them, and re-layouts: 20.9 us -> 16.5 us
  matrix products: 4.71 us -> 6.43 us
    all_to_all x1, waiting for transfers between devices: 8.37 us -> 12.1 us  [shards(): lax.all_to_all(jnp.broadcast_to(merged[None], (groups,) + merged.shape),...]
    all_to_all x1, waiting for transfers between devices: 10.5 us -> 12.9 us  [shards(): lax.all_to_all(parcel, 'grp', 0, 0, tiled=False)]
    all_to_all x1, waiting for transfers between devices: 4.42 us -> 5.8 us  [shards(): lax.all_to_all(outbound, 'req', split_axis=0, concat_axis=0, tiled=True)]
    eq x1, other arithmetic: 1.24 us -> 0.01 us  [shards(): mine = offset // slot_tokens == group_index]
    unnamed x34 -> x27, local copies, waits for them, and re-layouts: 5.38 us -> 5.24 us
  transfers between devices with their start and end apart: 4 -> 4, of which waited for: 3 -> 3; matrix products, arithmetic and copies ran while one was open for 18% -> 12% of each run, Pallas kernels for 0% -> 0%
where the time goes in v13:
time: 113 us; the launch traced here: 112 us
  starting transfers between devices  43.9 us (39%)
  waiting for transfers between devices  30.8 us (27%)
  local copies, waits for them, and re-layouts  16.5 us (15%)
  other arithmetic  13.1 us (12%)
  matrix products  6.43 us (6%)
    all_to_all x1, waiting for transfers between devices, shards(): lax.all_to_all(parcel, 'grp', 0, 0, tiled=False)  12.9 us
    all_to_all x1, starting transfers between devices, shards(): lax.all_to_all(parcel, 'grp', 0, 0, tiled=False)  12.6 us
    all_to_all x1, waiting for transfers between devices, shards(): lax.all_to_all(jnp.broadcast_to(merged[None], (groups,) + merged.shape),...  12.1 us
    all_to_all x1, starting transfers between devices, shards(): lax.all_to_all(outbound, 'req', split_axis=0, concat_axis=0, tiled=True)  11.9 us
    all_to_all x1, starting transfers between devices, shards(): summed = jnp.sum(lax.all_to_all(partial, 'req', 0, 0, tiled=False), axis=0)  11 us
    all_to_all x1, starting transfers between devices, shards(): lax.all_to_all(jnp.broadcast_to(merged[None], (groups,) + merged.shape),...  8.45 us
    all_to_all x1, waiting for transfers between devices, shards(): lax.all_to_all(outbound, 'req', split_axis=0, concat_axis=0, tiled=True)  5.8 us
    unnamed x27, local copies, waits for them, and re-layouts  5.24 us
  transfers between devices with their start and end apart: 4, of which 3 were waited for; matrix products, arithmetic and copies ran while one was open for 12% of the time, Pallas kernels for 0%

profile of v13, /device:TPU:1, one launch (start us, length us, event | category | flops | bytes accessed | tf_op | source)
XLA Modules:
  0.0 111.7 jit_solution(9875125827271664634)
XLA Ops:
  0.7 1.5 %copy.109 = bf16[320,1,2,8,128]{4,3,2,1,0:T(8,128)(2,1)S(1)} copy(bf16[320,1,2,8,128]{4,3,2,1,0:T(8,128)(2,1)} %param.19) | data formatting | bytes 2621440
  2.7 0.8 sub.98
  3.5 1.1 %copy.100 = bf16[32,8,8,128]{3,1,2,0:T(8,128)(2,1)S(1)} copy(bf16[32,8,8,128]{3,2,1,0:T(8,128)(2,1)} %bitcast.134) | data formatting | bytes 1048576
  4.7 1.2 %convolution_bitcast_fusion = f32[32,8,1152]{2,1,0:T(8,128)S(1)} fusion(bf16[256,256]{1,0:T(8,128)(2,1)S(1)} %copy-done.4, bf16[256,1024]{1,0:T(8,128)(2,1)S(1)} %bitcast.129, bf16[256,128]{1,0:T(8,128)(2,1)} %param.14), kind=kOutput, calls=%fused_computation.5 | convolution fusion | flops 152174592 | bytes 1900544 | tf_op jit(solution)/shard_map/dot_general | solution.py:78
  6.3 0.7 pad_maximum_fusion
  7.0 11.0 %all-to-all-start = ((f32[32,8,256]{2,1,0:T(8,128)}), f32[32,8,256]{2,1,0:T(8,128)}, u32[]{:S(2)}, u32[]{:S(2)}) async-start(f32[32,8,256]{2,1,0:T(8,128)} %pad_maximum_fusion), calls=%async_computation | async-start | bytes 524288 | tf_op jit(solution)/shard_map/all_to_all | solution.py:89
  19.7 0.9 copy-done.3
  20.6 1.1 fusion.51
  21.8 1.9 %fusion.46 = (f32[8,8,8]{1,2,0:T(8,128)S(1)}, bf16[8,8,8,256]{3,1,2,0:T(8,128)(2,1)}) fusion(f32[8,8,8,256]{3,1,2,0:T(8,128)} %get-tuple-element.69, f32[8,8,8]{1,2,0:T(8,128)S(1)} %get-tuple-element.68, pred[8,256]{1,0:T(8,128)(4,1)S(1)} %fusion.24), kind=kLoop, calls=%fused_computation.138 | loop fusion | flops 523776 | bytes 792576 | tf_op jit(solution)/shard_map/reduce_sum | solution.py:116
  25.7 1.2 %gather_fusion.1 = bf16[8,64,128]{2,1,0:T(8,128)(2,1)} fusion(bf16[128,64,128]{2,1,0:T(8,128)(2,1)S(1)} %copy-done, s32[1024]{0:T(1024)S(1)} %pad_clamp_fusion.1), kind=kCustom, calls=%fused_computation.1 | custom fusion | bytes 262176 | tf_op jit(solution)/shard_map/gather | solution.py:88
  26.9 2.0 %convolution_convert_fusion = bf16[8,8,8,128]{3,2,1,0:T(8,128)(2,1)} fusion(bf16[256,2,8,128]{3,0,2,1:T(8,128)(2,1)} %bitcast.131, bf16[8,8,8,256]{3,1,2,0:T(8,128)(2,1)} %get-tuple-element.50), kind=kOutput, calls=%fused_computation.9 | convolution fusion | flops 33554432 | bytes 917504 | tf_op jit(solution)/shard_map/hgis,shd->hgid/dot_general | solution.py:117
  28.9 1.0 reduce_sum.73
  29.9 1.7 %maximum_maximum_fusion = bf16[16,48,128]{2,1,0:T(8,128)(2,1)} fusion(bf16[16,2,128]{2,1,0:T(2,128)(2,1)S(1)} %reshape.460, bf16[16,8,128]{2,1,0:T(8,128)(2,1)S(1)} %broadcast_in_dim.83, bf16[16,32,128]{2,1,0:T(8,128)(2,1)} %bitcast.136, bf16[48]{0:T(256)(128)(2,1)S(1)} %pad.19.clone), kind=kLoop, calls=%fused_computation.27 | loop fusion | flops 786432 | bytes 368736 | tf_op jit(solution)/shard_map/concatenate | solution.py:133
  31.6 12.6 %all-to-all-start.1 = ((bf16[16,48,128]{2,1,0:T(8,128)(2,1)}), bf16[16,48,128]{2,1,0:T(8,128)(2,1)}, u32[]{:S(2)}, u32[]{:S(2)}) async-start(bf16[16,48,128]{2,1,0:T(8,128)(2,1)} %maximum_maximum_fusion), calls=%async_computation.1 | async-start | bytes 393216 | tf_op jit(solution)/shard_map/all_to_all | solution.py:143
  44.3 12.9 %all-to-all-done.1 = bf16[16,48,128]{2,1,0:T(8,128)(2,1)} async-done(((bf16[16,48,128]{2,1,0:T(8,128)(2,1)}), bf16[16,48,128]{2,1,0:T(8,128)(2,1)}, u32[]{:S(2)}, u32[]{:S(2)}) %all-to-all-start.1) | async-done | bytes 196640 | tf_op jit(solution)/shard_map/all_to_all | solution.py:143
  57.2 0.8 slice.125
  58.2 1.0 multiply_reduce_fusion
  59.2 0.8 select_reduce_fusion
  60.1 1.0 fusion.26
  62.2 8.4 %all-to-all-start.2 = ((bf16[16,48,128]{2,1,0:T(8,128)(2,1)}), bf16[16,48,128]{2,1,0:T(8,128)(2,1)}, u32[]{:S(2)}, u32[]{:S(2)}) async-start(bf16[16,48,128]{2,1,0:T(8,128)(2,1)} %broadcast_in_dim.133), calls=%async_computation.2 | async-start | bytes 393216 | tf_op jit(solution)/shard_map/all_to_all | solution.py:189
  71.1 12.1 %all-to-all-done.2 = bf16[16,48,128]{2,1,0:T(8,128)(2,1)} async-done(((bf16[16,48,128]{2,1,0:T(8,128)(2,1)}), bf16[16,48,128]{2,1,0:T(8,128)(2,1)}, u32[]{:S(2)}, u32[]{:S(2)}) %all-to-all-start.2) | async-done | bytes 196640 | tf_op jit(solution)/shard_map/all_to_all | solution.py:189
  83.2 0.7 fusion.47
  84.0 0.7 scatter_fusion
  84.8 0.9 slice.170
  86.4 0.8 slice.171
  87.5 1.3 %gather_fusion.3 = bf16[64,2,8,128]{3,2,1,0:T(8,128)(2,1)} fusion(bf16[320,2,8,128]{3,2,1,0:T(8,128)(2,1)S(1)} %bitcast.127, s32[1024]{0:T(1024)S(1)} %pad_clamp_fusion), kind=kCustom, calls=%fused_computation.3 | custom fusion | bytes 524544 | tf_op jit(solution)/shard_map/gather | solution.py:230
  88.8 11.9 %all-to-all-start.3 = ((bf16[32,2,1,2,8,128]{5,4,3,1,2,0:T(8,128)(2,1)}), bf16[32,2,1,2,8,128]{5,4,3,1,2,0:T(8,128)(2,1)}, u32[]{:S(2)}, u32[]{:S(2)}) async-start(bf16[32,2,1,2,8,128]{5,4,3,1,2,0:T(8,128)(2,1)} %bitcast.132), calls=%async_computation.3 | async-start | bytes 524288 | tf_op jit(solution)/shard_map/all_to_all | solution.py:232
  100.7 1.1 fusion.9
  101.9 1.9 %divide_convert_fusion = bf16[8,8,8,128]{3,2,1,0:T(8,128)(2,1)} fusion(f32[8,8,8,128]{3,2,1,0:T(8,128)} %convert.32, f32[8,8,8]{2,1,0:T(8,128)S(1)} %get-tuple-element.42, f32[8,8,128]{2,1,0:T(8,128)S(1)} %copy.63, f32[8,8,8]{2,1,0:T(8,128)S(1)} %get-tuple-element.44, f32[8,8,8]{2,1,0:T(8,128)S(1)} %get-tuple-element.43), kind=kLoop, calls=%fused_computation.23 | loop fusion | flops 327680 | bytes 432128 | tf_op jit(solution)/shard_map/convert_element_type | solution.py:38
  103.8 5.8 %all-to-all-done.3 = bf16[32,2,1,2,8,128]{5,4,3,1,2,0:T(8,128)(2,1)} async-done(((bf16[32,2,1,2,8,128]{5,4,3,1,2,0:T(8,128)(2,1)}), bf16[32,2,1,2,8,128]{5,4,3,1,2,0:T(8,128)(2,1)}, u32[]{:S(2)}, u32[]{:S(2)}) %all-to-all-start.3) | async-done | bytes 262176 | tf_op jit(solution)/shard_map/all_to_all | solution.py:232
  109.6 1.0 constant_dynamic-update-slice_fusion
  110.6 1.0 copy-done.2
  (85 shorter events, 7.8 us)
Async XLA Ops:
  0.6 25.0 %copy-start = (bf16[128,64,128]{2,1,0:T(8,128)(2,1)S(1)}, bf16[128,64,128]{2,1,0:T(8,128)(2,1)}, u32[]{:S(2)}) copy-start(bf16[128,64,128]{2,1,0:T(8,128)(2,1)} %param.16) | copy-start | bytes 6291460
  0.6 4.0 %copy-start.4 = (bf16[256,256]{1,0:T(8,128)(2,1)S(1)}, bf16[256,256]{1,0:T(8,128)(2,1)}, u32[]{:S(2)}) copy-start(bf16[256,256]{1,0:T(8,128)(2,1)} %param.13) | copy-start | bytes 393220
  0.7 1.5 %copy-start.5 = (s32[256,1]{0,1:T(1,128)S(1)}, s32[256,1]{0,1:T(1,128)}, u32[]{:S(2)}) copy-start(s32[256,1]{0,1:T(1,128)} %param.17) | copy-start | bytes 3076
  5.9 12.1 %copy-start.1 = (s32[8,32]{1,0:T(8,128)S(1)}, s32[8,32]{1,0:T(8,128)}, u32[]{:S(2)}) copy-start(s32[8,32]{1,0:T(8,128)} %param.21) | copy-start | bytes 3076
  7.0 21.9 %all-to-all-start = ((f32[32,8,256]{2,1,0:T(8,128)}), f32[32,8,256]{2,1,0:T(8,128)}, u32[]{:S(2)}, u32[]{:S(2)}) async-start(f32[32,8,256]{2,1,0:T(8,128)} %pad_maximum_fusion), calls=%async_computation | async-start | bytes 524288 | tf_op jit(solution)/shard_map/all_to_all | solution.py:89
  19.0 0.7 copy-start.9
  19.0 1.6 %copy-start.10 = (bf16[8,8192]{1,0:T(8,128)(2,1)S(1)}, bf16[8,8192]{1,0:T(8,128)(2,1)}, u32[]{:S(2)}) copy-start(bf16[8,8192]{1,0:T(8,128)(2,1)} %param.18) | copy-start | bytes 393220
  19.6 1.0 copy-start.3
  20.6 4.0 %copy-start.7 = (s32[32,1]{0,1:T(1,128)S(1)}, s32[32,1]{0,1:T(1,128)}, u32[]{:S(2)}) copy-start(s32[32,1]{0,1:T(1,128)} %param.23) | copy-start | bytes 388
  20.6 4.2 %copy-start.6 = (s32[256,1]{0,1:T(1,128)S(1)}, s32[256,1]{0,1:T(1,128)}, u32[]{:S(2)}) copy-start(s32[256,1]{0,1:T(1,128)} %param.17) | copy-start | bytes 3076
  28.9 41.9 %copy-start.8 = (s32[32]{0:T(128)S(1)}, s32[32]{0:T(128)}, u32[]{:S(2)}) copy-start(s32[32]{0:T(128)} %param.22) | copy-start | bytes 388
  31.6 25.6 %all-to-all-start.1 = ((bf16[16,48,128]{2,1,0:T(8,128)(2,1)}), bf16[16,48,128]{2,1,0:T(8,128)(2,1)}, u32[]{:S(2)}, u32[]{:S(2)}) async-start(bf16[16,48,128]{2,1,0:T(8,128)(2,1)} %maximum_maximum_fusion), calls=%async_computation.1 | async-start | bytes 393216 | tf_op jit(solution)/shard_map/all_to_all | solution.py:143
  62.2 21.0 %all-to-all-start.2 = ((bf16[16,48,128]{2,1,0:T(8,128)(2,1)}), bf16[16,48,128]{2,1,0:T(8,128)(2,1)}, u32[]{:S(2)}, u32[]{:S(2)}) async-start(bf16[16,48,128]{2,1,0:T(8,128)(2,1)} %broadcast_in_dim.133), calls=%async_computation.2 | async-start | bytes 393216 | tf_op jit(solution)/shard_map/all_to_all | solution.py:189
  88.8 20.8 %all-to-all-start.3 = ((bf16[32,2,1,2,8,128]{5,4,3,1,2,0:T(8,128)(2,1)}), bf16[32,2,1,2,8,128]{5,4,3,1,2,0:T(8,128)(2,1)}, u32[]{:S(2)}, u32[]{:S(2)}) async-start(bf16[32,2,1,2,8,128]{5,4,3,1,2,0:T(8,128)(2,1)} %bitcast.132), calls=%async_computation.3 | async-start | bytes 524288 | tf_op jit(solution)/shard_map/all_to_all | solution.py:232
  110.6 1.1 copy-start.2

commit v14 on v13

--- a/solution.py
+++ b/solution.py
@@ -133,11 +133,14 @@
     parcel = jnp.concatenate(
         [
             local_mixed.reshape(groups, block_rows, head_dim).astype(jnp.bfloat16),
-            jnp.broadcast_to(mid_rows[None], (groups,) + mid_rows.shape),
+            jnp.zeros((groups,) + mid_rows.shape, jnp.bfloat16),
             stat_pack,
             jnp.zeros((groups, spare_rows, head_dim), jnp.bfloat16),
         ],
         axis=1,
+    )
+    parcel = lax.dynamic_update_slice_in_dim(
+        parcel, jnp.broadcast_to(mid_rows[None], (groups,) + mid_rows.shape), block_rows, axis=1
     )
     received, up_weight_rows = lax.optimization_barrier(
         (lax.all_to_all(parcel, "grp", 0, 0, tiled=False), up_weight_rows)
@@ -220,11 +223,10 @@
     offset = lengths % page_size
     mine = offset // slot_tokens == group_index
     token_local = offset % slot_tokens
-    current = key_value_pages[page_slot, token_local]
     fresh = jnp.stack([new_keys, new_values], axis=0).transpose(2, 0, 1, 3)
-    written = key_value_pages.at[page_slot, token_local].set(
-        jnp.where(mine[:, None, None, None], fresh, current)
-    )
+    written = key_value_pages.at[
+        jnp.where(mine, page_slot, key_value_pages.shape[0]), token_local
+    ].set(fresh, mode="drop")
 
     written = written.at[live_slots].set(jnp.zeros((), key_value_pages.dtype))
     outbound = written[jnp.where(filled, source_slot, live_slots)]

time: 113 us -> 118 us (1.044)
  other arithmetic: 13.1 us -> 17.9 us
  waiting for transfers between devices: 30.8 us -> 28.2 us
  local copies, waits for them, and re-layouts: 16.5 us -> 18.8 us
    all_to_all x1, waiting for transfers between devices: 12.1 us -> 10.1 us  [shards(): lax.all_to_all(jnp.broadcast_to(merged[None], (groups,) + merged.shape),...]
    all_to_all x1, waiting for transfers between devices: 12.9 us -> 11.1 us  [shards(): lax.all_to_all(parcel, 'grp', 0, 0, tiled=False)]
    concatenate x1 -> x2, local copies, waits for them, and re-layouts: 0.08 us -> 1.28 us  [shards(): jnp.concatenate([local_mixed.reshape(groups, block_rows, head_dim).astype...]
    all_to_all x1, waiting for transfers between devices: 5.8 us -> 6.99 us  [shards(): lax.all_to_all(outbound, 'req', split_axis=0, concat_axis=0, tiled=True)]
    unnamed x27 -> x21, local copies, waits for them, and re-layouts: 5.24 us -> 5.78 us
  transfers between devices with their start and end apart: 4 -> 4, of which waited for: 3 -> 3; matrix products, arithmetic and copies ran while one was open for 12% -> 18% of each run, Pallas kernels for 0% -> 0%
where the time goes in v14:
time: 118 us; the launch traced here: 117 us
  starting transfers between devices  44 us (37%)
  waiting for transfers between devices  28.2 us (24%)
  local copies, waits for them, and re-layouts  18.8 us (16%)
  other arithmetic  17.9 us (15%)
  matrix products  6.82 us (6%)
    all_to_all x1, starting transfers between devices, shards(): lax.all_to_all(parcel, 'grp', 0, 0, tiled=False)  12.6 us
    all_to_all x1, starting transfers between devices, shards(): lax.all_to_all(outbound, 'req', split_axis=0, concat_axis=0, tiled=True)  11.9 us
    all_to_all x1, waiting for transfers between devices, shards(): lax.all_to_all(parcel, 'grp', 0, 0, tiled=False)  11.1 us
    all_to_all x1, starting transfers between devices, shards(): summed = jnp.sum(lax.all_to_all(partial, 'req', 0, 0, tiled=False), axis=0)  11 us
    all_to_all x1, waiting for transfers between devices, shards(): lax.all_to_all(jnp.broadcast_to(merged[None], (groups,) + merged.shape),...  10.1 us
    all_to_all x1, starting transfers between devices, shards(): lax.all_to_all(jnp.broadcast_to(merged[None], (groups,) + merged.shape),...  8.45 us
    all_to_all x1, waiting for transfers between devices, shards(): lax.all_to_all(outbound, 'req', split_axis=0, concat_axis=0, tiled=True)  6.99 us
    unnamed x21, local copies, waits for them, and re-layouts  5.78 us
  transfers between devices with their start and end apart: 4, of which 3 were waited for; matrix products, arithmetic and copies ran while one was open for 18% of the time, Pallas kernels for 0%

profile of v14, /device:TPU:1, one launch (start us, length us, event | category | flops | bytes accessed | tf_op | source)
XLA Modules:
  0.0 116.6 jit_solution(348321092309228025)
XLA Ops:
  0.7 1.5 %copy.89 = bf16[320,1,2,8,128]{4,3,2,1,0:T(8,128)(2,1)S(1)} copy(bf16[320,1,2,8,128]{4,3,2,1,0:T(8,128)(2,1)} %param.19) | data formatting | bytes 2621440
  2.2 1.9 %copy.81 = bf16[32,8,8,128]{3,1,2,0:T(8,128)(2,1)} copy(bf16[32,8,8,128]{3,2,1,0:T(8,128)(2,1)} %bitcast.122) | data formatting | bytes 1048576
  4.7 0.8 sub.100
  5.5 1.4 %convolution_bitcast_fusion = f32[32,8,1152]{2,1,0:T(8,128)S(1)} fusion(bf16[256,256]{1,0:T(8,128)(2,1)S(1)} %copy-done.3, bf16[256,1024]{1,0:T(8,128)(2,1)} %bitcast.117, bf16[256,128]{1,0:T(8,128)(2,1)} %param.14), kind=kOutput, calls=%fused_computation.4 | convolution fusion | flops 152174592 | bytes 1900544 | tf_op jit(solution)/shard_map/dot_general | solution.py:78
  8.0 11.0 %all-to-all-start = ((f32[32,8,256]{2,1,0:T(8,128)}), f32[32,8,256]{2,1,0:T(8,128)}, u32[]{:S(2)}, u32[]{:S(2)}) async-start(f32[32,8,256]{2,1,0:T(8,128)} %pad_maximum_fusion), calls=%async_computation | async-start | bytes 524288 | tf_op jit(solution)/shard_map/all_to_all | solution.py:89
  19.2 1.2 %copy.80 = bf16[256,1,2,8,128]{4,0,3,2,1:T(8,128)(2,1)} copy(bf16[256,1,2,8,128]{4,3,2,1,0:T(8,128)(2,1)S(1)} %slice.118) | data formatting | bytes 2097152
  21.4 2.2 %fusion.46 = (f32[8,8,8]{1,2,0:T(8,128)S(1)}, f32[8,8,8,256]{3,1,2,0:T(8,128)}) fusion(bf16[8,8,8,128]{3,0,2,1:T(8,128)(2,1)} %bitcast.134, bf16[256,2,8,128]{3,0,2,1:T(8,128)(2,1)} %bitcast.118, pred[8,256]{1,0:T(8,128)(4,1)S(1)} %fusion.23), kind=kOutput, calls=%fused_computation.138 | convolution fusion | flops 33947136 | bytes 1183744 | tf_op jit(solution)/shard_map/ihgd,shd->hgis/dot_general | solution.py:110
  23.6 1.9 %fusion.43 = (f32[8,8,8]{1,2,0:T(8,128)S(1)}, bf16[8,8,8,256]{3,1,2,0:T(8,128)(2,1)}) fusion(f32[8,8,8,256]{3,1,2,0:T(8,128)} %get-tuple-element.67, f32[8,8,8]{1,2,0:T(8,128)S(1)} %get-tuple-element.66, pred[8,256]{1,0:T(8,128)(4,1)S(1)} %fusion.23), kind=kLoop, calls=%fused_computation.135 | loop fusion | flops 523776 | bytes 792576 | tf_op jit(solution)/shard_map/reduce_sum | solution.py:116
  25.8 2.0 %convolution_convert_fusion = bf16[8,8,8,128]{3,2,1,0:T(8,128)(2,1)} fusion(bf16[256,2,8,128]{3,0,2,1:T(8,128)(2,1)} %bitcast.119, bf16[8,8,8,256]{3,1,2,0:T(8,128)(2,1)} %get-tuple-element.52), kind=kOutput, calls=%fused_computation.8 | convolution fusion | flops 33554432 | bytes 917504 | tf_op jit(solution)/shard_map/hgis,shd->hgid/dot_general | solution.py:117
  28.7 1.2 %gather_fusion = s32[8]{0:T(128)} fusion(s32[8,32]{1,0:T(8,128)S(1)} %copy-done.1, s32[8]{0:T(128)S(1)} %get-tuple-element.69), kind=kCustom, calls=%fused_computation | custom fusion | bytes 128 | tf_op jit(solution)/shard_map/gather | solution.py:222
  31.7 1.7 %maximum_maximum_fusion = bf16[16,48,128]{2,1,0:T(8,128)(2,1)} fusion(bf16[16,2,128]{2,1,0:T(2,128)(2,1)S(1)} %reshape.443, bf16[16,32,128]{2,1,0:T(8,128)(2,1)} %bitcast.123, bf16[48]{0:T(256)(128)(2,1)} %pad.23.clone, bf16[48]{0:T(256)(128)(2,1)} %pad.21.clone), kind=kLoop, calls=%fused_computation.26 | loop fusion | flops 786432 | bytes 336064 | tf_op jit(solution)/shard_map/concatenate | solution.py:133
  33.4 1.0 reduce_sum.74
  35.1 12.6 %all-to-all-start.1 = ((bf16[16,48,128]{2,1,0:T(8,128)(2,1)}), bf16[16,48,128]{2,1,0:T(8,128)(2,1)}, u32[]{:S(2)}, u32[]{:S(2)}) async-start(bf16[16,48,128]{2,1,0:T(8,128)(2,1)} %broadcast_dynamic-update-slice_fusion), calls=%async_computation.1 | async-start | bytes 393216 | tf_op jit(solution)/shard_map/all_to_all | solution.py:146
  47.7 1.1 iota_compare_fusion.7
  49.5 11.1 %all-to-all-done.1 = bf16[16,48,128]{2,1,0:T(8,128)(2,1)} async-done(((bf16[16,48,128]{2,1,0:T(8,128)(2,1)}), bf16[16,48,128]{2,1,0:T(8,128)(2,1)}, u32[]{:S(2)}, u32[]{:S(2)}) %all-to-all-start.1) | async-done | bytes 196640 | tf_op jit(solution)/shard_map/all_to_all | solution.py:146
  60.7 0.8 slice.125
  61.7 0.8 select_reduce_fusion
  62.8 1.0 multiply_reduce_fusion
  65.4 8.4 %all-to-all-start.2 = ((bf16[16,48,128]{2,1,0:T(8,128)(2,1)}), bf16[16,48,128]{2,1,0:T(8,128)(2,1)}, u32[]{:S(2)}, u32[]{:S(2)}) async-start(bf16[16,48,128]{2,1,0:T(8,128)(2,1)} %broadcast_in_dim.133), calls=%async_computation.2 | async-start | bytes 393216 | tf_op jit(solution)/shard_map/all_to_all | solution.py:192
  73.8 0.8 and_reduce_fusion
  74.6 0.8 fusion.11
  76.3 10.1 %all-to-all-done.2 = bf16[16,48,128]{2,1,0:T(8,128)(2,1)} async-done(((bf16[16,48,128]{2,1,0:T(8,128)(2,1)}), bf16[16,48,128]{2,1,0:T(8,128)(2,1)}, u32[]{:S(2)}, u32[]{:S(2)}) %all-to-all-start.2) | async-done | bytes 196640 | tf_op jit(solution)/shard_map/all_to_all | solution.py:192
  86.4 1.3 %fusion.44 = (bf16[8,8,128]{2,1,0:T(8,128)(2,1)S(1)}, bf16[1,8,8,128]{3,2,1,0:T(8,128)(2,1)S(1)}, bf16[1,8,8,128]{3,2,1,0:T(8,128)(2,1)S(1)}, bf16[8,8,128]{2,1,0:T(8,128)(2,1)}) fusion(bf16[16,48,128]{2,1,0:T(8,128)(2,1)} %all-to-all-done.2), kind=kLoop, calls=%fused_computation.136 | loop fusion | bytes 98304 | tf_op jit(solution)/shard_map/slice | solution.py:206
  88.5 0.9 slice.168
  90.1 0.8 slice.169
  91.2 1.3 %gather_fusion.2 = bf16[64,2,8,128]{3,2,1,0:T(8,128)(2,1)} fusion(bf16[320,2,8,128]{3,2,1,0:T(8,128)(2,1)S(1)} %bitcast.115, s32[1024]{0:T(1024)S(1)} %pad_clamp_fusion), kind=kCustom, calls=%fused_computation.2 | custom fusion | bytes 524544 | tf_op jit(solution)/shard_map/gather | solution.py:232
  92.5 1.1 fusion.9
  93.7 11.9 %all-to-all-start.3 = ((bf16[32,2,1,2,8,128]{5,4,3,1,2,0:T(8,128)(2,1)}), bf16[32,2,1,2,8,128]{5,4,3,1,2,0:T(8,128)(2,1)}, u32[]{:S(2)}, u32[]{:S(2)}) async-start(bf16[32,2,1,2,8,128]{5,4,3,1,2,0:T(8,128)(2,1)} %bitcast.120), calls=%async_computation.3 | async-start | bytes 524288 | tf_op jit(solution)/shard_map/all_to_all | solution.py:234
  105.7 1.9 %divide_convert_fusion = bf16[8,8,8,128]{3,2,1,0:T(8,128)(2,1)} fusion(f32[8,8,8,128]{3,2,1,0:T(8,128)} %convert.32, f32[8,8,8]{2,1,0:T(8,128)S(1)} %get-tuple-element.44, f32[8,8,128]{2,1,0:T(8,128)S(1)} %convert_element_type.58, f32[8,8,8]{2,1,0:T(8,128)S(1)} %get-tuple-element.46, f32[8,8,8]{2,1,0:T(8,128)S(1)} %get-tuple-element.45), kind=kLoop, calls=%fused_computation.22 | loop fusion | flops 327680 | bytes 432128 | tf_op jit(solution)/shard_map/convert_element_type | solution.py:38
  107.6 7.0 %all-to-all-done.3 = bf16[32,2,1,2,8,128]{5,4,3,1,2,0:T(8,128)(2,1)} async-done(((bf16[32,2,1,2,8,128]{5,4,3,1,2,0:T(8,128)(2,1)}), bf16[32,2,1,2,8,128]{5,4,3,1,2,0:T(8,128)(2,1)}, u32[]{:S(2)}, u32[]{:S(2)}) %all-to-all-start.3) | async-done | bytes 262176 | tf_op jit(solution)/shard_map/all_to_all | solution.py:234
  114.6 1.0 constant_dynamic-update-slice_fusion
  115.6 1.0 copy-done.2
  (78 shorter events, 12.0 us)
Async XLA Ops:
  0.6 30.5 %copy-start = (bf16[128,64,128]{2,1,0:T(8,128)(2,1)S(1)}, bf16[128,64,128]{2,1,0:T(8,128)(2,1)}, u32[]{:S(2)}) copy-start(bf16[128,64,128]{2,1,0:T(8,128)(2,1)} %param.16) | copy-start | bytes 6291460
  0.6 4.8 %copy-start.3 = (bf16[256,256]{1,0:T(8,128)(2,1)S(1)}, bf16[256,256]{1,0:T(8,128)(2,1)}, u32[]{:S(2)}) copy-start(bf16[256,256]{1,0:T(8,128)(2,1)} %param.13) | copy-start | bytes 393220
  0.7 3.4 %copy-start.5 = (s32[256,1]{0,1:T(1,128)S(1)}, s32[256,1]{0,1:T(1,128)}, u32[]{:S(2)}) copy-start(s32[256,1]{0,1:T(1,128)} %param.17) | copy-start | bytes 3076
  8.0 25.5 %all-to-all-start = ((f32[32,8,256]{2,1,0:T(8,128)}), f32[32,8,256]{2,1,0:T(8,128)}, u32[]{:S(2)}, u32[]{:S(2)}) async-start(f32[32,8,256]{2,1,0:T(8,128)} %pad_maximum_fusion), calls=%async_computation | async-start | bytes 524288 | tf_op jit(solution)/shard_map/all_to_all | solution.py:89
  19.2 1.3 %copy-start.1 = (s32[8,32]{1,0:T(8,128)S(1)}, s32[8,32]{1,0:T(8,128)}, u32[]{:S(2)}) copy-start(s32[8,32]{1,0:T(8,128)} %param.21) | copy-start | bytes 3076
  19.2 2.0 %copy-start.4 = (s32[8]{0:T(128)S(1)}, s32[8]{0:T(128)}, u32[]{:S(2)}) copy-start(s32[8]{0:T(128)} %param.20) | copy-start | bytes 100
  19.2 2.0 %copy-start.6 = (s32[256,1]{0,1:T(1,128)S(1)}, s32[256,1]{0,1:T(1,128)}, u32[]{:S(2)}) copy-start(s32[256,1]{0,1:T(1,128)} %param.17) | copy-start | bytes 3076
  23.6 4.2 %copy-start.7 = (s32[32,1]{0,1:T(1,128)S(1)}, s32[32,1]{0,1:T(1,128)}, u32[]{:S(2)}) copy-start(s32[32,1]{0,1:T(1,128)} %param.23) | copy-start | bytes 388
  35.1 25.6 %all-to-all-start.1 = ((bf16[16,48,128]{2,1,0:T(8,128)(2,1)}), bf16[16,48,128]{2,1,0:T(8,128)(2,1)}, u32[]{:S(2)}, u32[]{:S(2)}) async-start(bf16[16,48,128]{2,1,0:T(8,128)(2,1)} %broadcast_dynamic-update-slice_fusion), calls=%async_computation.1 | async-start | bytes 393216 | tf_op jit(solution)/shard_map/all_to_all | solution.py:146
  65.4 21.0 %all-to-all-start.2 = ((bf16[16,48,128]{2,1,0:T(8,128)(2,1)}), bf16[16,48,128]{2,1,0:T(8,128)(2,1)}, u32[]{:S(2)}, u32[]{:S(2)}) async-start(bf16[16,48,128]{2,1,0:T(8,128)(2,1)} %broadcast_in_dim.133), calls=%async_computation.2 | async-start | bytes 393216 | tf_op jit(solution)/shard_map/all_to_all | solution.py:192
  93.7 20.8 %all-to-all-start.3 = ((bf16[32,2,1,2,8,128]{5,4,3,1,2,0:T(8,128)(2,1)}), bf16[32,2,1,2,8,128]{5,4,3,1,2,0:T(8,128)(2,1)}, u32[]{:S(2)}, u32[]{:S(2)}) async-start(bf16[32,2,1,2,8,128]{5,4,3,1,2,0:T(8,128)(2,1)} %bitcast.120), calls=%async_computation.3 | async-start | bytes 524288 | tf_op jit(solution)/shard_map/all_to_all | solution.py:234
  115.6 1.1 copy-start.2

commit v15 on v14

--- a/solution.py
+++ b/solution.py
@@ -133,14 +133,11 @@
     parcel = jnp.concatenate(
         [
             local_mixed.reshape(groups, block_rows, head_dim).astype(jnp.bfloat16),
-            jnp.zeros((groups,) + mid_rows.shape, jnp.bfloat16),
+            jnp.broadcast_to(mid_rows[None], (groups,) + mid_rows.shape),
             stat_pack,
             jnp.zeros((groups, spare_rows, head_dim), jnp.bfloat16),
         ],
         axis=1,
-    )
-    parcel = lax.dynamic_update_slice_in_dim(
-        parcel, jnp.broadcast_to(mid_rows[None], (groups,) + mid_rows.shape), block_rows, axis=1
     )
     received, up_weight_rows = lax.optimization_barrier(
         (lax.all_to_all(parcel, "grp", 0, 0, tiled=False), up_weight_rows)

time: 118 us -> 113 us (0.958)
  waiting for transfers between devices: 28.2 us -> 25.8 us
  local copies, waits for them, and re-layouts: 18.8 us -> 16.7 us
  matrix products: 6.82 us -> 5.56 us
  other arithmetic: 17.9 us -> 19.1 us
    all_to_all x1, waiting for transfers between devices: 11.1 us -> 9.87 us  [shards(): lax.all_to_all(parcel, 'grp', 0, 0, tiled=False)]
    all_to_all x1, waiting for transfers between devices: 6.99 us -> 5.79 us  [shards(): lax.all_to_all(outbound, 'req', split_axis=0, concat_axis=0, tiled=True)]
    unnamed x21 -> x25, local copies, waits for them, and re-layouts: 5.78 us -> 4.88 us
  transfers between devices with their start and end apart: 4 -> 4, of which waited for: 3 -> 3; matrix products, arithmetic and copies ran while one was open for 18% -> 17% of each run, Pallas kernels for 0% -> 0%
where the time goes in v15:
time: 113 us; the launch traced here: 112 us
  starting transfers between devices  43.9 us (39%)
  waiting for transfers between devices  25.8 us (23%)
  other arithmetic  19.1 us (17%)
  local copies, waits for them, and re-layouts  16.7 us (15%)
  matrix products  5.56 us (5%)
    all_to_all x1, starting transfers between devices, shards(): lax.all_to_all(parcel, 'grp', 0, 0, tiled=False)  12.6 us
    all_to_all x1, starting transfers between devices, shards(): lax.all_to_all(outbound, 'req', split_axis=0, concat_axis=0, tiled=True)  11.9 us
    all_to_all x1, starting transfers between devices, shards(): summed = jnp.sum(lax.all_to_all(partial, 'req', 0, 0, tiled=False), axis=0)  11 us
    all_to_all x1, waiting for transfers between devices, shards(): lax.all_to_all(jnp.broadcast_to(merged[None], (groups,) + merged.shape),...  10.1 us
    all_to_all x1, waiting for transfers between devices, shards(): lax.all_to_all(parcel, 'grp', 0, 0, tiled=False)  9.87 us
    all_to_all x1, starting transfers between devices, shards(): lax.all_to_all(jnp.broadcast_to(merged[None], (groups,) + merged.shape),...  8.45 us
    all_to_all x1, waiting for transfers between devices, shards(): lax.all_to_all(outbound, 'req', split_axis=0, concat_axis=0, tiled=True)  5.79 us
    unnamed x25, local copies, waits for them, and re-layouts  4.88 us
  transfers between devices with their start and end apart: 4, of which 3 were waited for; matrix products, arithmetic and copies ran while one was open for 17% of the time, Pallas kernels for 0%

profile of v15, /device:TPU:1, one launch (start us, length us, event | category | flops | bytes accessed | tf_op | source)
XLA Modules:
  0.0 112.0 jit_solution(17565571946411863845)
XLA Ops:
  0.7 1.5 %copy.88 = bf16[320,1,2,8,128]{4,3,2,1,0:T(8,128)(2,1)S(1)} copy(bf16[320,1,2,8,128]{4,3,2,1,0:T(8,128)(2,1)} %param.19) | data formatting | bytes 2621440
  2.7 0.8 sub.98
  3.5 1.1 %copy.81 = bf16[32,8,8,128]{3,1,2,0:T(8,128)(2,1)S(1)} copy(bf16[32,8,8,128]{3,2,1,0:T(8,128)(2,1)} %bitcast.122) | data formatting | bytes 1048576
  4.7 1.2 %convolution_bitcast_fusion = f32[32,8,1152]{2,1,0:T(8,128)S(1)} fusion(bf16[256,256]{1,0:T(8,128)(2,1)S(1)} %copy-done.4, bf16[256,1024]{1,0:T(8,128)(2,1)S(1)} %bitcast.117, bf16[256,128]{1,0:T(8,128)(2,1)} %param.14), kind=kOutput, calls=%fused_computation.4 | convolution fusion | flops 152174592 | bytes 1900544 | tf_op jit(solution)/shard_map/dot_general | solution.py:78
  7.0 11.0 %all-to-all-start = ((f32[32,8,256]{2,1,0:T(8,128)}), f32[32,8,256]{2,1,0:T(8,128)}, u32[]{:S(2)}, u32[]{:S(2)}) async-start(f32[32,8,256]{2,1,0:T(8,128)} %pad_maximum_fusion), calls=%async_computation | async-start | bytes 524288 | tf_op jit(solution)/shard_map/all_to_all | solution.py:89
  20.2 1.1 fusion.46
  21.4 1.9 %fusion.43 = (f32[8,8,8]{1,2,0:T(8,128)S(1)}, bf16[8,8,8,256]{3,1,2,0:T(8,128)(2,1)}) fusion(f32[8,8,8,256]{3,1,2,0:T(8,128)} %get-tuple-element.67, f32[8,8,8]{1,2,0:T(8,128)S(1)} %get-tuple-element.66, pred[8,256]{1,0:T(8,128)(4,1)S(1)} %fusion.23), kind=kLoop, calls=%fused_computation.134 | loop fusion | flops 523776 | bytes 792576 | tf_op jit(solution)/shard_map/reduce_sum | solution.py:116
  24.5 1.2 %gather_fusion = s32[8]{0:T(128)} fusion(s32[8,32]{1,0:T(8,128)S(1)} %copy-done.1, s32[8]{0:T(128)S(1)} %get-tuple-element.69), kind=kCustom, calls=%fused_computation | custom fusion | bytes 128 | tf_op jit(solution)/shard_map/gather | solution.py:219
  26.9 2.0 %convolution_convert_fusion = bf16[8,8,8,128]{3,2,1,0:T(8,128)(2,1)} fusion(bf16[256,2,8,128]{3,0,2,1:T(8,128)(2,1)} %bitcast.119, bf16[8,8,8,256]{3,1,2,0:T(8,128)(2,1)} %get-tuple-element.52), kind=kOutput, calls=%fused_computation.8 | convolution fusion | flops 33554432 | bytes 917504 | tf_op jit(solution)/shard_map/hgis,shd->hgid/dot_general | solution.py:117
  28.9 1.0 reduce_sum.73
  30.0 1.7 %maximum_maximum_fusion = bf16[16,48,128]{2,1,0:T(8,128)(2,1)} fusion(bf16[16,2,128]{2,1,0:T(2,128)(2,1)S(1)} %reshape.446, bf16[16,8,128]{2,1,0:T(8,128)(2,1)S(1)} %broadcast_in_dim.124, bf16[16,32,128]{2,1,0:T(8,128)(2,1)} %bitcast.123, bf16[48]{0:T(256)(128)(2,1)} %pad.19.clone), kind=kLoop, calls=%fused_computation.26 | loop fusion | flops 786432 | bytes 368736 | tf_op jit(solution)/shard_map/concatenate | solution.py:133
  31.7 12.6 %all-to-all-start.1 = ((bf16[16,48,128]{2,1,0:T(8,128)(2,1)}), bf16[16,48,128]{2,1,0:T(8,128)(2,1)}, u32[]{:S(2)}, u32[]{:S(2)}) async-start(bf16[16,48,128]{2,1,0:T(8,128)(2,1)} %maximum_maximum_fusion), calls=%async_computation.1 | async-start | bytes 393216 | tf_op jit(solution)/shard_map/all_to_all | solution.py:143
  45.0 1.2 %iota_compare_fusion.7 = pred[2,32]{1,0:T(4,128)(4,1)} fusion(s32[32]{0:T(128)} %convert_reduce_fusion), kind=kLoop, calls=%fused_computation.107 | loop fusion | flops 64 | bytes 192 | tf_op jit(solution)/shard_map/eq | solution.py:214
  47.4 9.9 %all-to-all-done.1 = bf16[16,48,128]{2,1,0:T(8,128)(2,1)} async-done(((bf16[16,48,128]{2,1,0:T(8,128)(2,1)}), bf16[16,48,128]{2,1,0:T(8,128)(2,1)}, u32[]{:S(2)}, u32[]{:S(2)}) %all-to-all-start.1) | async-done | bytes 196640 | tf_op jit(solution)/shard_map/all_to_all | solution.py:143
  57.3 0.8 slice.125
  58.2 1.0 multiply_reduce_fusion
  59.3 0.8 select_reduce_fusion
  61.9 8.4 %all-to-all-start.2 = ((bf16[16,48,128]{2,1,0:T(8,128)(2,1)}), bf16[16,48,128]{2,1,0:T(8,128)(2,1)}, u32[]{:S(2)}, u32[]{:S(2)}) async-start(bf16[16,48,128]{2,1,0:T(8,128)(2,1)} %broadcast_in_dim.129), calls=%async_computation.2 | async-start | bytes 393216 | tf_op jit(solution)/shard_map/all_to_all | solution.py:189
  70.4 0.8 and_reduce_fusion
  71.2 0.8 fusion.11
  72.8 10.1 %all-to-all-done.2 = bf16[16,48,128]{2,1,0:T(8,128)(2,1)} async-done(((bf16[16,48,128]{2,1,0:T(8,128)(2,1)}), bf16[16,48,128]{2,1,0:T(8,128)(2,1)}, u32[]{:S(2)}, u32[]{:S(2)}) %all-to-all-start.2) | async-done | bytes 196640 | tf_op jit(solution)/shard_map/all_to_all | solution.py:189
  83.0 1.3 %fusion.44 = (bf16[8,8,128]{2,1,0:T(8,128)(2,1)S(1)}, bf16[1,8,8,128]{3,2,1,0:T(8,128)(2,1)S(1)}, bf16[1,8,8,128]{3,2,1,0:T(8,128)(2,1)S(1)}, bf16[8,8,128]{2,1,0:T(8,128)(2,1)}) fusion(bf16[16,48,128]{2,1,0:T(8,128)(2,1)} %all-to-all-done.2), kind=kLoop, calls=%fused_computation.135 | loop fusion | bytes 98304 | tf_op jit(solution)/shard_map/slice | solution.py:203
  84.3 0.7 scatter_fusion
  85.1 0.9 slice.168
  86.7 0.8 slice.169
  87.8 1.3 %gather_fusion.2 = bf16[64,2,8,128]{3,2,1,0:T(8,128)(2,1)} fusion(bf16[320,2,8,128]{3,2,1,0:T(8,128)(2,1)S(1)} %bitcast.115, s32[1024]{0:T(1024)S(1)} %pad_clamp_fusion), kind=kCustom, calls=%fused_computation.2 | custom fusion | bytes 524544 | tf_op jit(solution)/shard_map/gather | solution.py:229
  89.1 11.9 %all-to-all-start.3 = ((bf16[32,2,1,2,8,128]{5,4,3,1,2,0:T(8,128)(2,1)}), bf16[32,2,1,2,8,128]{5,4,3,1,2,0:T(8,128)(2,1)}, u32[]{:S(2)}, u32[]{:S(2)}) async-start(bf16[32,2,1,2,8,128]{5,4,3,1,2,0:T(8,128)(2,1)} %bitcast.120), calls=%async_computation.3 | async-start | bytes 524288 | tf_op jit(solution)/shard_map/all_to_all | solution.py:231
  101.0 1.1 fusion.9
  102.3 1.9 %divide_convert_fusion = bf16[8,8,8,128]{3,2,1,0:T(8,128)(2,1)} fusion(f32[8,8,8,128]{3,2,1,0:T(8,128)} %convert.32, f32[8,8,8]{2,1,0:T(8,128)S(1)} %get-tuple-element.44, f32[8,8,128]{2,1,0:T(8,128)S(1)} %convert_element_type.58, f32[8,8,8]{2,1,0:T(8,128)S(1)} %get-tuple-element.46, f32[8,8,8]{2,1,0:T(8,128)S(1)} %get-tuple-element.45), kind=kLoop, calls=%fused_computation.22 | loop fusion | flops 327680 | bytes 432128 | tf_op jit(solution)/shard_map/convert_element_type | solution.py:38
  104.2 5.8 %all-to-all-done.3 = bf16[32,2,1,2,8,128]{5,4,3,1,2,0:T(8,128)(2,1)} async-done(((bf16[32,2,1,2,8,128]{5,4,3,1,2,0:T(8,128)(2,1)}), bf16[32,2,1,2,8,128]{5,4,3,1,2,0:T(8,128)(2,1)}, u32[]{:S(2)}, u32[]{:S(2)}) %all-to-all-start.3) | async-done | bytes 262176 | tf_op jit(solution)/shard_map/all_to_all | solution.py:231
  110.0 1.0 constant_dynamic-update-slice_fusion
  111.0 1.0 copy-done.2
  (80 shorter events, 12.4 us)
Async XLA Ops:
  0.6 25.7 %copy-start = (bf16[128,64,128]{2,1,0:T(8,128)(2,1)S(1)}, bf16[128,64,128]{2,1,0:T(8,128)(2,1)}, u32[]{:S(2)}) copy-start(bf16[128,64,128]{2,1,0:T(8,128)(2,1)} %param.16) | copy-start | bytes 6291460
  0.6 4.0 %copy-start.4 = (bf16[256,256]{1,0:T(8,128)(2,1)S(1)}, bf16[256,256]{1,0:T(8,128)(2,1)}, u32[]{:S(2)}) copy-start(bf16[256,256]{1,0:T(8,128)(2,1)} %param.13) | copy-start | bytes 393220
  0.7 1.5 %copy-start.6 = (s32[256,1]{0,1:T(1,128)S(1)}, s32[256,1]{0,1:T(1,128)}, u32[]{:S(2)}) copy-start(s32[256,1]{0,1:T(1,128)} %param.17) | copy-start | bytes 3076
  5.9 12.1 %copy-start.1 = (s32[8,32]{1,0:T(8,128)S(1)}, s32[8,32]{1,0:T(8,128)}, u32[]{:S(2)}) copy-start(s32[8,32]{1,0:T(8,128)} %param.21) | copy-start | bytes 3076
  7.0 22.0 %all-to-all-start = ((f32[32,8,256]{2,1,0:T(8,128)}), f32[32,8,256]{2,1,0:T(8,128)}, u32[]{:S(2)}, u32[]{:S(2)}) async-start(f32[32,8,256]{2,1,0:T(8,128)} %pad_maximum_fusion), calls=%async_computation | async-start | bytes 524288 | tf_op jit(solution)/shard_map/all_to_all | solution.py:89
  19.0 0.7 copy-start.5
  19.0 1.3 %copy-start.9 = (bf16[8,8192]{1,0:T(8,128)(2,1)S(1)}, bf16[8,8192]{1,0:T(8,128)(2,1)}, u32[]{:S(2)}) copy-start(bf16[8,8192]{1,0:T(8,128)(2,1)} %param.18) | copy-start | bytes 393220
  19.3 1.0 copy-start.3
  19.3 4.3 %copy-start.7 = (s32[256,1]{0,1:T(1,128)S(1)}, s32[256,1]{0,1:T(1,128)}, u32[]{:S(2)}) copy-start(s32[256,1]{0,1:T(1,128)} %param.17) | copy-start | bytes 3076
  19.3 4.4 %copy-start.8 = (s32[32,1]{0,1:T(1,128)S(1)}, s32[32,1]{0,1:T(1,128)}, u32[]{:S(2)}) copy-start(s32[32,1]{0,1:T(1,128)} %param.23) | copy-start | bytes 388
  31.7 25.6 %all-to-all-start.1 = ((bf16[16,48,128]{2,1,0:T(8,128)(2,1)}), bf16[16,48,128]{2,1,0:T(8,128)(2,1)}, u32[]{:S(2)}, u32[]{:S(2)}) async-start(bf16[16,48,128]{2,1,0:T(8,128)(2,1)} %maximum_maximum_fusion), calls=%async_computation.1 | async-start | bytes 393216 | tf_op jit(solution)/shard_map/all_to_all | solution.py:143
  61.9 21.0 %all-to-all-start.2 = ((bf16[16,48,128]{2,1,0:T(8,128)(2,1)}), bf16[16,48,128]{2,1,0:T(8,128)(2,1)}, u32[]{:S(2)}, u32[]{:S(2)}) async-start(bf16[16,48,128]{2,1,0:T(8,128)(2,1)} %broadcast_in_dim.129), calls=%async_computation.2 | async-start | bytes 393216 | tf_op jit(solution)/shard_map/all_to_all | solution.py:189
  89.1 20.8 %all-to-all-start.3 = ((bf16[32,2,1,2,8,128]{5,4,3,1,2,0:T(8,128)(2,1)}), bf16[32,2,1,2,8,128]{5,4,3,1,2,0:T(8,128)(2,1)}, u32[]{:S(2)}, u32[]{:S(2)}) async-start(bf16[32,2,1,2,8,128]{5,4,3,1,2,0:T(8,128)(2,1)} %bitcast.120), calls=%async_computation.3 | async-start | bytes 524288 | tf_op jit(solution)/shard_map/all_to_all | solution.py:231
  110.9 1.1 copy-start.2

commit v16 on v13

--- a/solution.py
+++ b/solution.py
@@ -139,8 +139,13 @@
         ],
         axis=1,
     )
-    received, up_weight_rows = lax.optimization_barrier(
-        (lax.all_to_all(parcel, "grp", 0, 0, tiled=False), up_weight_rows)
+    received, up_weight_rows, departing_slots, departing_target = lax.optimization_barrier(
+        (
+            lax.all_to_all(parcel, "grp", 0, 0, tiled=False),
+            up_weight_rows,
+            departing_slots,
+            departing_target,
+        )
     )
     stat_at = block_rows + rows
     shard_mixed = received[:, :block_rows].astype(jnp.float32).reshape(

time: 113 us -> 113 us (level)
  waiting for transfers between devices: 30.8 us -> 26.9 us
  other arithmetic: 13.1 us -> 16.9 us
    all_to_all x1, waiting for transfers between devices: 12.9 us -> 9.05 us  [shards(): lax.all_to_all(parcel, 'grp', 0, 0, tiled=False)]
    unnamed x27 -> x23, local copies, waits for them, and re-layouts: 5.24 us -> 5.24 us
  transfers between devices with their start and end apart: 4 -> 4, of which waited for: 3 -> 3; matrix products, arithmetic and copies ran while one was open for 12% -> 14% of each run, Pallas kernels for 0% -> 0%
where the time goes in v16:
time: 113 us; the launch traced here: 112 us
  starting transfers between devices  44.1 us (39%)
  waiting for transfers between devices  26.9 us (24%)
  local copies, waits for them, and re-layouts  17.6 us (16%)
  other arithmetic  16.9 us (15%)
  matrix products  5.77 us (5%)
    all_to_all x1, starting transfers between devices, shards(): lax.all_to_all(parcel, 'grp', 0, 0, tiled=False)  12.7 us
    all_to_all x1, waiting for transfers between devices, shards(): lax.all_to_all(jnp.broadcast_to(merged[None], (groups,) + merged.shape),...  12.1 us
    all_to_all x1, starting transfers between devices, shards(): lax.all_to_all(outbound, 'req', split_axis=0, concat_axis=0, tiled=True)  11.9 us
    all_to_all x1, starting transfers between devices, shards(): summed = jnp.sum(lax.all_to_all(partial, 'req', 0, 0, tiled=False), axis=0)  11 us
    all_to_all x1, waiting for transfers between devices, shards(): lax.all_to_all(parcel, 'grp', 0, 0, tiled=False)  9.05 us
    all_to_all x1, starting transfers between devices, shards(): lax.all_to_all(jnp.broadcast_to(merged[None], (groups,) + merged.shape),...  8.45 us
    all_to_all x1, waiting for transfers between devices, shards(): lax.all_to_all(outbound, 'req', split_axis=0, concat_axis=0, tiled=True)  5.8 us
    unnamed x23, local copies, waits for them, and re-layouts  5.24 us
  transfers between devices with their start and end apart: 4, of which 3 were waited for; matrix products, arithmetic and copies ran while one was open for 14% of the time, Pallas kernels for 0%

profile of v16, /device:TPU:1, one launch (start us, length us, event | category | flops | bytes accessed | tf_op | source)
XLA Modules:
  0.0 112.2 jit_solution(11174725703047307312)
XLA Ops:
  0.7 1.5 %copy.109 = bf16[320,1,2,8,128]{4,3,2,1,0:T(8,128)(2,1)S(1)} copy(bf16[320,1,2,8,128]{4,3,2,1,0:T(8,128)(2,1)} %param.19) | data formatting | bytes 2621440
  2.7 0.8 sub.98
  3.5 1.1 %copy.100 = bf16[32,8,8,128]{3,1,2,0:T(8,128)(2,1)S(1)} copy(bf16[32,8,8,128]{3,2,1,0:T(8,128)(2,1)} %bitcast.134) | data formatting | bytes 1048576
  4.7 1.2 %convolution_bitcast_fusion = f32[32,8,1152]{2,1,0:T(8,128)S(1)} fusion(bf16[256,256]{1,0:T(8,128)(2,1)S(1)} %copy-done.4, bf16[256,1024]{1,0:T(8,128)(2,1)S(1)} %bitcast.129, bf16[256,128]{1,0:T(8,128)(2,1)} %param.14), kind=kOutput, calls=%fused_computation.5 | convolution fusion | flops 152174592 | bytes 1900544 | tf_op jit(solution)/shard_map/dot_general | solution.py:78
  7.0 11.0 %all-to-all-start = ((f32[32,8,256]{2,1,0:T(8,128)}), f32[32,8,256]{2,1,0:T(8,128)}, u32[]{:S(2)}, u32[]{:S(2)}) async-start(f32[32,8,256]{2,1,0:T(8,128)} %pad_maximum_fusion), calls=%async_computation | async-start | bytes 524288 | tf_op jit(solution)/shard_map/all_to_all | solution.py:89
  19.7 0.9 copy-done.3
  20.6 1.1 fusion.51
  21.8 1.9 %fusion.46 = (f32[8,8,8]{1,2,0:T(8,128)S(1)}, bf16[8,8,8,256]{3,1,2,0:T(8,128)(2,1)}) fusion(f32[8,8,8,256]{3,1,2,0:T(8,128)} %get-tuple-element.73, f32[8,8,8]{1,2,0:T(8,128)S(1)} %get-tuple-element.72, pred[8,256]{1,0:T(8,128)(4,1)S(1)} %fusion.24), kind=kLoop, calls=%fused_computation.138 | loop fusion | flops 523776 | bytes 792576 | tf_op jit(solution)/shard_map/reduce_sum | solution.py:116
  24.1 1.1 %gather_fusion = s32[8]{0:T(128)} fusion(s32[8,32]{1,0:T(8,128)S(1)} %copy-done.1, s32[8]{0:T(128)S(1)} %fusion.41), kind=kCustom, calls=%fused_computation | custom fusion | bytes 128 | tf_op jit(solution)/shard_map/gather | solution.py:224
  25.9 1.3 %convolution_convert_fusion = bf16[8,8,8,128]{3,2,1,0:T(8,128)(2,1)S(1)} fusion(bf16[256,2,8,128]{3,0,2,1:T(8,128)(2,1)} %bitcast.131, bf16[8,8,8,256]{3,1,2,0:T(8,128)(2,1)} %get-tuple-element.54), kind=kOutput, calls=%fused_computation.9 | convolution fusion | flops 33554432 | bytes 917504 | tf_op jit(solution)/shard_map/hgis,shd->hgid/dot_general | solution.py:117
  27.3 1.0 reduce_sum.73
  28.3 1.4 %maximum_maximum_fusion = bf16[16,48,128]{2,1,0:T(8,128)(2,1)} fusion(bf16[16,2,128]{2,1,0:T(2,128)(2,1)S(1)} %reshape.460, bf16[16,8,128]{2,1,0:T(8,128)(2,1)S(1)} %broadcast_in_dim.83, bf16[16,32,128]{2,1,0:T(8,128)(2,1)S(1)} %bitcast.136, bf16[48]{0:T(256)(128)(2,1)} %pad.19.clone), kind=kLoop, calls=%fused_computation.27 | loop fusion | flops 786432 | bytes 368736 | tf_op jit(solution)/shard_map/concatenate | solution.py:133
  29.7 12.7 %all-to-all-start.1 = ((bf16[16,48,128]{2,1,0:T(8,128)(2,1)}), bf16[16,48,128]{2,1,0:T(8,128)(2,1)}, u32[]{:S(2)}, u32[]{:S(2)}) async-start(bf16[16,48,128]{2,1,0:T(8,128)(2,1)} %maximum_maximum_fusion), calls=%async_computation.1 | async-start | bytes 393216 | tf_op jit(solution)/shard_map/all_to_all | solution.py:144
  42.4 0.8 shift-left_bitcast_fusion
  43.8 1.2 %gather_fusion.1 = bf16[8,64,128]{2,1,0:T(8,128)(2,1)} fusion(bf16[128,64,128]{2,1,0:T(8,128)(2,1)S(1)} %copy-done, s32[1024]{0:T(1024)S(1)} %pad_clamp_fusion.1), kind=kCustom, calls=%fused_computation.1 | custom fusion | bytes 262176 | tf_op jit(solution)/shard_map/gather | solution.py:88
  46.4 9.0 %all-to-all-done.1 = bf16[16,48,128]{2,1,0:T(8,128)(2,1)} async-done(((bf16[16,48,128]{2,1,0:T(8,128)(2,1)}), bf16[16,48,128]{2,1,0:T(8,128)(2,1)}, u32[]{:S(2)}, u32[]{:S(2)}) %all-to-all-start.1) | async-done | bytes 196640 | tf_op jit(solution)/shard_map/all_to_all | solution.py:144
  56.1 0.9 convert_reduce_fusion
  57.0 0.8 slice.125
  58.0 1.0 multiply_reduce_fusion
  59.0 0.8 select_reduce_fusion
  60.0 1.0 fusion.26
  62.7 8.4 %all-to-all-start.2 = ((bf16[16,48,128]{2,1,0:T(8,128)(2,1)}), bf16[16,48,128]{2,1,0:T(8,128)(2,1)}, u32[]{:S(2)}, u32[]{:S(2)}) async-start(bf16[16,48,128]{2,1,0:T(8,128)(2,1)} %broadcast_in_dim.133), calls=%async_computation.2 | async-start | bytes 393216 | tf_op jit(solution)/shard_map/all_to_all | solution.py:194
  71.6 12.1 %all-to-all-done.2 = bf16[16,48,128]{2,1,0:T(8,128)(2,1)} async-done(((bf16[16,48,128]{2,1,0:T(8,128)(2,1)}), bf16[16,48,128]{2,1,0:T(8,128)(2,1)}, u32[]{:S(2)}, u32[]{:S(2)}) %all-to-all-start.2) | async-done | bytes 196640 | tf_op jit(solution)/shard_map/all_to_all | solution.py:194
  85.3 0.9 slice.170
  86.9 0.8 slice.171
  88.0 1.3 %gather_fusion.3 = bf16[64,2,8,128]{3,2,1,0:T(8,128)(2,1)} fusion(bf16[320,2,8,128]{3,2,1,0:T(8,128)(2,1)S(1)} %bitcast.127, s32[1024]{0:T(1024)S(1)} %pad_clamp_fusion), kind=kCustom, calls=%fused_computation.3 | custom fusion | bytes 524544 | tf_op jit(solution)/shard_map/gather | solution.py:235
  89.3 11.9 %all-to-all-start.3 = ((bf16[32,2,1,2,8,128]{5,4,3,1,2,0:T(8,128)(2,1)}), bf16[32,2,1,2,8,128]{5,4,3,1,2,0:T(8,128)(2,1)}, u32[]{:S(2)}, u32[]{:S(2)}) async-start(bf16[32,2,1,2,8,128]{5,4,3,1,2,0:T(8,128)(2,1)} %bitcast.132), calls=%async_computation.3 | async-start | bytes 524288 | tf_op jit(solution)/shard_map/all_to_all | solution.py:237
  101.2 1.1 fusion.9
  102.4 1.9 %divide_convert_fusion = bf16[8,8,8,128]{3,2,1,0:T(8,128)(2,1)} fusion(f32[8,8,8,128]{3,2,1,0:T(8,128)} %convert.32, f32[8,8,8]{2,1,0:T(8,128)S(1)} %get-tuple-element.46, f32[8,8,128]{2,1,0:T(8,128)S(1)} %copy.63, f32[8,8,8]{2,1,0:T(8,128)S(1)} %get-tuple-element.48, f32[8,8,8]{2,1,0:T(8,128)S(1)} %get-tuple-element.47), kind=kLoop, calls=%fused_computation.23 | loop fusion | flops 327680 | bytes 432128 | tf_op jit(solution)/shard_map/convert_element_type | solution.py:38
  104.3 5.8 %all-to-all-done.3 = bf16[32,2,1,2,8,128]{5,4,3,1,2,0:T(8,128)(2,1)} async-done(((bf16[32,2,1,2,8,128]{5,4,3,1,2,0:T(8,128)(2,1)}), bf16[32,2,1,2,8,128]{5,4,3,1,2,0:T(8,128)(2,1)}, u32[]{:S(2)}, u32[]{:S(2)}) %all-to-all-start.3) | async-done | bytes 262176 | tf_op jit(solution)/shard_map/all_to_all | solution.py:237
  110.1 1.0 constant_dynamic-update-slice_fusion
  111.1 1.0 copy-done.2
  (81 shorter events, 12.2 us)
Async XLA Ops:
  0.6 43.1 %copy-start = (bf16[128,64,128]{2,1,0:T(8,128)(2,1)S(1)}, bf16[128,64,128]{2,1,0:T(8,128)(2,1)}, u32[]{:S(2)}) copy-start(bf16[128,64,128]{2,1,0:T(8,128)(2,1)} %param.16) | copy-start | bytes 6291460
  0.6 4.0 %copy-start.4 = (bf16[256,256]{1,0:T(8,128)(2,1)S(1)}, bf16[256,256]{1,0:T(8,128)(2,1)}, u32[]{:S(2)}) copy-start(bf16[256,256]{1,0:T(8,128)(2,1)} %param.13) | copy-start | bytes 393220
  0.7 1.5 %copy-start.5 = (s32[256,1]{0,1:T(1,128)S(1)}, s32[256,1]{0,1:T(1,128)}, u32[]{:S(2)}) copy-start(s32[256,1]{0,1:T(1,128)} %param.17) | copy-start | bytes 3076
  5.9 12.1 %copy-start.1 = (s32[8,32]{1,0:T(8,128)S(1)}, s32[8,32]{1,0:T(8,128)}, u32[]{:S(2)}) copy-start(s32[8,32]{1,0:T(8,128)} %param.21) | copy-start | bytes 3076
  7.0 20.3 %all-to-all-start = ((f32[32,8,256]{2,1,0:T(8,128)}), f32[32,8,256]{2,1,0:T(8,128)}, u32[]{:S(2)}, u32[]{:S(2)}) async-start(f32[32,8,256]{2,1,0:T(8,128)} %pad_maximum_fusion), calls=%async_computation | async-start | bytes 524288 | tf_op jit(solution)/shard_map/all_to_all | solution.py:89
  19.0 0.7 copy-start.6
  19.0 1.6 %copy-start.8 = (bf16[8,8192]{1,0:T(8,128)(2,1)S(1)}, bf16[8,8192]{1,0:T(8,128)(2,1)}, u32[]{:S(2)}) copy-start(bf16[8,8192]{1,0:T(8,128)(2,1)} %param.18) | copy-start | bytes 393220
  19.6 1.0 copy-start.3
  29.7 41.5 %copy-start.7 = (s32[32]{0:T(128)S(1)}, s32[32]{0:T(128)}, u32[]{:S(2)}) copy-start(s32[32]{0:T(128)} %param.22) | copy-start | bytes 388
  29.7 25.7 %all-to-all-start.1 = ((bf16[16,48,128]{2,1,0:T(8,128)(2,1)}), bf16[16,48,128]{2,1,0:T(8,128)(2,1)}, u32[]{:S(2)}, u32[]{:S(2)}) async-start(bf16[16,48,128]{2,1,0:T(8,128)(2,1)} %maximum_maximum_fusion), calls=%async_computation.1 | async-start | bytes 393216 | tf_op jit(solution)/shard_map/all_to_all | solution.py:144
  62.7 21.0 %all-to-all-start.2 = ((bf16[16,48,128]{2,1,0:T(8,128)(2,1)}), bf16[16,48,128]{2,1,0:T(8,128)(2,1)}, u32[]{:S(2)}, u32[]{:S(2)}) async-start(bf16[16,48,128]{2,1,0:T(8,128)(2,1)} %broadcast_in_dim.133), calls=%async_computation.2 | async-start | bytes 393216 | tf_op jit(solution)/shard_map/all_to_all | solution.py:194
  89.3 20.8 %all-to-all-start.3 = ((bf16[32,2,1,2,8,128]{5,4,3,1,2,0:T(8,128)(2,1)}), bf16[32,2,1,2,8,128]{5,4,3,1,2,0:T(8,128)(2,1)}, u32[]{:S(2)}, u32[]{:S(2)}) async-start(bf16[32,2,1,2,8,128]{5,4,3,1,2,0:T(8,128)(2,1)} %bitcast.132), calls=%async_computation.3 | async-start | bytes 524288 | tf_op jit(solution)/shard_map/all_to_all | solution.py:237
  111.1 1.1 copy-start.2
